TPU v7x, 32 devices: a whole 2x2x4 slice. The times are simulated.
32 devices in a mesh: search: 4 (over y, core), net: 8 (over z, x).
Axes of the slice: x: 2, y: 2, z: 4, core: 2. Of those that a mesh axis runs over, the one named last changes fastest.
Arguments:
- states: bfloat16 [4096, 11552], P(('search', 'net')), may hold values from -6 to 6
- counts: int32 [32], P(('search', 'net')), may hold values from 1 to 128, 1024 in all
- owners: int32 [4096], P(('search', 'net')), may hold values from 0 to 255
- legal: int32 [4096, 8, 361], P(('search', 'net')), may hold values 0 or 1
- in_weight: bfloat16 [3, 3, 32, 256], replicated, may hold values from -0.375 to 0.375
- mid_weight: bfloat16 [1, 3, 3, 256, 256], replicated, may hold values from -0.125 to 0.125
- out_weight: bfloat16 [1, 3, 3, 256, 256], replicated, may hold values from -0.125 to 0.125
- policy_weight: bfloat16 [256, 8], replicated, may hold values from -0.75 to 0.75
- pass_weight: bfloat16 [256, 8], replicated, may hold values from -1.5 to 1.5
- value_weight: bfloat16 [256], replicated, may hold values from -1.5 to 1.5
- logit_scale: float32 [8], replicated, may hold values from 0.25 to 4
Outputs:
- priors: float32 [4096, 8, 362], P(('search', 'net'))
- leaf_values: float32 [4096], P(('search', 'net'))
- tree_value: float32 [256], P(('search', 'net'))
Inputs may be any that keep to these rules, and one draw needn't show every extreme that they name: counts sum to exactly 32 times the number of devices, and one device holds 128 live leaves.
All inputs are finite; a program needn't handle non-finite values. No bound on the sum of `legal` on one device may be relied on, other than what follows from the above.
Results may differ from a plain program's by a relative error of at most 0.03.
Values may be sent and summed in bfloat16 or wider, within the bound.
No kernel may reach another device: no remote copies, remote signals or barrier semaphores. Data moves between devices by JAX's collectives and lax.ppermute only.
A program may use at most 128 MiB of HBM per device.

v0:
```python
import functools

import jax
import jax.numpy as jnp
from jax import lax
from jax.experimental import pallas as pl
from jax.experimental.pallas import tpu as pltpu
from jax.sharding import PartitionSpec as P

SIDE = 19
BOARD = 361
MOVES = 362
PLANES = 32
FACT = 8
TREE_DEV = 8
AXES = ("search", "net")
CHUNK = 40
PASSES = 3
CORE_CAP = 64
LINK_CAP = 32
FAR_CAP = 16


def convolve(inputs, kernel):
    return lax.conv_general_dilated(
        inputs,
        kernel,
        (1, 1),
        "SAME",
        dimension_numbers=("NHWC", "HWIO", "NHWC"),
        preferred_element_type=jnp.float32,
    )


def evaluate(batch, in_weight, mid_weight, out_weight, policy_weight, pass_weight, value_weight):
    leaves = batch.shape[0]
    board = batch.reshape(leaves, SIDE, SIDE, PLANES)
    hidden = jax.nn.relu(convolve(board, in_weight)).astype(jnp.bfloat16)
    inner = jax.nn.relu(convolve(hidden, mid_weight[0])).astype(jnp.bfloat16)
    hidden = jax.nn.relu(hidden.astype(jnp.float32) + convolve(inner, out_weight[0])).astype(
        jnp.bfloat16
    )
    cells = jnp.einsum(
        "bhwc,cf->bfhw", hidden, policy_weight, preferred_element_type=jnp.float32
    ).reshape(leaves, FACT, BOARD)
    pooled = jnp.mean(hidden, axis=(1, 2), dtype=jnp.float32)
    passing = jnp.dot(pooled, pass_weight.astype(jnp.float32), precision=lax.Precision.HIGHEST)
    logits = jnp.concatenate([cells, passing[:, :, None]], axis=2).astype(jnp.bfloat16)
    values = jnp.tanh(
        jnp.dot(pooled, value_weight.astype(jnp.float32), precision=lax.Precision.HIGHEST)
    ).astype(jnp.bfloat16)
    return (logits, values)


def masked_priors(logits, legal, logit_scale):
    scaled = logit_scale[None, :, None] * logits.astype(jnp.float32)
    allowed = jnp.concatenate(
        [legal > 0, jnp.ones(legal.shape[:2] + (1,), dtype=jnp.bool_)], axis=2
    )
    peak = jnp.max(jnp.where(allowed, scaled, -1e30), axis=2, keepdims=True)
    weights = jnp.exp(jnp.where(allowed, scaled - peak, -1e30))
    return weights / jnp.sum(weights, axis=2, keepdims=True)


def plan_kernel(masks, caps, slot_count, work_rows, counts_ref, me_ref, out_ref, idx_ref):
    counts_all = counts_ref[...]
    lanes = counts_all.shape[1]
    lane = lax.broadcasted_iota(jnp.int32, counts_all.shape, 1)

    def swap(x, mask):
        up = pltpu.roll(x, mask, 1)
        up_from = pltpu.roll(lane, mask, 1)
        down = pltpu.roll(x, lanes - mask, 1)
        return jnp.where(up_from == (lane ^ mask), up, down)

    flows = [jnp.zeros_like(counts_all) for _ in masks]
    for _ in range(PASSES):
        for e, (mask, cap) in enumerate(zip(masks, caps)):
            sent = sum(flows)
            got = sum(swap(f, m) for f, m in zip(flows, masks))
            load = counts_all - sent + got
            own = counts_all - sent
            move = jnp.right_shift(jnp.maximum(load - swap(load, mask), 0), 1)
            cancel = jnp.minimum(move, swap(flows[e], mask))
            add = jnp.clip(move - cancel, 0, jnp.minimum(cap - flows[e], own))
            flows[e] = flows[e] + add - swap(cancel, mask)
    into = [swap(f, m) for f, m in zip(flows, masks)]
    keep = counts_all - sum(flows)
    starts, places = [], []
    for e in range(len(masks)):
        starts.append(keep + sum(flows[:e]))
        places.append(keep + sum(into[:e]))
    rows = flows + into + starts + places + [keep, keep + sum(into)]
    rows = rows + [jnp.zeros_like(counts_all)] * (out_ref.shape[0] - len(rows))
    out_ref[...] = jnp.concatenate(rows, axis=0)

    me = me_ref[...]

    def mine(v):
        return jnp.sum(jnp.where(lane == me, v, 0), axis=1, keepdims=True)

    k = lax.broadcasted_iota(jnp.int32, (1, idx_ref.shape[1]), 1)
    work_idx = k
    pick = k
    work_base = slot_count
    pick_base = work_rows
    for e, cap in enumerate(caps):
        place, got_e = mine(places[e]), mine(into[e])
        work_idx = jnp.where((k >= place) & (k < place + got_e), work_base + k - place, work_idx)
        start, sent_e = mine(starts[e]), mine(flows[e])
        pick = jnp.where((k >= start) & (k < start + sent_e), pick_base + k - start, pick)
        work_base = work_base + cap
        pick_base = pick_base + cap
    work_idx = jnp.clip(work_idx, 0, work_base - 1)
    pick = jnp.clip(pick, 0, pick_base - 1)
    idx_ref[...] = jnp.concatenate([work_idx, pick] + [k * 0] * (idx_ref.shape[0] - 2), axis=0)


def make_plan(counts_all, me, masks, caps, slot_count, work_rows):
    groups = counts_all.shape[0]
    lanes = -(-groups // 128) * 128
    padded = jnp.zeros((1, lanes), jnp.int32).at[0, :groups].set(counts_all)
    rows = -(-(4 * len(masks) + 2) // 8) * 8
    width = -(-max(work_rows, slot_count) // 128) * 128
    return pl.pallas_call(
        functools.partial(plan_kernel, masks, caps, slot_count, work_rows),
        out_shape=(
            jax.ShapeDtypeStruct((rows, lanes), jnp.int32),
            jax.ShapeDtypeStruct((8, width), jnp.int32),
        ),
    )(padded, jnp.full((1, lanes), me, jnp.int32))


def body(
    states,
    counts,
    owners,
    legal,
    in_weight,
    mid_weight,
    out_weight,
    policy_weight,
    pass_weight,
    value_weight,
    logit_scale,
):
    weights = (in_weight, mid_weight, out_weight, policy_weight, pass_weight, value_weight)
    slot_count, row = states.shape
    groups = lax.axis_size(AXES)
    net_size = lax.axis_size("net")
    me = lax.axis_index(AXES)
    own_count = counts[0]

    counts_all = lax.all_to_all(
        jnp.broadcast_to(counts, (groups, 1)), AXES, 0, 0, tiled=True
    ).reshape(groups)

    masks = (4, 2, 2 * net_size, 1, net_size)
    caps = (FAR_CAP, LINK_CAP, LINK_CAP, LINK_CAP, CORE_CAP)
    work_rows = -(-slot_count // CHUNK) * CHUNK
    plan, lists = make_plan(counts_all, me, masks, caps, slot_count, work_rows)
    mine = lax.dynamic_slice(plan, (0, me), (plan.shape[0], 1))[:, 0]
    edges = len(masks)
    send = [mine[e] for e in range(edges)]
    starts = [mine[2 * edges + e] for e in range(edges)]
    places = [mine[3 * edges + e] for e in range(edges)]
    work_count = mine[4 * edges + 1]

    recv = [mine[edges + e] for e in range(edges)]

    margin = max(caps)
    padded = jnp.concatenate([states, jnp.zeros((margin, row), states.dtype)])
    pairs = [[(d, d ^ m) for d in range(groups)] for m in masks]
    incoming = [
        lax.ppermute(lax.dynamic_slice(padded, (starts[e], 0), (cap, row)), AXES, pairs[e])
        for e, cap in enumerate(caps)
    ]

    pool = jnp.concatenate([states] + incoming, axis=0)
    work_idx = lists[0, :work_rows]
    flat = FACT * MOVES

    def step(t, carry):
        logits_acc, values_acc = carry
        idx = lax.dynamic_slice(work_idx, (t * CHUNK,), (CHUNK,))
        logits, values = evaluate(jnp.take(pool, idx, axis=0), *weights)
        logits_acc = lax.dynamic_update_slice(
            logits_acc, logits.reshape(CHUNK, flat), (t * CHUNK, 0)
        )
        values_acc = lax.dynamic_update_slice(values_acc, values, (t * CHUNK,))
        return logits_acc, values_acc

    work_logits, work_values = lax.fori_loop(
        0,
        (work_count + CHUNK - 1) // CHUNK,
        step,
        (jnp.zeros((work_rows, flat), jnp.bfloat16), jnp.zeros((work_rows,), jnp.bfloat16)),
    )

    back_logits, back_values = [], []
    for e, cap in enumerate(caps):
        idx = jnp.clip(places[e] + jnp.arange(cap, dtype=jnp.int32), 0, work_rows - 1)
        back_logits.append(lax.ppermute(jnp.take(work_logits, idx, axis=0), AXES, pairs[e]))
        back_values.append(lax.ppermute(jnp.take(work_values, idx, axis=0), AXES, pairs[e]))

    all_logits = jnp.concatenate([work_logits] + back_logits, axis=0)
    all_values = jnp.concatenate([work_values] + back_values, axis=0)
    slot = jnp.arange(slot_count, dtype=jnp.int32)
    pick = lists[1, :slot_count]
    slot_logits = jnp.take(all_logits, pick, axis=0).reshape(slot_count, FACT, MOVES)
    slot_values = jnp.take(all_values, pick, axis=0)

    alive = slot < own_count
    priors = jnp.where(
        alive[:, None, None], masked_priors(slot_logits, legal, logit_scale), 0.0
    )
    leaf_values = jnp.where(alive, slot_values.astype(jnp.float32), 0.0)
    tree_total = TREE_DEV * groups
    onehot = (owners[:, None] == jnp.arange(tree_total, dtype=jnp.int32)[None, :]).astype(
        jnp.float32
    )
    partial_sums = jnp.dot(leaf_values, onehot, precision=lax.Precision.HIGHEST)
    spread = lax.all_to_all(partial_sums.reshape(groups, TREE_DEV), AXES, 0, 0, tiled=True)
    tree_value = jnp.sum(spread, axis=0)
    return (priors, leaf_values, tree_value)


def solution(mesh):
    in_specs = (
        P(AXES, None),
        P(AXES),
        P(AXES),
        P(AXES, None, None),
        P(),
        P(),
        P(),
        P(),
        P(),
        P(),
        P(),
    )
    out_specs = (P(AXES, None, None), P(AXES), P(AXES))
    return jax.shard_map(body, mesh=mesh, in_specs=in_specs, out_specs=out_specs, check_vma=False)
```

profile of v0, /device:TPU:0, one launch (start us, length us, event | category | flops | bytes accessed | tf_op | source)
XLA Modules:
  0.0 198.3 jit_solution(9024411217812990278)
XLA Ops:
  1.9 7.3 %all-to-all-start = ((s32[32,1,1]{2,1,0:T(1,128)}), s32[32,1,1]{2,1,0:T(1,128)S(1)}, u32[]{:S(2)}, u32[]{:S(2)}) async-start(s32[32,1,1]{2,1,0:T(1,128)} %broadcast_in_dim.122), calls=%async_computation | async-start | bytes 32768 | tf_op jit(solution)/shard_map/all_to_all | solution.py:154
  9.8 3.4 %copy.46 = bf16[128,11552]{1,0:T(8,128)(2,1)S(1)} copy(bf16[128,11552]{0,1:T(8,128)(2,1)} %param.19) | data formatting | bytes 5914624 | tf_op args[0]
  13.2 1.8 constant_dynamic-update-slice_fusion.6
  15.1 1.0 broadcast_compare_fusion
  17.3 1.3 fusion.17
  19.7 4.6 %shard_map.130 = (s32[24,128]{1,0:T(8,128)}, s32[8,256]{1,0:T(8,128)}) custom-call(s32[1,128]{1,0:T(1,128)} %scatter.4.counts_ref, s32[1,128]{1,0:T(1,128)} %broadcast_in_dim.123.me_ref), custom_call_target="tpu_custom_call" | custom-call | tf_op jit(solution)/shard_map/pallas_call | solution.py:125
  24.3 1.6 fusion.36
  32.9 1.1 compare_and_fusion.5
  34.7 1.2 compare_and_fusion.3
  35.8 1.2 compare_and_fusion.2
  37.0 1.2 compare_select_fusion.1
  38.2 1.2 compare_and_fusion.1
  40.1 1.2 compare_and_fusion.4
  43.0 1.9 pad_dynamic-slice_fusion.1
  44.9 1.8 collective-permute-start.1
  47.3 0.9 pad_dynamic-slice_fusion.4
  48.2 2.4 %collective-permute-start = (bf16[16,11552]{1,0:T(8,128)(2,1)}, bf16[16,11552]{1,0:T(8,128)(2,1)S(1)}, u32[]{:S(2)}, u32[]{:S(2)}) collective-permute-start(bf16[16,11552]{1,0:T(8,128)(2,1)} %pad_dynamic-slice_fusion.4), channel_id=1, source_target_pairs={{0,4},{1,5},{2,6},{3,7},{4,0},{5,1},{6,2},{7,3},{8,12},{9,13},{10,... | collective-permute-start | bytes 1109000 | tf_op jit(solution)/shard_map/ppermute | solution.py:175
  50.7 1.5 collective-permute-start.2
  52.2 1.5 collective-permute-start.3
  57.2 1.7 pad_dynamic-slice_fusion
  58.9 0.7 slice.68
  60.9 10.3 %collective-permute-done = bf16[16,11552]{1,0:T(8,128)(2,1)S(1)} collective-permute-done((bf16[16,11552]{1,0:T(8,128)(2,1)}, bf16[16,11552]{1,0:T(8,128)(2,1)S(1)}, u32[]{:S(2)}, u32[]{:S(2)}) %collective-permute-start) | collective-permute-done | bytes 369696 | tf_op jit(solution)/shard_map/ppermute | solution.py:175
  71.2 0.8 constant_dynamic-update-slice_fusion.5
  72.1 2.0 %constant_dynamic-update-slice_fusion.4 = bf16[304,11552]{1,0:T(8,128)(2,1)} fusion(bf16[304,11552]{1,0:T(8,128)(2,1)} %constant_dynamic-update-slice_fusion.5, bf16[32,11552]{1,0:T(8,128)(2,1)} %collective-permute-done.1), kind=kLoop, calls=%fused_computation.64 | loop fusion | bytes 1490944
  74.1 2.0 %constant_dynamic-update-slice_fusion.3 = bf16[304,11552]{1,0:T(8,128)(2,1)} fusion(bf16[304,11552]{1,0:T(8,128)(2,1)} %constant_dynamic-update-slice_fusion.4, bf16[32,11552]{1,0:T(8,128)(2,1)} %collective-permute-done.2), kind=kLoop, calls=%fused_computation.63 | loop fusion | bytes 1490944
  76.2 2.2 %constant_dynamic-update-slice_fusion.2 = bf16[304,11552]{1,0:T(8,128)(2,1)} fusion(bf16[304,11552]{1,0:T(8,128)(2,1)} %constant_dynamic-update-slice_fusion.3, bf16[32,11552]{1,0:T(8,128)(2,1)} %collective-permute-done.3), kind=kLoop, calls=%fused_computation.62 | loop fusion | bytes 1490944
  78.3 1.2 constant_dynamic-update-slice_fusion.1
  79.7 63.5 %while.13 = (s32[]{:T(128)}, bf16[160,2896]{1,0:T(8,128)(2,1)S(1)}, bf16[160]{0:T(256)(128)(2,1)S(1)}, s32[]{:T(128)}, s32[160]{0:T(256)S(1)}, /*index=5*/bf16[3...) while((s32[]{:T(128)}, bf16[160,2896]{1,0:T(8,128)(2,1)S(1)}, ...), condition=%wide.region_3.4_spmd, body=%wide.region_1.3_spmd.sunk | while | flops 33800157184 | bytes 67678120 | solution.py:193
  80.0 5.9 %gather_fusion = bf16[40,11552]{1,0:T(8,128)(2,1)S(1)} fusion(bf16[304,11552]{1,0:T(8,128)(2,1)} %get-tuple-element.261, s32[1024]{0:T(1024)S(1)} %pad_clamp_fusion.8), kind=kCustom, calls=%fused_computation.clone.1 | custom fusion | bytes 1848480 | tf_op jit(solution)/shard_map/while/body/jit(_take)/gather | solution.py:186
  86.0 5.0 %gather.87 = bf16[40,19,19,32]{3,2,1,0:T(8,128)(2,1)} reshape(bf16[40,11552]{1,0:T(8,128)(2,1)S(1)} %gather_fusion) | data formatting | bytes 1848320 | tf_op jit(solution)/shard_map/while/body/jit(_take)/gather | solution.py:186
  91.0 2.8 %broadcast_select_fusion.14 = bf16[40,19,19,32]{3,2,1,0:T(8,128)(2,1)S(1)} fusion(bf16[40,19,19,32]{3,2,1,0:T(8,128)(2,1)} %gather.87, pred[40]{0:T(512)(128)(4,1)S(1)} %get-tuple-element.221), kind=kLoop, calls=%fused_computation.17.clone.1 | loop fusion | flops 462080 | bytes 1848360 | tf_op jit(solution)/shard_map/while/body/jit(_take)/select_n | solution.py:186
  93.8 6.7 %maximum_convert_fusion.5 = bf16[40,19,19,256]{3,0,2,1:T(8,128)(2,1)S(1)} fusion(bf16[3,3,32,256]{3,2,1,0:T(8,128)(2,1)S(1)} %get-tuple-element.262, bf16[40,19,19,32]{3,2,1,0:T(8,128)(2,1)S(1)} %broadcast_select_fusion.14), kind=kOutput, calls=%fused_computation.16.clone.1 | convolution fusion | flops 1989857280 | bytes 8464896 | tf_op jit(solution)/shard_map/while/body/conv_general_dilated | solution.py:25
  100.5 18.3 %maximum_convert_fusion.6 = bf16[40,19,19,256]{3,0,2,1:T(8,128)(2,1)S(1)} fusion(bf16[40,19,19,256]{3,0,2,1:T(8,128)(2,1)S(1)} %maximum_convert_fusion.5, bf16[1,3,3,256,256]{4,3,2,1,0:T(8,128)(2,1)S(1)} %get-tuple-element.263), kind=kOutput, calls=%fused_computation.15.clone.1 | convolution fusion | flops 15867105280 | bytes 15966208 | tf_op jit(solution)/shard_map/while/body/conv_general_dilated | solution.py:25
  118.8 18.6 %convert_reduce_fusion.2 = (f32[40,256]{1,0:T(8,128)S(1)}, bf16[40,19,19,256]{3,0,2,1:T(8,128)(2,1)S(1)}) fusion(bf16[40,19,19,256]{3,0,2,1:T(8,128)(2,1)S(1)} %maximum_convert_fusion.6, bf16[1,3,3,256,256]{4,3,2,1,0:T(8,128)(2,1)S(1)} %copy-done.14, bf16[40,19,19,256]{3,0,2,1:T(8,128)(2,1)S(1)} %maximum_convert_fusion.5), kind=kOutput, calls=%fused_computation.13.clone.1 | convolution fusion | flops 15881881600 | bytes 23400448 | tf_op jit(solution)/shard_map/while/body/conv_general_dilated | solution.py:25
  137.4 4.1 %convolution_convert_fusion.3 = bf16[40,19,19,8]{0,3,2,1:T(8,128)(2,1)S(1)} fusion(bf16[40,19,19,256]{3,0,2,1:T(8,128)(2,1)S(1)} %get-tuple-element.223, bf16[256,8]{0,1:T(8,128)(2,1)S(1)} %get-tuple-element.265), kind=kOutput, calls=%fused_computation.19.clone.1 | convolution fusion | flops 59261760 | bytes 7628416 | tf_op jit(solution)/shard_map/while/body/bhwc,cf->bfhw/dot_general | solution.py:43
  143.3 1.4 gather_fusion.1
  144.7 0.8 gather_fusion.4
  145.5 0.8 gather_fusion.10
  146.3 0.8 gather_fusion.7
  147.1 0.8 gather_fusion.11
  148.0 1.5 gather_fusion.8
  149.4 1.0 gather_fusion.12
  150.4 1.5 gather_fusion.9
  151.9 1.0 gather_fusion.5
  152.9 1.0 gather_fusion.2
  154.5 1.7 collective-permute-start.12
  156.8 1.5 collective-permute-start.13
  159.0 3.1 %collective-permute-start.10 = (bf16[16]{0:T(256)(128)(2,1)S(1)}, bf16[16]{0:T(256)(128)(2,1)S(1)}, u32[]{:S(2)}, u32[]{:S(2)}) collective-permute-start(bf16[16]{0:T(256)(128)(2,1)S(1)} %broadcast_select_fusion.12), channel_id=1, source_target_pairs={{0,4},{1,5},{2,6},{3,7},{4,0},{5,1},{6,2},{7,3},{8,12},{9,13},{10,... | collective-permute-start | bytes 104 | tf_op jit(solution)/shard_map/ppermute | solution.py:204
  162.7 1.0 collective-permute-start.11
  164.4 1.0 broadcast_select_fusion.6
  165.4 0.8 broadcast_select_fusion.5
  166.2 1.7 broadcast_select_fusion.4
  167.9 1.0 broadcast_select_fusion.3
  169.0 2.1 %collective-permute-start.5 = (bf16[16,2896]{1,0:T(8,128)(2,1)S(1)}, bf16[16,2896]{1,0:T(8,128)(2,1)}, u32[]{:S(2)}, u32[]{:S(2)}) collective-permute-start(bf16[16,2896]{1,0:T(8,128)(2,1)S(1)} %broadcast_select_fusion.6), channel_id=1, source_target_pairs={{0,4},{1,5},{2,6},{3,7},{4,0},{5,1},{6,2},{7,3},{8,12},{9,13},{10,... | collective-permute-start | bytes 278024 | tf_op jit(solution)/shard_map/ppermute | solution.py:203
  172.4 1.4 gather_fusion.6
  173.8 2.3 %convolution_bitcast_fusion.1 = f32[32,1,8]{2,1,0:T(1,128)} fusion(s32[32,8]{1,0:T(8,128)S(1)} %copy-done.4, s32[128]{0:T(128)} %param.21, bf16[128]{0:T(256)(128)(2,1)S(1)} %gather_fusion.6, s32[]{:T(128)} %bitcast.96, s32[8,256]{1,0:T(8,128)S(1)} %copy-done.12), kind=kOutput, calls=%fused_computation.49 | convolution fusion | flops 427264 | bytes 18948 | tf_op jit(solution)/shard_map/dot_general | solution.py:222
  176.2 4.6 %all-to-all-start.1 = ((f32[32,1,8]{2,1,0:T(1,128)}), f32[32,1,8]{2,1,0:T(1,128)S(1)}, u32[]{:S(2)}, u32[]{:S(2)}) async-start(f32[32,1,8]{2,1,0:T(1,128)} %convolution_bitcast_fusion.1), calls=%async_computation.1 | async-start | bytes 32768 | tf_op jit(solution)/shard_map/all_to_all | solution.py:223
  181.2 6.6 %all-to-all-done.1 = f32[32,1,8]{2,1,0:T(1,128)S(1)} async-done(((f32[32,1,8]{2,1,0:T(1,128)}), f32[32,1,8]{2,1,0:T(1,128)S(1)}, u32[]{:S(2)}, u32[]{:S(2)}) %all-to-all-start.1) | async-done | bytes 1056 | tf_op jit(solution)/shard_map/all_to_all | solution.py:223
  188.4 0.9 constant_dynamic-update-slice_fusion.11
  189.4 0.9 constant_dynamic-update-slice_fusion.8
  190.4 2.0 %gather_fusion.3 = bf16[128,2896]{1,0:T(8,128)(2,1)} fusion(bf16[336,2896]{1,0:T(8,128)(2,1)S(1)} %constant_dynamic-update-slice_fusion.7, s32[1024]{0:T(1024)} %pad_clamp_fusion.1), kind=kCustom, calls=%fused_computation.9 | custom fusion | bytes 1483264 | tf_op jit(solution)/shard_map/jit(_take)/gather | solution.py:210
  192.4 2.3 %reshape.372 = bf16[128,8,362]{2,1,0:T(8,128)(2,1)S(1)} reshape(bf16[128,2896]{1,0:T(8,128)(2,1)} %gather_fusion.3) | data formatting | bytes 1482752 | tf_op jit(solution)/shard_map/jit(_take)/gather | solution.py:210
  194.7 0.7 copy.48
  196.6 1.7 divide_select_fusion
  (99 shorter events, 18.5 us)
Async XLA Ops:
  1.9 15.4 %all-to-all-start = ((s32[32,1,1]{2,1,0:T(1,128)}), s32[32,1,1]{2,1,0:T(1,128)S(1)}, u32[]{:S(2)}, u32[]{:S(2)}) async-start(s32[32,1,1]{2,1,0:T(1,128)} %broadcast_in_dim.122), calls=%async_computation | async-start | bytes 32768 | tf_op jit(solution)/shard_map/all_to_all | solution.py:154
  13.2 1.9 copy-start.1
  44.9 27.1 %collective-permute-start.1 = (bf16[32,11552]{1,0:T(8,128)(2,1)}, bf16[32,11552]{1,0:T(8,128)(2,1)}, u32[]{:S(2)}, u32[]{:S(2)}) collective-permute-start(bf16[32,11552]{1,0:T(8,128)(2,1)} %get-tuple-element.127), channel_id=1, source_target_pairs={{0,2},{1,3},{2,0},{3,1},{4,6},{5,7},{6,4},{7,5},{8,10},{9,11},{10,... | collective-permute-start | bytes 2217992 | tf_op jit(solution)/shard_map/ppermute | solution.py:175
  48.2 23.0 %collective-permute-start = (bf16[16,11552]{1,0:T(8,128)(2,1)}, bf16[16,11552]{1,0:T(8,128)(2,1)S(1)}, u32[]{:S(2)}, u32[]{:S(2)}) collective-permute-start(bf16[16,11552]{1,0:T(8,128)(2,1)} %pad_dynamic-slice_fusion.4), channel_id=1, source_target_pairs={{0,4},{1,5},{2,6},{3,7},{4,0},{5,1},{6,2},{7,3},{8,12},{9,13},{10,... | collective-permute-start | bytes 1109000 | tf_op jit(solution)/shard_map/ppermute | solution.py:175
  50.7 23.4 %collective-permute-start.2 = (bf16[32,11552]{1,0:T(8,128)(2,1)}, bf16[32,11552]{1,0:T(8,128)(2,1)}, u32[]{:S(2)}, u32[]{:S(2)}) collective-permute-start(bf16[32,11552]{1,0:T(8,128)(2,1)} %get-tuple-element.128), channel_id=1, source_target_pairs={{0,16},{1,17},{2,18},{3,19},{4,20},{5,21},{6,22},{7,23},{8,24},{9,... | collective-permute-start | bytes 2217992 | tf_op jit(solution)/shard_map/ppermute | solution.py:175
  52.2 24.0 %collective-permute-start.3 = (bf16[32,11552]{1,0:T(8,128)(2,1)}, bf16[32,11552]{1,0:T(8,128)(2,1)}, u32[]{:S(2)}, u32[]{:S(2)}) collective-permute-start(bf16[32,11552]{1,0:T(8,128)(2,1)} %get-tuple-element.126), channel_id=1, source_target_pairs={{0,1},{1,0},{2,3},{3,2},{4,5},{5,4},{6,7},{7,6},{8,9},{9,8},{10,11... | collective-permute-start | bytes 2217992 | tf_op jit(solution)/shard_map/ppermute | solution.py:175
  58.9 19.4 %collective-permute-start.4 = (bf16[64,11552]{1,0:T(8,128)(2,1)}, bf16[64,11552]{1,0:T(8,128)(2,1)S(1)}, u32[]{:S(2)}, u32[]{:S(2)}) collective-permute-start(bf16[64,11552]{1,0:T(8,128)(2,1)} %pad_dynamic-slice_fusion), channel_id=1, source_target_pairs={{0,8},{1,9},{2,10},{3,11},{4,12},{5,13},{6,14},{7,15},{8,0},{9,1},... | collective-permute-start | bytes 4435976 | tf_op jit(solution)/shard_map/ppermute | solution.py:175
  76.1 3.5 %copy-start.2 = (bf16[256,8]{0,1:T(8,128)(2,1)S(1)}, bf16[256,8]{0,1:T(8,128)(2,1)}, u32[]{:S(2)}) copy-start(bf16[256,8]{0,1:T(8,128)(2,1)} %param.26) | copy-start | bytes 12292
  76.1 3.5 %copy-start.3 = (bf16[256,8]{0,1:T(8,128)(2,1)S(1)}, bf16[256,8]{0,1:T(8,128)(2,1)}, u32[]{:S(2)}) copy-start(bf16[256,8]{0,1:T(8,128)(2,1)} %param.27) | copy-start | bytes 12292
  76.1 3.5 %copy-start.13 = (bf16[1,3,3,256,256]{4,3,2,1,0:T(8,128)(2,1)S(1)}, bf16[1,3,3,256,256]{4,3,2,1,0:T(8,128)(2,1)}, u32[]{:S(2)}) copy-start(bf16[1,3,3,256,256]{4,3,2,1,0:T(8,128)(2,1)} %param.24) | copy-start | bytes 3538948
  76.1 3.6 %copy-start.15 = (bf16[3,3,32,256]{3,2,1,0:T(8,128)(2,1)S(1)}, bf16[3,3,32,256]{3,2,1,0:T(8,128)(2,1)}, u32[]{:S(2)}) copy-start(bf16[3,3,32,256]{3,2,1,0:T(8,128)(2,1)} %param.23) | copy-start | bytes 442372
  76.1 3.6 %copy-start.16 = (bf16[256]{0:T(256)(128)(2,1)S(1)}, bf16[256]{0:T(256)(128)(2,1)}, u32[]{:S(2)}) copy-start(bf16[256]{0:T(256)(128)(2,1)} %param.28) | copy-start | bytes 1540
  100.5 18.3 %copy-start.14 = (bf16[1,3,3,256,256]{4,3,2,1,0:T(8,128)(2,1)S(1)}, bf16[1,3,3,256,256]{4,3,2,1,0:T(8,128)(2,1)}, u32[]{:S(2)}) copy-start(bf16[1,3,3,256,256]{4,3,2,1,0:T(8,128)(2,1)} %get-tuple-element.264) | copy-start | bytes 3538948 | tf_op jit(solution)/shard_map/while
  149.4 15.0 %copy-start.11 = (pred[16]{0:T(512)(128)(4,1)S(1)}, pred[16]{0:T(512)(128)(4,1)}, u32[]{:S(2)}) copy-start(pred[16]{0:T(512)(128)(4,1)} %compare_and_fusion.5) | copy-start | bytes 52
  150.4 15.0 %copy-start.10 = (pred[32]{0:T(512)(128)(4,1)S(1)}, pred[32]{0:T(512)(128)(4,1)}, u32[]{:S(2)}) copy-start(pred[32]{0:T(512)(128)(4,1)} %compare_and_fusion.3) | copy-start | bytes 100
  150.4 15.8 %copy-start.7 = (pred[32]{0:T(512)(128)(4,1)S(1)}, pred[32]{0:T(512)(128)(4,1)}, u32[]{:S(2)}) copy-start(pred[32]{0:T(512)(128)(4,1)} %compare_and_fusion.2) | copy-start | bytes 100
  150.4 17.5 %copy-start.8 = (pred[32]{0:T(512)(128)(4,1)S(1)}, pred[32]{0:T(512)(128)(4,1)}, u32[]{:S(2)}) copy-start(pred[32]{0:T(512)(128)(4,1)} %compare_and_fusion.1) | copy-start | bytes 100
  151.8 17.0 %copy-start.9 = (pred[64]{0:T(512)(128)(4,1)S(1)}, pred[64]{0:T(512)(128)(4,1)}, u32[]{:S(2)}) copy-start(pred[64]{0:T(512)(128)(4,1)} %compare_and_fusion.4) | copy-start | bytes 196
  152.9 20.9 %copy-start.4 = (s32[32,8]{1,0:T(8,128)S(1)}, s32[32,8]{1,0:T(8,128)}, u32[]{:S(2)}) copy-start(s32[32,8]{1,0:T(8,128)} %multiply_add_fusion) | copy-start | bytes 3076
  152.9 21.0 %copy-start.12 = (s32[8,256]{1,0:T(8,128)S(1)}, s32[8,256]{1,0:T(8,128)}, u32[]{:S(2)}) copy-start(s32[8,256]{1,0:T(8,128)} %get-tuple-element.83) | copy-start | bytes 24580
  154.5 16.7 %collective-permute-start.12 = (bf16[32]{0:T(256)(128)(2,1)S(1)}, bf16[32]{0:T(256)(128)(2,1)S(1)}, u32[]{:S(2)}, u32[]{:S(2)}) collective-permute-start(bf16[32]{0:T(256)(128)(2,1)S(1)} %broadcast_select_fusion.9), channel_id=1, source_target_pairs={{0,16},{1,17},{2,18},{3,19},{4,20},{5,21},{6,22},{7,23},{8,24},{9,... | collective-permute-start | bytes 200 | tf_op jit(solution)/shard_map/ppermute | solution.py:204
  156.8 14.3 %collective-permute-start.13 = (bf16[32]{0:T(256)(128)(2,1)S(1)}, bf16[32]{0:T(256)(128)(2,1)S(1)}, u32[]{:S(2)}, u32[]{:S(2)}) collective-permute-start(bf16[32]{0:T(256)(128)(2,1)S(1)} %broadcast_select_fusion.8), channel_id=1, source_target_pairs={{0,1},{1,0},{2,3},{3,2},{4,5},{5,4},{6,7},{7,6},{8,9},{9,8},{10,11... | collective-permute-start | bytes 200 | tf_op jit(solution)/shard_map/ppermute | solution.py:204
  159.0 10.1 %collective-permute-start.10 = (bf16[16]{0:T(256)(128)(2,1)S(1)}, bf16[16]{0:T(256)(128)(2,1)S(1)}, u32[]{:S(2)}, u32[]{:S(2)}) collective-permute-start(bf16[16]{0:T(256)(128)(2,1)S(1)} %broadcast_select_fusion.12), channel_id=1, source_target_pairs={{0,4},{1,5},{2,6},{3,7},{4,0},{5,1},{6,2},{7,3},{8,12},{9,13},{10,... | collective-permute-start | bytes 104 | tf_op jit(solution)/shard_map/ppermute | solution.py:204
  162.7 9.1 %collective-permute-start.11 = (bf16[32]{0:T(256)(128)(2,1)S(1)}, bf16[32]{0:T(256)(128)(2,1)S(1)}, u32[]{:S(2)}, u32[]{:S(2)}) collective-permute-start(bf16[32]{0:T(256)(128)(2,1)S(1)} %broadcast_select_fusion.10), channel_id=1, source_target_pairs={{0,2},{1,3},{2,0},{3,1},{4,6},{5,7},{6,4},{7,5},{8,10},{9,11},{10,... | collective-permute-start | bytes 200 | tf_op jit(solution)/shard_map/ppermute | solution.py:204
  164.3 8.0 %collective-permute-start.14 = (bf16[64]{0:T(256)(128)(2,1)S(1)}, bf16[64]{0:T(256)(128)(2,1)S(1)}, u32[]{:S(2)}, u32[]{:S(2)}) collective-permute-start(bf16[64]{0:T(256)(128)(2,1)S(1)} %broadcast_select_fusion.11), channel_id=1, source_target_pairs={{0,8},{1,9},{2,10},{3,11},{4,12},{5,13},{6,14},{7,15},{8,0},{9,1},... | collective-permute-start | bytes 392 | tf_op jit(solution)/shard_map/ppermute | solution.py:204
  169.0 19.4 %collective-permute-start.5 = (bf16[16,2896]{1,0:T(8,128)(2,1)S(1)}, bf16[16,2896]{1,0:T(8,128)(2,1)}, u32[]{:S(2)}, u32[]{:S(2)}) collective-permute-start(bf16[16,2896]{1,0:T(8,128)(2,1)S(1)} %broadcast_select_fusion.6), channel_id=1, source_target_pairs={{0,4},{1,5},{2,6},{3,7},{4,0},{5,1},{6,2},{7,3},{8,12},{9,13},{10,... | collective-permute-start | bytes 278024 | tf_op jit(solution)/shard_map/ppermute | solution.py:203
  171.2 18.2 %collective-permute-start.6 = (bf16[32,2896]{1,0:T(8,128)(2,1)}, bf16[32,2896]{1,0:T(8,128)(2,1)S(1)}, u32[]{:S(2)}, u32[]{:S(2)}) collective-permute-start(bf16[32,2896]{1,0:T(8,128)(2,1)} %broadcast_select_fusion.5), channel_id=1, source_target_pairs={{0,2},{1,3},{2,0},{3,1},{4,6},{5,7},{6,4},{7,5},{8,10},{9,11},{10,... | collective-permute-start | bytes 556040 | tf_op jit(solution)/shard_map/ppermute | solution.py:203
  171.2 18.2 %collective-permute-start.7 = (bf16[32,2896]{1,0:T(8,128)(2,1)}, bf16[32,2896]{1,0:T(8,128)(2,1)S(1)}, u32[]{:S(2)}, u32[]{:S(2)}) collective-permute-start(bf16[32,2896]{1,0:T(8,128)(2,1)} %broadcast_select_fusion.4), channel_id=1, source_target_pairs={{0,16},{1,17},{2,18},{3,19},{4,20},{5,21},{6,22},{7,23},{8,24},{9,... | collective-permute-start | bytes 556040 | tf_op jit(solution)/shard_map/ppermute | solution.py:203
  171.8 17.6 %collective-permute-start.8 = (bf16[32,2896]{1,0:T(8,128)(2,1)S(1)}, bf16[32,2896]{1,0:T(8,128)(2,1)}, u32[]{:S(2)}, u32[]{:S(2)}) collective-permute-start(bf16[32,2896]{1,0:T(8,128)(2,1)S(1)} %broadcast_select_fusion.3), channel_id=1, source_target_pairs={{0,1},{1,0},{2,3},{3,2},{4,5},{5,4},{6,7},{7,6},{8,9},{9,8},{10,11... | collective-permute-start | bytes 556040 | tf_op jit(solution)/shard_map/ppermute | solution.py:203
  172.3 18.0 %collective-permute-start.9 = (bf16[64,2896]{1,0:T(8,128)(2,1)S(1)}, bf16[64,2896]{1,0:T(8,128)(2,1)S(1)}, u32[]{:S(2)}, u32[]{:S(2)}) collective-permute-start(bf16[64,2896]{1,0:T(8,128)(2,1)S(1)} %broadcast_select_fusion.2), channel_id=1, source_target_pairs={{0,8},{1,9},{2,10},{3,11},{4,12},{5,13},{6,14},{7,15},{8,0},{9,1},... | collective-permute-start | bytes 1112072 | tf_op jit(solution)/shard_map/ppermute | solution.py:203
  176.2 11.7 %all-to-all-start.1 = ((f32[32,1,8]{2,1,0:T(1,128)}), f32[32,1,8]{2,1,0:T(1,128)S(1)}, u32[]{:S(2)}, u32[]{:S(2)}) async-start(f32[32,1,8]{2,1,0:T(1,128)} %convolution_bitcast_fusion.1), calls=%async_computation.1 | async-start | bytes 32768 | tf_op jit(solution)/shard_map/all_to_all | solution.py:223
  192.4 3.0 %copy-start = (pred[128,8,361]{0,1,2:T(8,128)(4,1)S(1)}, pred[128,8,361]{0,1,2:T(8,128)(4,1)}, u32[]{:S(2)}) copy-start(pred[128,8,361]{0,1,2:T(8,128)(4,1)} %broadcast_compare_fusion) | copy-start | bytes 1108996
  192.4 3.0 %copy-start.5 = (f32[8]{0:T(128)S(1)}, f32[8]{0:T(128)}, u32[]{:S(2)}) copy-start(f32[8]{0:T(128)} %param.29) | copy-start | bytes 100
  192.4 4.2 %copy-start.6 = (pred[128]{0:T(512)(128)(4,1)S(1)}, pred[128]{0:T(512)(128)(4,1)}, u32[]{:S(2)}) copy-start(pred[128]{0:T(512)(128)(4,1)} %iota_compare_fusion) | copy-start | bytes 388
where the time goes:
time: 199 us; the launch traced here: 198 us
  local copies, waits for them, and re-layouts  53.3 us (27%)
  matrix products  50.2 us (25%)
  other arithmetic  31.8 us (16%)
  starting transfers between devices  29.7 us (15%)
  waiting for transfers between devices  17 us (9%)
  between operations  11.1 us (6%)
  Pallas kernels  4.62 us (2%)
    conv_general_dilated x3, matrix products, convolve(): lax.conv_general_dilated(inputs, kernel, (1, 1), 'SAME', dimension_number...  43.5 us
    unnamed x43, local copies, waits for them, and re-layouts  14.3 us
    gather x2, local copies, waits for them, and re-layouts, step(): logits, values = evaluate(jnp.take(pool, idx, axis=0), *weights)  10.9 us
    ppermute x5, waiting for transfers between devices, body(): lax.ppermute(lax.dynamic_slice(padded, (starts[e], 0), (cap, row)), AXES,...  10.4 us
    select_n x9, other arithmetic, body(): jnp.take(work_logits, idx, axis=0)  7.61 us
    ppermute x5, starting transfers between devices, body(): lax.ppermute(jnp.take(work_values, idx, axis=0), AXES, pairs[e])  7.36 us
    all_to_all x1, starting transfers between devices, body(): lax.all_to_all(jnp.broadcast_to(counts, (groups, 1)), AXES, 0, 0, tiled=T...  7.33 us
    ppermute x5, starting transfers between devices, body(): lax.ppermute(lax.dynamic_slice(padded, (starts[e], 0), (cap, row)), AXES,...  7.16 us
  transfers between devices with their start and end apart: 17, of which 3 were waited for; matrix products, arithmetic and copies ran while one was open for 18% of the time, Pallas kernels for 0%

commit v1 on v0

--- a/solution.py
+++ b/solution.py
@@ -103,7 +103,7 @@
     work_idx = k
     pick = k
     work_base = slot_count
-    pick_base = work_rows
+    pick_base = work_rows + max(caps)
     for e, cap in enumerate(caps):
         place, got_e = mine(places[e]), mine(into[e])
         work_idx = jnp.where((k >= place) & (k < place + got_e), work_base + k - place, work_idx)
@@ -111,7 +111,7 @@
         pick = jnp.where((k >= start) & (k < start + sent_e), pick_base + k - start, pick)
         work_base = work_base + cap
         pick_base = pick_base + cap
-    work_idx = jnp.clip(work_idx, 0, work_base - 1)
+    work_idx = jnp.where(k < mine(keep + sum(into)), jnp.clip(work_idx, 0, work_base - 1), work_base - 1)
     pick = jnp.clip(pick, 0, pick_base - 1)
     idx_ref[...] = jnp.concatenate([work_idx, pick] + [k * 0] * (idx_ref.shape[0] - 2), axis=0)
 
@@ -183,7 +183,8 @@
     def step(t, carry):
         logits_acc, values_acc = carry
         idx = lax.dynamic_slice(work_idx, (t * CHUNK,), (CHUNK,))
-        logits, values = evaluate(jnp.take(pool, idx, axis=0), *weights)
+        rows = jnp.take(pool, idx, axis=0, mode="clip", indices_are_sorted=True)
+        logits, values = evaluate(rows, *weights)
         logits_acc = lax.dynamic_update_slice(
             logits_acc, logits.reshape(CHUNK, flat), (t * CHUNK, 0)
         )
@@ -194,21 +195,25 @@
         0,
         (work_count + CHUNK - 1) // CHUNK,
         step,
-        (jnp.zeros((work_rows, flat), jnp.bfloat16), jnp.zeros((work_rows,), jnp.bfloat16)),
+        (
+            jnp.zeros((work_rows + margin, flat), jnp.bfloat16),
+            jnp.zeros((work_rows + margin,), jnp.bfloat16),
+        ),
     )
 
     back_logits, back_values = [], []
     for e, cap in enumerate(caps):
-        idx = jnp.clip(places[e] + jnp.arange(cap, dtype=jnp.int32), 0, work_rows - 1)
-        back_logits.append(lax.ppermute(jnp.take(work_logits, idx, axis=0), AXES, pairs[e]))
-        back_values.append(lax.ppermute(jnp.take(work_values, idx, axis=0), AXES, pairs[e]))
+        window = lax.dynamic_slice(work_logits, (places[e], 0), (cap, flat))
+        back_logits.append(lax.ppermute(window, AXES, pairs[e]))
+        window = lax.dynamic_slice(work_values, (places[e],), (cap,))
+        back_values.append(lax.ppermute(window, AXES, pairs[e]))
 
     all_logits = jnp.concatenate([work_logits] + back_logits, axis=0)
     all_values = jnp.concatenate([work_values] + back_values, axis=0)
     slot = jnp.arange(slot_count, dtype=jnp.int32)
     pick = lists[1, :slot_count]
-    slot_logits = jnp.take(all_logits, pick, axis=0).reshape(slot_count, FACT, MOVES)
-    slot_values = jnp.take(all_values, pick, axis=0)
+    slot_logits = jnp.take(all_logits, pick, axis=0, mode="clip").reshape(slot_count, FACT, MOVES)
+    slot_values = jnp.take(all_values, pick, axis=0, mode="clip")
 
     alive = slot < own_count
     priors = jnp.where(

time: 199 us -> 184 us (0.925)
  other arithmetic: 31.8 us -> 7.67 us
  between operations: 11.1 us -> 20.9 us
  matrix products: 50.2 us -> 54.1 us
  local copies, waits for them, and re-layouts: 53.3 us -> 50 us
    gather x16 -> x4, local copies, waits for them, and re-layouts: 27.9 us -> 10.5 us  [the longest x1 6.82 us: step(): rows = jnp.take(pool, idx, axis=0, mode='clip', indices_are_sorted=True)]
    select_n x16 -> x0, other arithmetic: 14.2 us -> none  [the longest x9 7.61 us: body(): jnp.take(work_logits, idx, axis=0)]
    and x6 -> x0, other arithmetic: 5.98 us -> none  [the longest x5 5.89 us: body(): jnp.take(work_logits, idx, axis=0)]
    all_to_all x1, waiting for transfers between devices: 6.63 us -> 1.3 us  [body(): lax.all_to_all(partial_sums.reshape(groups, TREE_DEV), AXES, 0, 0, tiled=...]
    ppermute x10, waiting for transfers between devices: 0.03 us -> 3.71 us  [the longest x5 3.56 us: body(): back_values.append(lax.ppermute(window, AXES, pairs[e]))]
    unnamed x43 -> x33, local copies, waits for them, and re-layouts: 14.3 us -> 17.7 us
    reshape x0 -> x1, local copies, waits for them, and re-layouts: none -> 3.3 us  [evaluate(): board = batch.reshape(leaves, SIDE, SIDE, PLANES)]
    dot_general x1, matrix products: 4.11 us -> 7.22 us  [evaluate(): jnp.einsum('bhwc,cf->bfhw', hidden, policy_weight, preferred_element_type...]
  transfers between devices with their start and end apart: 17 -> 17, of which waited for: 3 -> 4; matrix products, arithmetic and copies ran while one was open for 18% -> 14% of each run, Pallas kernels for 0% -> 0%
where the time goes in v1:
time: 184 us; the launch traced here: 183 us
  matrix products  54.1 us (29%)
  local copies, waits for them, and re-layouts  50 us (27%)
  starting transfers between devices  29.6 us (16%)
  between operations  20.9 us (11%)
  waiting for transfers between devices  15.3 us (8%)
  other arithmetic  7.67 us (4%)
  Pallas kernels  4.6 us (2%)
    conv_general_dilated x3, matrix products, convolve(): lax.conv_general_dilated(inputs, kernel, (1, 1), 'SAME', dimension_number...  46.5 us
    unnamed x33, local copies, waits for them, and re-layouts  17.7 us
    ppermute x5, waiting for transfers between devices, body(): lax.ppermute(lax.dynamic_slice(padded, (starts[e], 0), (cap, row)), AXES,...  10.3 us
    all_to_all x1, starting transfers between devices, body(): lax.all_to_all(jnp.broadcast_to(counts, (groups, 1)), AXES, 0, 0, tiled=T...  7.33 us
    dot_general x1, matrix products, evaluate(): jnp.einsum('bhwc,cf->bfhw', hidden, policy_weight, preferred_element_type...  7.22 us
    ppermute x5, starting transfers between devices, body(): lax.ppermute(lax.dynamic_slice(padded, (starts[e], 0), (cap, row)), AXES,...  7.16 us
    ppermute x5, starting transfers between devices, body(): back_values.append(lax.ppermute(window, AXES, pairs[e]))  7.04 us
    gather x1, local copies, waits for them, and re-layouts, step(): rows = jnp.take(pool, idx, axis=0, mode='clip', indices_are_sorted=True)  6.82 us
  transfers between devices with their start and end apart: 17, of which 4 were waited for; matrix products, arithmetic and copies ran while one was open for 14% of the time, Pallas kernels for 0%

profile of v1, /device:TPU:0, one launch (start us, length us, event | category | flops | bytes accessed | tf_op | source)
XLA Modules:
  0.0 182.7 jit_solution(12278408744323564421)
XLA Ops:
  1.3 0.6 broadcast_in_dim.59
  1.9 7.3 %all-to-all-start = ((s32[32,1,1]{2,1,0:T(1,128)}), s32[32,1,1]{2,1,0:T(1,128)S(1)}, u32[]{:S(2)}, u32[]{:S(2)}) async-start(s32[32,1,1]{2,1,0:T(1,128)} %broadcast_in_dim.59), calls=%async_computation | async-start | bytes 32768 | tf_op jit(solution)/shard_map/all_to_all | solution.py:154
  9.2 3.4 %copy.48 = bf16[128,11552]{1,0:T(8,128)(2,1)S(1)} copy(bf16[128,11552]{0,1:T(8,128)(2,1)} %param.15) | data formatting | bytes 5914624 | tf_op args[0]
  12.6 1.9 %constant_dynamic-update-slice_fusion.6 = bf16[304,11552]{1,0:T(8,128)(2,1)} fusion(bf16[128,11552]{1,0:T(8,128)(2,1)S(1)} %copy.48), kind=kLoop, calls=%fused_computation.45 | loop fusion | bytes 5939200
  14.5 1.0 broadcast_compare_fusion
  16.0 0.7 compare_reduce_fusion
  16.6 1.3 fusion.15
  17.9 0.6 scatter.4.counts_ref
  19.0 4.6 %shard_map.130 = (s32[24,128]{1,0:T(8,128)}, s32[8,256]{1,0:T(8,128)}) custom-call(s32[1,128]{1,0:T(1,128)} %scatter.4.counts_ref, s32[1,128]{1,0:T(1,128)} %broadcast_in_dim.60.me_ref), custom_call_target="tpu_custom_call" | custom-call | tf_op jit(solution)/shard_map/pallas_call | solution.py:125
  23.6 1.6 fusion.17
  40.3 1.9 %pad_dynamic-slice_fusion.1 = (bf16[32,11552]{1,0:T(8,128)(2,1)}, bf16[32,11552]{1,0:T(8,128)(2,1)}, bf16[32,11552]{1,0:T(8,128)(2,1)}) fusion(s32[]{:T(128)S(6)} %select_n.70, bf16[128,11552]{1,0:T(8,128)(2,1)S(1)} %copy.48, s32[]{:T(128)S(6)} %select_n.68, s32[]{:T(128)S(6)} %select_n.69), kind=kLoop, calls=%fused_computation.26 | loop fusion | bytes 5175308 | tf_op jit(solution)/shard_map/dynamic_slice | solution.py:175
  42.1 1.8 collective-permute-start.1
  44.5 0.9 pad_dynamic-slice_fusion.4
  45.5 2.4 %collective-permute-start = (bf16[16,11552]{1,0:T(8,128)(2,1)}, bf16[16,11552]{1,0:T(8,128)(2,1)S(1)}, u32[]{:S(2)}, u32[]{:S(2)}) collective-permute-start(bf16[16,11552]{1,0:T(8,128)(2,1)} %pad_dynamic-slice_fusion.4), channel_id=1, source_target_pairs={{0,4},{1,5},{2,6},{3,7},{4,0},{5,1},{6,2},{7,3},{8,12},{9,13},{10,... | collective-permute-start | bytes 1109000 | tf_op jit(solution)/shard_map/ppermute | solution.py:175
  47.9 1.5 collective-permute-start.2
  49.4 1.5 collective-permute-start.3
  51.5 1.6 pad_dynamic-slice_fusion
  53.1 0.7 slice.67
  56.9 0.7 slice_bitcast_fusion
  57.6 0.6 pad_clamp_fusion.1
  58.2 10.3 %collective-permute-done = bf16[16,11552]{1,0:T(8,128)(2,1)S(1)} collective-permute-done((bf16[16,11552]{1,0:T(8,128)(2,1)}, bf16[16,11552]{1,0:T(8,128)(2,1)S(1)}, u32[]{:S(2)}, u32[]{:S(2)}) %collective-permute-start) | collective-permute-done | bytes 369696 | tf_op jit(solution)/shard_map/ppermute | solution.py:175
  68.4 0.8 constant_dynamic-update-slice_fusion.5
  69.3 2.0 %constant_dynamic-update-slice_fusion.4 = bf16[304,11552]{1,0:T(8,128)(2,1)} fusion(bf16[304,11552]{1,0:T(8,128)(2,1)} %constant_dynamic-update-slice_fusion.5, bf16[32,11552]{1,0:T(8,128)(2,1)} %collective-permute-done.1), kind=kLoop, calls=%fused_computation.43 | loop fusion | bytes 1490944
  71.3 2.1 %constant_dynamic-update-slice_fusion.3 = bf16[304,11552]{1,0:T(8,128)(2,1)} fusion(bf16[304,11552]{1,0:T(8,128)(2,1)} %constant_dynamic-update-slice_fusion.4, bf16[32,11552]{1,0:T(8,128)(2,1)} %collective-permute-done.2), kind=kLoop, calls=%fused_computation.42 | loop fusion | bytes 1490944
  73.4 2.1 %constant_dynamic-update-slice_fusion.2 = bf16[304,11552]{1,0:T(8,128)(2,1)} fusion(bf16[304,11552]{1,0:T(8,128)(2,1)} %constant_dynamic-update-slice_fusion.3, bf16[32,11552]{1,0:T(8,128)(2,1)} %collective-permute-done.3), kind=kLoop, calls=%fused_computation.41 | loop fusion | bytes 1490944
  75.5 1.2 constant_dynamic-update-slice_fusion.1
  76.7 1.1 broadcast_in_dim.57
  77.9 66.6 %while.13 = (s32[]{:T(128)}, bf16[224,2896]{1,0:T(8,128)(2,1)}, bf16[224]{0:T(256)(128)(2,1)S(1)}, s32[]{:T(128)}, s32[160]{0:T(256)S(1)}, /*index=5*/bf16[304,1...) while((s32[]{:T(128)}, bf16[224,2896]{1,0:T(8,128)(2,1)}, ...), condition=%wide.region_3.4_spmd, body=%wide.region_1.3_spmd.sunk | while | flops 33799694336 | bytes 70544528 | solution.py:194
  78.2 6.8 %gather_fusion = bf16[40,11552]{1,0:T(8,128)(2,1)} fusion(bf16[304,11552]{1,0:T(8,128)(2,1)} %get-tuple-element.257, s32[1024]{0:T(1024)S(1)} %pad_clamp_fusion.3), kind=kCustom, calls=%fused_computation.clone.1 | custom fusion | bytes 1848480 | tf_op jit(solution)/shard_map/while/body/jit(_take)/gather | solution.py:186
  85.0 3.3 %copy.66 = bf16[40,11552]{0,1:T(8,128)(2,1)S(1)} copy(bf16[40,11552]{1,0:T(8,128)(2,1)} %gather_fusion) | data formatting | bytes 1848320 | tf_op jit(solution)/shard_map/while/body/reshape | solution.py:37
  88.3 8.2 %maximum_convert_fusion.5 = bf16[40,19,19,256]{3,0,2,1:T(8,128)(2,1)S(1)} fusion(bf16[40,19,19,32]{0,3,2,1:T(8,128)(2,1)S(1)} %bitcast.87, bf16[3,3,32,256]{3,2,1,0:T(8,128)(2,1)S(1)} %get-tuple-element.258), kind=kOutput, calls=%fused_computation.6.clone.1 | convolution fusion | flops 1989857280 | bytes 8464896 | tf_op jit(solution)/shard_map/while/body/conv_general_dilated | solution.py:25
  96.5 18.3 %maximum_convert_fusion.6 = bf16[40,19,19,256]{3,0,2,1:T(8,128)(2,1)S(1)} fusion(bf16[40,19,19,256]{3,0,2,1:T(8,128)(2,1)S(1)} %maximum_convert_fusion.5, bf16[1,3,3,256,256]{4,3,2,1,0:T(8,128)(2,1)S(1)} %copy-done.8), kind=kOutput, calls=%fused_computation.5.clone.1 | convolution fusion | flops 15867105280 | bytes 15966208 | tf_op jit(solution)/shard_map/while/body/conv_general_dilated | solution.py:25
  114.9 19.9 %convert_reduce_fusion.2 = (f32[40,256]{1,0:T(8,128)S(1)}, bf16[40,19,19,256]{3,0,2,1:T(8,128)(2,1)}) fusion(bf16[40,19,19,256]{3,0,2,1:T(8,128)(2,1)S(1)} %maximum_convert_fusion.6, bf16[1,3,3,256,256]{4,3,2,1,0:T(8,128)(2,1)S(1)} %copy-done.9, bf16[40,19,19,256]{3,0,2,1:T(8,128)(2,1)S(1)} %maximum_convert_fusion.5), kind=kOutput, calls=%fused_computation.3.clone.1 | convolution fusion | flops 15881881600 | bytes 23400448 | tf_op jit(solution)/shard_map/while/body/conv_general_dilated | solution.py:25
  135.1 7.2 %convolution_convert_fusion.3 = bf16[40,19,19,8]{0,3,2,1:T(8,128)(2,1)S(1)} fusion(bf16[40,19,19,256]{3,0,2,1:T(8,128)(2,1)} %get-tuple-element.217, bf16[256,8]{0,1:T(8,128)(2,1)S(1)} %get-tuple-element.261), kind=kOutput, calls=%fused_computation.7.clone.1 | convolution fusion | flops 59261760 | bytes 7628416 | tf_op jit(solution)/shard_map/while/body/bhwc,cf->bfhw/dot_general | solution.py:43
  142.4 0.6 copy.68
  143.3 0.7 constant_dynamic-update-slice_fusion.14
  144.5 1.5 constant_dynamic-update-slice_fusion.12
  146.2 0.7 constant_dynamic-slice_fusion.4
  147.0 0.8 constant_dynamic-slice_fusion.1
  147.8 3.2 %collective-permute-start.11 = (bf16[32]{0:T(256)(128)(2,1)S(1)}, bf16[32]{0:T(256)(128)(2,1)S(1)}, u32[]{:S(2)}, u32[]{:S(2)}) collective-permute-start(bf16[32]{0:T(256)(128)(2,1)S(1)} %get-tuple-element.139), channel_id=1, source_target_pairs={{0,2},{1,3},{2,0},{3,1},{4,6},{5,7},{6,4},{7,5},{8,10},{9,11},{10,... | collective-permute-start | bytes 200 | tf_op jit(solution)/shard_map/ppermute | solution.py:209
  151.1 1.5 collective-permute-start.12
  152.6 1.5 collective-permute-start.13
  154.0 0.8 collective-permute-start.10
  155.0 3.5 %collective-permute-done.10 = bf16[16]{0:T(256)(128)(2,1)S(1)} collective-permute-done((bf16[16]{0:T(256)(128)(2,1)S(1)}, bf16[16]{0:T(256)(128)(2,1)S(1)}, u32[]{:S(2)}, u32[]{:S(2)}) %collective-permute-start.10) | collective-permute-done | bytes 64 | tf_op jit(solution)/shard_map/ppermute | solution.py:209
  158.5 0.8 collective-permute-start.5
  159.5 1.4 gather_fusion.2
  161.1 0.7 all_to_all.11
  161.8 2.6 %all-to-all-start.1 = ((f32[32,1,8]{2,1,0:T(1,128)}), f32[32,1,8]{2,1,0:T(1,128)S(1)}, u32[]{:S(2)}, u32[]{:S(2)}) async-start(f32[32,1,8]{2,1,0:T(1,128)} %bitcast.26), calls=%async_computation.1 | async-start | bytes 32768 | tf_op jit(solution)/shard_map/all_to_all | solution.py:228
  164.4 1.1 constant_dynamic-slice_fusion
  165.5 1.8 collective-permute-start.6
  167.2 1.5 collective-permute-start.7
  168.7 1.5 collective-permute-start.8
  170.2 1.3 all-to-all-done.1
  171.5 0.6 reduce_sum.28
  172.1 0.9 constant_dynamic-update-slice_fusion.11
  173.0 0.9 constant_dynamic-update-slice_fusion.10
  174.0 0.9 constant_dynamic-update-slice_fusion.9
  175.0 0.9 constant_dynamic-update-slice_fusion.8
  176.0 1.2 gather_fusion.1
  177.3 1.2 copy.49
  178.4 1.3 reshape.116
  179.7 0.6 select_reduce_fusion
  180.3 0.6 fusion.12
  180.9 1.8 divide_select_fusion
  (62 shorter events, 3.2 us)
Async XLA Ops:
  1.9 14.8 %all-to-all-start = ((s32[32,1,1]{2,1,0:T(1,128)}), s32[32,1,1]{2,1,0:T(1,128)S(1)}, u32[]{:S(2)}, u32[]{:S(2)}) async-start(s32[32,1,1]{2,1,0:T(1,128)} %broadcast_in_dim.59), calls=%async_computation | async-start | bytes 32768 | tf_op jit(solution)/shard_map/all_to_all | solution.py:154
  12.6 1.9 %copy-start.3 = (s32[128,8,361]{0,1,2:T(8,128)S(1)}, s32[128,8,361]{0,1,2:T(8,128)}, u32[]{:S(2)}) copy-start(s32[128,8,361]{0,1,2:T(8,128)} %param.18) | copy-start | bytes 4435972
  42.1 27.1 %collective-permute-start.1 = (bf16[32,11552]{1,0:T(8,128)(2,1)}, bf16[32,11552]{1,0:T(8,128)(2,1)}, u32[]{:S(2)}, u32[]{:S(2)}) collective-permute-start(bf16[32,11552]{1,0:T(8,128)(2,1)} %get-tuple-element.121), channel_id=1, source_target_pairs={{0,2},{1,3},{2,0},{3,1},{4,6},{5,7},{6,4},{7,5},{8,10},{9,11},{10,... | collective-permute-start | bytes 2217992 | tf_op jit(solution)/shard_map/ppermute | solution.py:175
  45.5 23.0 %collective-permute-start = (bf16[16,11552]{1,0:T(8,128)(2,1)}, bf16[16,11552]{1,0:T(8,128)(2,1)S(1)}, u32[]{:S(2)}, u32[]{:S(2)}) collective-permute-start(bf16[16,11552]{1,0:T(8,128)(2,1)} %pad_dynamic-slice_fusion.4), channel_id=1, source_target_pairs={{0,4},{1,5},{2,6},{3,7},{4,0},{5,1},{6,2},{7,3},{8,12},{9,13},{10,... | collective-permute-start | bytes 1109000 | tf_op jit(solution)/shard_map/ppermute | solution.py:175
  47.9 23.4 %collective-permute-start.2 = (bf16[32,11552]{1,0:T(8,128)(2,1)}, bf16[32,11552]{1,0:T(8,128)(2,1)}, u32[]{:S(2)}, u32[]{:S(2)}) collective-permute-start(bf16[32,11552]{1,0:T(8,128)(2,1)} %get-tuple-element.122), channel_id=1, source_target_pairs={{0,16},{1,17},{2,18},{3,19},{4,20},{5,21},{6,22},{7,23},{8,24},{9,... | collective-permute-start | bytes 2217992 | tf_op jit(solution)/shard_map/ppermute | solution.py:175
  49.4 24.0 %collective-permute-start.3 = (bf16[32,11552]{1,0:T(8,128)(2,1)}, bf16[32,11552]{1,0:T(8,128)(2,1)}, u32[]{:S(2)}, u32[]{:S(2)}) collective-permute-start(bf16[32,11552]{1,0:T(8,128)(2,1)} %get-tuple-element.120), channel_id=1, source_target_pairs={{0,1},{1,0},{2,3},{3,2},{4,5},{5,4},{6,7},{7,6},{8,9},{9,8},{10,11... | collective-permute-start | bytes 2217992 | tf_op jit(solution)/shard_map/ppermute | solution.py:175
  53.1 22.4 %collective-permute-start.4 = (bf16[64,11552]{1,0:T(8,128)(2,1)}, bf16[64,11552]{1,0:T(8,128)(2,1)S(1)}, u32[]{:S(2)}, u32[]{:S(2)}) collective-permute-start(bf16[64,11552]{1,0:T(8,128)(2,1)} %pad_dynamic-slice_fusion), channel_id=1, source_target_pairs={{0,8},{1,9},{2,10},{3,11},{4,12},{5,13},{6,14},{7,15},{8,0},{9,1},... | collective-permute-start | bytes 4435976 | tf_op jit(solution)/shard_map/ppermute | solution.py:175
  75.5 2.4 %copy-start.2 = (bf16[3,3,32,256]{3,2,1,0:T(8,128)(2,1)S(1)}, bf16[3,3,32,256]{3,2,1,0:T(8,128)(2,1)}, u32[]{:S(2)}) copy-start(bf16[3,3,32,256]{3,2,1,0:T(8,128)(2,1)} %param.19) | copy-start | bytes 442372
  75.5 2.4 %copy-start.4 = (bf16[256,8]{0,1:T(8,128)(2,1)S(1)}, bf16[256,8]{0,1:T(8,128)(2,1)}, u32[]{:S(2)}) copy-start(bf16[256,8]{0,1:T(8,128)(2,1)} %param.22) | copy-start | bytes 12292
  75.5 2.4 %copy-start.5 = (bf16[256,8]{0,1:T(8,128)(2,1)S(1)}, bf16[256,8]{0,1:T(8,128)(2,1)}, u32[]{:S(2)}) copy-start(bf16[256,8]{0,1:T(8,128)(2,1)} %param.23) | copy-start | bytes 12292
  75.5 2.4 %copy-start.10 = (bf16[256]{0:T(256)(128)(2,1)S(1)}, bf16[256]{0:T(256)(128)(2,1)}, u32[]{:S(2)}) copy-start(bf16[256]{0:T(256)(128)(2,1)} %param.24) | copy-start | bytes 1540
  88.3 8.2 %copy-start.8 = (bf16[1,3,3,256,256]{4,3,2,1,0:T(8,128)(2,1)S(1)}, bf16[1,3,3,256,256]{4,3,2,1,0:T(8,128)(2,1)}, u32[]{:S(2)}) copy-start(bf16[1,3,3,256,256]{4,3,2,1,0:T(8,128)(2,1)} %get-tuple-element.259) | copy-start | bytes 3538948 | tf_op jit(solution)/shard_map/while
  96.5 18.4 %copy-start.9 = (bf16[1,3,3,256,256]{4,3,2,1,0:T(8,128)(2,1)S(1)}, bf16[1,3,3,256,256]{4,3,2,1,0:T(8,128)(2,1)}, u32[]{:S(2)}) copy-start(bf16[1,3,3,256,256]{4,3,2,1,0:T(8,128)(2,1)} %get-tuple-element.260) | copy-start | bytes 3538948 | tf_op jit(solution)/shard_map/while
  144.5 1.7 copy-start
  144.5 16.4 %copy-start.11 = (s32[128]{0:T(128)S(1)}, s32[128]{0:T(128)}, u32[]{:S(2)}) copy-start(s32[128]{0:T(128)} %param.17) | copy-start | bytes 1540
  147.8 11.5 %collective-permute-start.11 = (bf16[32]{0:T(256)(128)(2,1)S(1)}, bf16[32]{0:T(256)(128)(2,1)S(1)}, u32[]{:S(2)}, u32[]{:S(2)}) collective-permute-start(bf16[32]{0:T(256)(128)(2,1)S(1)} %get-tuple-element.139), channel_id=1, source_target_pairs={{0,2},{1,3},{2,0},{3,1},{4,6},{5,7},{6,4},{7,5},{8,10},{9,11},{10,... | collective-permute-start | bytes 200 | tf_op jit(solution)/shard_map/ppermute | solution.py:209
  151.1 8.3 %collective-permute-start.12 = (bf16[32]{0:T(256)(128)(2,1)S(1)}, bf16[32]{0:T(256)(128)(2,1)S(1)}, u32[]{:S(2)}, u32[]{:S(2)}) collective-permute-start(bf16[32]{0:T(256)(128)(2,1)S(1)} %get-tuple-element.138), channel_id=1, source_target_pairs={{0,16},{1,17},{2,18},{3,19},{4,20},{5,21},{6,22},{7,23},{8,24},{9,... | collective-permute-start | bytes 200 | tf_op jit(solution)/shard_map/ppermute | solution.py:209
  152.6 6.8 %collective-permute-start.13 = (bf16[32]{0:T(256)(128)(2,1)S(1)}, bf16[32]{0:T(256)(128)(2,1)S(1)}, u32[]{:S(2)}, u32[]{:S(2)}) collective-permute-start(bf16[32]{0:T(256)(128)(2,1)S(1)} %get-tuple-element.137), channel_id=1, source_target_pairs={{0,1},{1,0},{2,3},{3,2},{4,5},{5,4},{6,7},{7,6},{8,9},{9,8},{10,11... | collective-permute-start | bytes 200 | tf_op jit(solution)/shard_map/ppermute | solution.py:209
  154.0 4.5 %collective-permute-start.10 = (bf16[16]{0:T(256)(128)(2,1)S(1)}, bf16[16]{0:T(256)(128)(2,1)S(1)}, u32[]{:S(2)}, u32[]{:S(2)}) collective-permute-start(bf16[16]{0:T(256)(128)(2,1)S(1)} %dynamic_slice.62), channel_id=1, source_target_pairs={{0,4},{1,5},{2,6},{3,7},{4,0},{5,1},{6,2},{7,3},{8,12},{9,13},{10,... | collective-permute-start | bytes 104 | tf_op jit(solution)/shard_map/ppermute | solution.py:209
  155.0 4.4 %collective-permute-start.14 = (bf16[64]{0:T(256)(128)(2,1)S(1)}, bf16[64]{0:T(256)(128)(2,1)S(1)}, u32[]{:S(2)}, u32[]{:S(2)}) collective-permute-start(bf16[64]{0:T(256)(128)(2,1)S(1)} %dynamic_slice.66), channel_id=1, source_target_pairs={{0,8},{1,9},{2,10},{3,11},{4,12},{5,13},{6,14},{7,15},{8,0},{9,1},... | collective-permute-start | bytes 392 | tf_op jit(solution)/shard_map/ppermute | solution.py:209
  158.5 13.6 %collective-permute-start.5 = (bf16[16,2896]{1,0:T(8,128)(2,1)}, bf16[16,2896]{1,0:T(8,128)(2,1)}, u32[]{:S(2)}, u32[]{:S(2)}) collective-permute-start(bf16[16,2896]{1,0:T(8,128)(2,1)} %constant_dynamic-slice_fusion.4), channel_id=1, source_target_pairs={{0,4},{1,5},{2,6},{3,7},{4,0},{5,1},{6,2},{7,3},{8,12},{9,13},{10,... | collective-permute-start | bytes 278024 | tf_op jit(solution)/shard_map/ppermute | solution.py:207
  160.9 16.3 %copy-start.12 = (f32[128]{0:T(128)}, f32[128]{0:T(128)S(1)}, u32[]{:S(2)}) copy-start(f32[128]{0:T(128)S(1)} %convert_select_fusion) | copy-start | bytes 1540
  161.8 9.7 %all-to-all-start.1 = ((f32[32,1,8]{2,1,0:T(1,128)}), f32[32,1,8]{2,1,0:T(1,128)S(1)}, u32[]{:S(2)}, u32[]{:S(2)}) async-start(f32[32,1,8]{2,1,0:T(1,128)} %bitcast.26), calls=%async_computation.1 | async-start | bytes 32768 | tf_op jit(solution)/shard_map/all_to_all | solution.py:228
  165.5 7.5 %collective-permute-start.6 = (bf16[32,2896]{1,0:T(8,128)(2,1)}, bf16[32,2896]{1,0:T(8,128)(2,1)}, u32[]{:S(2)}, u32[]{:S(2)}) collective-permute-start(bf16[32,2896]{1,0:T(8,128)(2,1)} %get-tuple-element.125), channel_id=1, source_target_pairs={{0,2},{1,3},{2,0},{3,1},{4,6},{5,7},{6,4},{7,5},{8,10},{9,11},{10,... | collective-permute-start | bytes 556040 | tf_op jit(solution)/shard_map/ppermute | solution.py:207
  167.2 6.7 %collective-permute-start.7 = (bf16[32,2896]{1,0:T(8,128)(2,1)S(1)}, bf16[32,2896]{1,0:T(8,128)(2,1)}, u32[]{:S(2)}, u32[]{:S(2)}) collective-permute-start(bf16[32,2896]{1,0:T(8,128)(2,1)S(1)} %get-tuple-element.124), channel_id=1, source_target_pairs={{0,16},{1,17},{2,18},{3,19},{4,20},{5,21},{6,22},{7,23},{8,24},{9,... | collective-permute-start | bytes 556040 | tf_op jit(solution)/shard_map/ppermute | solution.py:207
  168.7 6.3 %collective-permute-start.8 = (bf16[32,2896]{1,0:T(8,128)(2,1)S(1)}, bf16[32,2896]{1,0:T(8,128)(2,1)}, u32[]{:S(2)}, u32[]{:S(2)}) collective-permute-start(bf16[32,2896]{1,0:T(8,128)(2,1)S(1)} %get-tuple-element.123), channel_id=1, source_target_pairs={{0,1},{1,0},{2,3},{3,2},{4,5},{5,4},{6,7},{7,6},{8,9},{9,8},{10,11... | collective-permute-start | bytes 556040 | tf_op jit(solution)/shard_map/ppermute | solution.py:207
  170.2 5.8 %collective-permute-start.9 = (bf16[64,2896]{1,0:T(8,128)(2,1)S(1)}, bf16[64,2896]{1,0:T(8,128)(2,1)S(1)}, u32[]{:S(2)}, u32[]{:S(2)}) collective-permute-start(bf16[64,2896]{1,0:T(8,128)(2,1)S(1)} %constant_dynamic-slice_fusion), channel_id=1, source_target_pairs={{0,8},{1,9},{2,10},{3,11},{4,12},{5,13},{6,14},{7,15},{8,0},{9,1},... | collective-permute-start | bytes 1112072 | tf_op jit(solution)/shard_map/ppermute | solution.py:207
  177.2 2.5 %copy-start.1 = (pred[128,8,361]{0,1,2:T(8,128)(4,1)S(1)}, pred[128,8,361]{0,1,2:T(8,128)(4,1)}, u32[]{:S(2)}) copy-start(pred[128,8,361]{0,1,2:T(8,128)(4,1)} %broadcast_compare_fusion) | copy-start | bytes 1108996
  177.2 2.5 %copy-start.6 = (f32[8]{0:T(128)S(1)}, f32[8]{0:T(128)}, u32[]{:S(2)}) copy-start(f32[8]{0:T(128)} %param.25) | copy-start | bytes 100
  179.7 1.2 copy-start.7

commit v2 on v1

--- a/solution.py
+++ b/solution.py
@@ -179,41 +179,40 @@
     pool = jnp.concatenate([states] + incoming, axis=0)
     work_idx = lists[0, :work_rows]
     flat = FACT * MOVES
-
-    def step(t, carry):
-        logits_acc, values_acc = carry
+    width = -(-(flat + 1) // 128) * 128
+
+    def step(t, acc):
         idx = lax.dynamic_slice(work_idx, (t * CHUNK,), (CHUNK,))
         rows = jnp.take(pool, idx, axis=0, mode="clip", indices_are_sorted=True)
         logits, values = evaluate(rows, *weights)
-        logits_acc = lax.dynamic_update_slice(
-            logits_acc, logits.reshape(CHUNK, flat), (t * CHUNK, 0)
+        packed = jnp.concatenate(
+            [
+                logits.reshape(CHUNK, flat),
+                values[:, None],
+                jnp.zeros((CHUNK, width - flat - 1), jnp.bfloat16),
+            ],
+            axis=1,
         )
-        values_acc = lax.dynamic_update_slice(values_acc, values, (t * CHUNK,))
-        return logits_acc, values_acc
-
-    work_logits, work_values = lax.fori_loop(
+        return lax.dynamic_update_slice(acc, packed, (t * CHUNK, 0))
+
+    results = lax.fori_loop(
         0,
         (work_count + CHUNK - 1) // CHUNK,
         step,
-        (
-            jnp.zeros((work_rows + margin, flat), jnp.bfloat16),
-            jnp.zeros((work_rows + margin,), jnp.bfloat16),
-        ),
-    )
-
-    back_logits, back_values = [], []
-    for e, cap in enumerate(caps):
-        window = lax.dynamic_slice(work_logits, (places[e], 0), (cap, flat))
-        back_logits.append(lax.ppermute(window, AXES, pairs[e]))
-        window = lax.dynamic_slice(work_values, (places[e],), (cap,))
-        back_values.append(lax.ppermute(window, AXES, pairs[e]))
-
-    all_logits = jnp.concatenate([work_logits] + back_logits, axis=0)
-    all_values = jnp.concatenate([work_values] + back_values, axis=0)
+        jnp.zeros((work_rows + margin, width), jnp.bfloat16),
+    )
+
+    back = [
+        lax.ppermute(lax.dynamic_slice(results, (places[e], 0), (cap, width)), AXES, pairs[e])
+        for e, cap in enumerate(caps)
+    ]
+
+    gathered = jnp.take(
+        jnp.concatenate([results] + back, axis=0), lists[1, :slot_count], axis=0, mode="clip"
+    )
+    slot_logits = gathered[:, :flat].reshape(slot_count, FACT, MOVES)
+    slot_values = gathered[:, flat]
     slot = jnp.arange(slot_count, dtype=jnp.int32)
-    pick = lists[1, :slot_count]
-    slot_logits = jnp.take(all_logits, pick, axis=0, mode="clip").reshape(slot_count, FACT, MOVES)
-    slot_values = jnp.take(all_values, pick, axis=0, mode="clip")
 
     alive = slot < own_count
     priors = jnp.where(

time: 184 us -> 177 us (0.962)
  local copies, waits for them, and re-layouts: 50 us -> 41.5 us
  starting transfers between devices: 29.6 us -> 25.4 us
  waiting for transfers between devices: 15.3 us -> 18.8 us
    ppermute x10 -> x5, starting transfers between devices: 12.6 us -> 7.24 us  [body(): lax.ppermute(lax.dynamic_slice(results, (places[e], 0), (cap, width)), AX...]
    all_to_all x1, waiting for transfers between devices: 1.3 us -> 4.82 us  [body(): lax.all_to_all(partial_sums.reshape(groups, TREE_DEV), AXES, 0, 0, tiled=...]
    gather x3 -> x1, local copies, waits for them, and re-layouts: 3.72 us -> 1.18 us  [body(): jnp.take(jnp.concatenate([results] + back, axis=0), lists[1, :slot_count]...]
    unnamed x33 -> x34, local copies, waits for them, and re-layouts: 17.7 us -> 15.2 us
    dynamic_slice x6 -> x3, local copies, waits for them, and re-layouts: 2.8 us -> 0.27 us  [body(): lax.dynamic_slice(results, (places[e], 0), (cap, width))]
    ppermute x10 -> x5, waiting for transfers between devices: 3.71 us -> 3.85 us  [body(): lax.ppermute(lax.dynamic_slice(results, (places[e], 0), (cap, width)), AX...]
  transfers between devices with their start and end apart: 17 -> 12, of which waited for: 4 -> 5; matrix products, arithmetic and copies ran while one was open for 14% -> 12% of each run, Pallas kernels for 0% -> 0%
where the time goes in v2:
time: 177 us; the launch traced here: 176 us
  matrix products  55.5 us (31%)
  local copies, waits for them, and re-layouts  41.5 us (23%)
  starting transfers between devices  25.4 us (14%)
  between operations  21.3 us (12%)
  waiting for transfers between devices  18.8 us (11%)
  other arithmetic  8.98 us (5%)
  Pallas kernels  4.62 us (3%)
    conv_general_dilated x3, matrix products, convolve(): lax.conv_general_dilated(inputs, kernel, (1, 1), 'SAME', dimension_number...  46.4 us
    unnamed x34, local copies, waits for them, and re-layouts  15.2 us
    ppermute x5, waiting for transfers between devices, body(): lax.ppermute(lax.dynamic_slice(padded, (starts[e], 0), (cap, row)), AXES,...  10.2 us
    all_to_all x1, starting transfers between devices, body(): lax.all_to_all(jnp.broadcast_to(counts, (groups, 1)), AXES, 0, 0, tiled=T...  7.33 us
    ppermute x5, starting transfers between devices, body(): lax.ppermute(lax.dynamic_slice(results, (places[e], 0), (cap, width)), AX...  7.24 us
    dot_general x1, matrix products, evaluate(): jnp.einsum('bhwc,cf->bfhw', hidden, policy_weight, preferred_element_type...  7.22 us
    ppermute x5, starting transfers between devices, body(): lax.ppermute(lax.dynamic_slice(padded, (starts[e], 0), (cap, row)), AXES,...  7.16 us
    gather x1, local copies, waits for them, and re-layouts, step(): rows = jnp.take(pool, idx, axis=0, mode='clip', indices_are_sorted=True)  6.81 us
  transfers between devices with their start and end apart: 12, of which 5 were waited for; matrix products, arithmetic and copies ran while one was open for 12% of the time, Pallas kernels for 0%

profile of v2, /device:TPU:0, one launch (start us, length us, event | category | flops | bytes accessed | tf_op | source)
XLA Modules:
  0.0 176.4 jit_solution(7352196370295394630)
XLA Ops:
  1.3 0.6 broadcast_in_dim.58
  1.9 7.3 %all-to-all-start = ((s32[32,1,1]{2,1,0:T(1,128)}), s32[32,1,1]{2,1,0:T(1,128)S(1)}, u32[]{:S(2)}, u32[]{:S(2)}) async-start(s32[32,1,1]{2,1,0:T(1,128)} %broadcast_in_dim.58), calls=%async_computation | async-start | bytes 32768 | tf_op jit(solution)/shard_map/all_to_all | solution.py:154
  9.2 0.6 multiply_add_fusion
  9.8 3.4 %copy.51 = bf16[128,11552]{1,0:T(8,128)(2,1)S(1)} copy(bf16[128,11552]{0,1:T(8,128)(2,1)} %param.15) | data formatting | bytes 5914624 | tf_op args[0]
  13.2 1.8 %constant_dynamic-update-slice_fusion.6 = bf16[304,11552]{1,0:T(8,128)(2,1)} fusion(bf16[128,11552]{1,0:T(8,128)(2,1)S(1)} %copy.51), kind=kLoop, calls=%fused_computation.50 | loop fusion | bytes 5939200
  15.1 1.0 broadcast_compare_fusion
  16.1 0.5 iota_compare_fusion.1
  16.6 0.6 compare_reduce_fusion
  17.3 1.3 fusion.18
  18.6 0.5 scatter.4.counts_ref
  19.1 0.5 broadcast_in_dim.59.me_ref
  19.6 4.6 %shard_map.130 = (s32[24,128]{1,0:T(8,128)}, s32[8,256]{1,0:T(8,128)}) custom-call(s32[1,128]{1,0:T(1,128)} %scatter.4.counts_ref, s32[1,128]{1,0:T(1,128)} %broadcast_in_dim.59.me_ref), custom_call_target="tpu_custom_call" | custom-call | tf_op jit(solution)/shard_map/pallas_call | solution.py:125
  24.2 1.6 fusion.20
  41.1 1.9 %pad_dynamic-slice_fusion.1 = (bf16[32,11552]{1,0:T(8,128)(2,1)}, bf16[32,11552]{1,0:T(8,128)(2,1)}, bf16[32,11552]{1,0:T(8,128)(2,1)}) fusion(s32[]{:T(128)S(6)} %select_n.69, bf16[128,11552]{1,0:T(8,128)(2,1)S(1)} %copy.51, s32[]{:T(128)S(6)} %select_n.67, s32[]{:T(128)S(6)} %select_n.68), kind=kLoop, calls=%fused_computation.26 | loop fusion | bytes 5175308 | tf_op jit(solution)/shard_map/dynamic_slice | solution.py:175
  43.0 1.8 %collective-permute-start.1 = (bf16[32,11552]{1,0:T(8,128)(2,1)}, bf16[32,11552]{1,0:T(8,128)(2,1)}, u32[]{:S(2)}, u32[]{:S(2)}) collective-permute-start(bf16[32,11552]{1,0:T(8,128)(2,1)} %get-tuple-element.114), channel_id=1, source_target_pairs={{0,2},{1,3},{2,0},{3,1},{4,6},{5,7},{6,4},{7,5},{8,10},{9,11},{10,... | collective-permute-start | bytes 2217992 | tf_op jit(solution)/shard_map/ppermute | solution.py:175
  45.4 0.9 pad_dynamic-slice_fusion.4
  46.3 2.4 %collective-permute-start = (bf16[16,11552]{1,0:T(8,128)(2,1)}, bf16[16,11552]{1,0:T(8,128)(2,1)S(1)}, u32[]{:S(2)}, u32[]{:S(2)}) collective-permute-start(bf16[16,11552]{1,0:T(8,128)(2,1)} %pad_dynamic-slice_fusion.4), channel_id=1, source_target_pairs={{0,4},{1,5},{2,6},{3,7},{4,0},{5,1},{6,2},{7,3},{8,12},{9,13},{10,... | collective-permute-start | bytes 1109000 | tf_op jit(solution)/shard_map/ppermute | solution.py:175
  48.7 1.5 collective-permute-start.2
  50.2 1.5 collective-permute-start.3
  52.3 1.6 pad_dynamic-slice_fusion
  53.9 0.7 slice.73
  57.9 0.7 slice_bitcast_fusion
  58.5 0.6 pad_clamp_fusion.1
  59.1 10.1 %collective-permute-done = bf16[16,11552]{1,0:T(8,128)(2,1)S(1)} collective-permute-done((bf16[16,11552]{1,0:T(8,128)(2,1)}, bf16[16,11552]{1,0:T(8,128)(2,1)S(1)}, u32[]{:S(2)}, u32[]{:S(2)}) %collective-permute-start) | collective-permute-done | bytes 369696 | tf_op jit(solution)/shard_map/ppermute | solution.py:175
  69.2 0.8 constant_dynamic-update-slice_fusion.5
  70.1 2.1 %constant_dynamic-update-slice_fusion.4 = bf16[304,11552]{1,0:T(8,128)(2,1)} fusion(bf16[304,11552]{1,0:T(8,128)(2,1)} %constant_dynamic-update-slice_fusion.5, bf16[32,11552]{1,0:T(8,128)(2,1)} %collective-permute-done.1), kind=kLoop, calls=%fused_computation.48 | loop fusion | bytes 1490944
  72.1 2.0 %constant_dynamic-update-slice_fusion.3 = bf16[304,11552]{1,0:T(8,128)(2,1)} fusion(bf16[304,11552]{1,0:T(8,128)(2,1)} %constant_dynamic-update-slice_fusion.4, bf16[32,11552]{1,0:T(8,128)(2,1)} %collective-permute-done.2), kind=kLoop, calls=%fused_computation.47 | loop fusion | bytes 1490944
  74.2 2.1 %constant_dynamic-update-slice_fusion.2 = bf16[304,11552]{1,0:T(8,128)(2,1)} fusion(bf16[304,11552]{1,0:T(8,128)(2,1)} %constant_dynamic-update-slice_fusion.3, bf16[32,11552]{1,0:T(8,128)(2,1)} %collective-permute-done.3), kind=kLoop, calls=%fused_computation.46 | loop fusion | bytes 1490944
  76.3 1.2 constant_dynamic-update-slice_fusion.1
  77.5 1.1 broadcast_in_dim.57
  78.7 66.4 %while.11 = (s32[]{:T(128)}, bf16[224,2944]{1,0:T(8,128)(2,1)}, s32[]{:T(128)}, s32[160]{0:T(256)S(1)}, bf16[304,11552]{1,0:T(8,128)(2,1)}, /*index=5*/bf16[3,3,...) while((s32[]{:T(128)}, bf16[224,2944]{1,0:T(8,128)(2,1)}, ...), condition=%wide.region_3.4_spmd, body=%wide.region_1.3_spmd.sunk | while | flops 33799694336 | bytes 71023168 | solution.py:198
  78.9 6.8 %gather_fusion = bf16[40,11552]{1,0:T(8,128)(2,1)} fusion(bf16[304,11552]{1,0:T(8,128)(2,1)} %get-tuple-element.240, s32[1024]{0:T(1024)S(1)} %pad_clamp_fusion.3), kind=kCustom, calls=%fused_computation.clone.1 | custom fusion | bytes 1848480 | tf_op jit(solution)/shard_map/while/body/jit(_take)/gather | solution.py:186
  85.8 3.3 %copy.71 = bf16[40,11552]{0,1:T(8,128)(2,1)S(1)} copy(bf16[40,11552]{1,0:T(8,128)(2,1)} %gather_fusion) | data formatting | bytes 1848320 | tf_op jit(solution)/shard_map/while/body/reshape | solution.py:37
  89.1 8.2 %maximum_convert_fusion.5 = bf16[40,19,19,256]{3,0,2,1:T(8,128)(2,1)S(1)} fusion(bf16[40,19,19,32]{0,3,2,1:T(8,128)(2,1)S(1)} %bitcast.97, bf16[3,3,32,256]{3,2,1,0:T(8,128)(2,1)S(1)} %get-tuple-element.241), kind=kOutput, calls=%fused_computation.5.clone.1 | convolution fusion | flops 1989857280 | bytes 8464896 | tf_op jit(solution)/shard_map/while/body/conv_general_dilated | solution.py:25
  97.3 18.4 %maximum_convert_fusion.6 = bf16[40,19,19,256]{3,0,2,1:T(8,128)(2,1)S(1)} fusion(bf16[40,19,19,256]{3,0,2,1:T(8,128)(2,1)S(1)} %maximum_convert_fusion.5, bf16[1,3,3,256,256]{4,3,2,1,0:T(8,128)(2,1)S(1)} %copy-done.9), kind=kOutput, calls=%fused_computation.4.clone.1 | convolution fusion | flops 15867105280 | bytes 15966208 | tf_op jit(solution)/shard_map/while/body/conv_general_dilated | solution.py:25
  115.6 19.9 %convert_reduce_fusion.3 = (f32[40,256]{1,0:T(8,128)S(1)}, bf16[40,19,19,256]{3,0,2,1:T(8,128)(2,1)}) fusion(bf16[40,19,19,256]{3,0,2,1:T(8,128)(2,1)S(1)} %maximum_convert_fusion.6, bf16[1,3,3,256,256]{4,3,2,1,0:T(8,128)(2,1)S(1)} %copy-done.10, bf16[40,19,19,256]{3,0,2,1:T(8,128)(2,1)S(1)} %maximum_convert_fusion.5), kind=kOutput, calls=%fused_computation.2.clone.1 | convolution fusion | flops 15881881600 | bytes 23400448 | tf_op jit(solution)/shard_map/while/body/conv_general_dilated | solution.py:25
  135.5 0.1 fusion.52
  135.6 0.2 copy.72
  135.8 7.2 %convolution_convert_fusion.3 = bf16[40,19,19,8]{0,3,2,1:T(8,128)(2,1)S(1)} fusion(bf16[40,19,19,256]{3,0,2,1:T(8,128)(2,1)} %get-tuple-element.201, bf16[256,8]{0,1:T(8,128)(2,1)S(1)} %get-tuple-element.244), kind=kOutput, calls=%fused_computation.6.clone.1 | convolution fusion | flops 59261760 | bytes 7628416 | tf_op jit(solution)/shard_map/while/body/bhwc,cf->bfhw/dot_general | solution.py:43
  143.0 0.6 copy.73
  143.7 0.2 convert_element_type.69
  144.0 0.1 fusion.53
  144.3 0.7 constant_dynamic-update-slice_fusion.14
  145.0 1.5 constant_dynamic-update-slice_fusion.12
  146.6 0.2 copy-done
  146.8 3.3 %collective-permute-start.5 = (bf16[16,2944]{1,0:T(8,128)(2,1)S(1)}, bf16[16,2944]{1,0:T(8,128)(2,1)S(1)}, u32[]{:S(2)}, u32[]{:S(2)}) collective-permute-start(bf16[16,2944]{1,0:T(8,128)(2,1)S(1)} %constant_dynamic-slice_fusion.4), channel_id=1, source_target_pairs={{0,4},{1,5},{2,6},{3,7},{4,0},{5,1},{6,2},{7,3},{8,12},{9,13},{10,... | collective-permute-start | bytes 282632 | tf_op jit(solution)/shard_map/ppermute | solution.py:206
  150.0 0.1 constant_dynamic-slice_fusion.1
  150.2 0.9 collective-permute-start.6
  151.1 1.5 collective-permute-start.7
  152.6 1.5 collective-permute-start.8
  154.3 2.3 %collective-permute-done.6 = bf16[32,2944]{1,0:T(8,128)(2,1)S(1)} collective-permute-done((bf16[32,2944]{1,0:T(8,128)(2,1)S(1)}, bf16[32,2944]{1,0:T(8,128)(2,1)S(1)}, u32[]{:S(2)}, u32[]{:S(2)}) %collective-permute-start.6) | collective-permute-done | bytes 188448 | tf_op jit(solution)/shard_map/ppermute | solution.py:206
  156.7 1.5 collective-permute-done.8
  158.3 1.2 gather_fusion.1
  159.5 1.2 copy.57
  160.6 1.3 reshape.142
  162.0 0.6 select_reduce_fusion
  162.5 0.6 fusion.13
  163.2 0.2 fusion.15
  163.4 1.7 convolution_bitcast_fusion.1
  165.0 3.7 %all-to-all-start.1 = ((f32[32,1,8]{2,1,0:T(1,128)}), f32[32,1,8]{2,1,0:T(1,128)S(1)}, u32[]{:S(2)}, u32[]{:S(2)}) async-start(f32[32,1,8]{2,1,0:T(1,128)} %convolution_bitcast_fusion.1), calls=%async_computation.1 | async-start | bytes 32768 | tf_op jit(solution)/shard_map/all_to_all | solution.py:227
  168.7 1.8 %divide_select_fusion = f32[128,8,362]{0,1,2:T(8,128)} fusion(f32[128,8,362]{0,2,1:T(8,128)S(1)} %reshape.142, pred[128,8,361]{0,1,2:T(8,128)(4,1)S(1)} %copy-done.1, f32[128,8]{0,1:T(8,128)S(1)} %fusion.13, f32[128,8]{0,1:T(8,128)S(1)} %select_reduce_fusion, f32[8]{0:T(128)S(1)} %copy-done.7, pred[128]{0:T(512)(128)(4,1)S(1)} %copy-done.8), kind=kLoop, calls=%fused_computation.31 | loop fusion | flops 1853440 | bytes 3343520 | tf_op jit(solution)/shard_map/jit(_where)/select_n | solution.py:218
  170.5 0.5 broadcast_select_fusion.1
  171.0 4.8 %all-to-all-done.1 = f32[32,1,8]{2,1,0:T(1,128)S(1)} async-done(((f32[32,1,8]{2,1,0:T(1,128)}), f32[32,1,8]{2,1,0:T(1,128)S(1)}, u32[]{:S(2)}, u32[]{:S(2)}) %all-to-all-start.1) | async-done | bytes 1056 | tf_op jit(solution)/shard_map/all_to_all | solution.py:227
  175.9 0.6 reduce_sum.28
  (49 shorter events, 1.0 us)
Async XLA Ops:
  1.9 15.4 %all-to-all-start = ((s32[32,1,1]{2,1,0:T(1,128)}), s32[32,1,1]{2,1,0:T(1,128)S(1)}, u32[]{:S(2)}, u32[]{:S(2)}) async-start(s32[32,1,1]{2,1,0:T(1,128)} %broadcast_in_dim.58), calls=%async_computation | async-start | bytes 32768 | tf_op jit(solution)/shard_map/all_to_all | solution.py:154
  13.2 1.9 %copy-start.3 = (s32[128,8,361]{0,1,2:T(8,128)S(1)}, s32[128,8,361]{0,1,2:T(8,128)}, u32[]{:S(2)}) copy-start(s32[128,8,361]{0,1,2:T(8,128)} %param.18) | copy-start | bytes 4435972
  43.0 27.1 %collective-permute-start.1 = (bf16[32,11552]{1,0:T(8,128)(2,1)}, bf16[32,11552]{1,0:T(8,128)(2,1)}, u32[]{:S(2)}, u32[]{:S(2)}) collective-permute-start(bf16[32,11552]{1,0:T(8,128)(2,1)} %get-tuple-element.114), channel_id=1, source_target_pairs={{0,2},{1,3},{2,0},{3,1},{4,6},{5,7},{6,4},{7,5},{8,10},{9,11},{10,... | collective-permute-start | bytes 2217992 | tf_op jit(solution)/shard_map/ppermute | solution.py:175
  46.3 22.9 %collective-permute-start = (bf16[16,11552]{1,0:T(8,128)(2,1)}, bf16[16,11552]{1,0:T(8,128)(2,1)S(1)}, u32[]{:S(2)}, u32[]{:S(2)}) collective-permute-start(bf16[16,11552]{1,0:T(8,128)(2,1)} %pad_dynamic-slice_fusion.4), channel_id=1, source_target_pairs={{0,4},{1,5},{2,6},{3,7},{4,0},{5,1},{6,2},{7,3},{8,12},{9,13},{10,... | collective-permute-start | bytes 1109000 | tf_op jit(solution)/shard_map/ppermute | solution.py:175
  48.7 23.4 %collective-permute-start.2 = (bf16[32,11552]{1,0:T(8,128)(2,1)}, bf16[32,11552]{1,0:T(8,128)(2,1)}, u32[]{:S(2)}, u32[]{:S(2)}) collective-permute-start(bf16[32,11552]{1,0:T(8,128)(2,1)} %get-tuple-element.115), channel_id=1, source_target_pairs={{0,16},{1,17},{2,18},{3,19},{4,20},{5,21},{6,22},{7,23},{8,24},{9,... | collective-permute-start | bytes 2217992 | tf_op jit(solution)/shard_map/ppermute | solution.py:175
  50.2 24.0 %collective-permute-start.3 = (bf16[32,11552]{1,0:T(8,128)(2,1)}, bf16[32,11552]{1,0:T(8,128)(2,1)}, u32[]{:S(2)}, u32[]{:S(2)}) collective-permute-start(bf16[32,11552]{1,0:T(8,128)(2,1)} %get-tuple-element.113), channel_id=1, source_target_pairs={{0,1},{1,0},{2,3},{3,2},{4,5},{5,4},{6,7},{7,6},{8,9},{9,8},{10,11... | collective-permute-start | bytes 2217992 | tf_op jit(solution)/shard_map/ppermute | solution.py:175
  53.9 22.3 %collective-permute-start.4 = (bf16[64,11552]{1,0:T(8,128)(2,1)}, bf16[64,11552]{1,0:T(8,128)(2,1)S(1)}, u32[]{:S(2)}, u32[]{:S(2)}) collective-permute-start(bf16[64,11552]{1,0:T(8,128)(2,1)} %pad_dynamic-slice_fusion), channel_id=1, source_target_pairs={{0,8},{1,9},{2,10},{3,11},{4,12},{5,13},{6,14},{7,15},{8,0},{9,1},... | collective-permute-start | bytes 4435976 | tf_op jit(solution)/shard_map/ppermute | solution.py:175
  76.2 2.4 %copy-start.2 = (bf16[3,3,32,256]{3,2,1,0:T(8,128)(2,1)S(1)}, bf16[3,3,32,256]{3,2,1,0:T(8,128)(2,1)}, u32[]{:S(2)}) copy-start(bf16[3,3,32,256]{3,2,1,0:T(8,128)(2,1)} %param.19) | copy-start | bytes 442372
  76.2 2.4 %copy-start.4 = (bf16[256,8]{0,1:T(8,128)(2,1)S(1)}, bf16[256,8]{0,1:T(8,128)(2,1)}, u32[]{:S(2)}) copy-start(bf16[256,8]{0,1:T(8,128)(2,1)} %param.22) | copy-start | bytes 12292
  76.3 2.4 %copy-start.5 = (bf16[256,8]{0,1:T(8,128)(2,1)S(1)}, bf16[256,8]{0,1:T(8,128)(2,1)}, u32[]{:S(2)}) copy-start(bf16[256,8]{0,1:T(8,128)(2,1)} %param.23) | copy-start | bytes 12292
  76.3 2.4 %copy-start.11 = (bf16[256]{0:T(256)(128)(2,1)S(1)}, bf16[256]{0:T(256)(128)(2,1)}, u32[]{:S(2)}) copy-start(bf16[256]{0:T(256)(128)(2,1)} %param.24) | copy-start | bytes 1540
  89.1 8.2 %copy-start.9 = (bf16[1,3,3,256,256]{4,3,2,1,0:T(8,128)(2,1)S(1)}, bf16[1,3,3,256,256]{4,3,2,1,0:T(8,128)(2,1)}, u32[]{:S(2)}) copy-start(bf16[1,3,3,256,256]{4,3,2,1,0:T(8,128)(2,1)} %get-tuple-element.242) | copy-start | bytes 3538948 | tf_op jit(solution)/shard_map/while
  97.3 18.4 %copy-start.10 = (bf16[1,3,3,256,256]{4,3,2,1,0:T(8,128)(2,1)S(1)}, bf16[1,3,3,256,256]{4,3,2,1,0:T(8,128)(2,1)}, u32[]{:S(2)}) copy-start(bf16[1,3,3,256,256]{4,3,2,1,0:T(8,128)(2,1)} %get-tuple-element.243) | copy-start | bytes 3538948 | tf_op jit(solution)/shard_map/while
  145.0 1.7 copy-start
  146.8 7.5 %collective-permute-start.5 = (bf16[16,2944]{1,0:T(8,128)(2,1)S(1)}, bf16[16,2944]{1,0:T(8,128)(2,1)S(1)}, u32[]{:S(2)}, u32[]{:S(2)}) collective-permute-start(bf16[16,2944]{1,0:T(8,128)(2,1)S(1)} %constant_dynamic-slice_fusion.4), channel_id=1, source_target_pairs={{0,4},{1,5},{2,6},{3,7},{4,0},{5,1},{6,2},{7,3},{8,12},{9,13},{10,... | collective-permute-start | bytes 282632 | tf_op jit(solution)/shard_map/ppermute | solution.py:206
  150.2 6.4 %collective-permute-start.6 = (bf16[32,2944]{1,0:T(8,128)(2,1)S(1)}, bf16[32,2944]{1,0:T(8,128)(2,1)S(1)}, u32[]{:S(2)}, u32[]{:S(2)}) collective-permute-start(bf16[32,2944]{1,0:T(8,128)(2,1)S(1)} %get-tuple-element.118), channel_id=1, source_target_pairs={{0,2},{1,3},{2,0},{3,1},{4,6},{5,7},{6,4},{7,5},{8,10},{9,11},{10,... | collective-permute-start | bytes 565256 | tf_op jit(solution)/shard_map/ppermute | solution.py:206
  151.1 5.6 %collective-permute-start.7 = (bf16[32,2944]{1,0:T(8,128)(2,1)S(1)}, bf16[32,2944]{1,0:T(8,128)(2,1)S(1)}, u32[]{:S(2)}, u32[]{:S(2)}) collective-permute-start(bf16[32,2944]{1,0:T(8,128)(2,1)S(1)} %get-tuple-element.117), channel_id=1, source_target_pairs={{0,16},{1,17},{2,18},{3,19},{4,20},{5,21},{6,22},{7,23},{8,24},{9,... | collective-permute-start | bytes 565256 | tf_op jit(solution)/shard_map/ppermute | solution.py:206
  152.6 5.6 %collective-permute-start.8 = (bf16[32,2944]{1,0:T(8,128)(2,1)S(1)}, bf16[32,2944]{1,0:T(8,128)(2,1)S(1)}, u32[]{:S(2)}, u32[]{:S(2)}) collective-permute-start(bf16[32,2944]{1,0:T(8,128)(2,1)S(1)} %get-tuple-element.116), channel_id=1, source_target_pairs={{0,1},{1,0},{2,3},{3,2},{4,5},{5,4},{6,7},{7,6},{8,9},{9,8},{10,11... | collective-permute-start | bytes 565256 | tf_op jit(solution)/shard_map/ppermute | solution.py:206
  154.2 4.0 %collective-permute-start.9 = (bf16[64,2944]{1,0:T(8,128)(2,1)S(1)}, bf16[64,2944]{1,0:T(8,128)(2,1)S(1)}, u32[]{:S(2)}, u32[]{:S(2)}) collective-permute-start(bf16[64,2944]{1,0:T(8,128)(2,1)S(1)} %constant_dynamic-slice_fusion), channel_id=1, source_target_pairs={{0,8},{1,9},{2,10},{3,11},{4,12},{5,13},{6,14},{7,15},{8,0},{9,1},... | collective-permute-start | bytes 1130504 | tf_op jit(solution)/shard_map/ppermute | solution.py:206
  159.5 2.5 %copy-start.1 = (pred[128,8,361]{0,1,2:T(8,128)(4,1)S(1)}, pred[128,8,361]{0,1,2:T(8,128)(4,1)}, u32[]{:S(2)}) copy-start(pred[128,8,361]{0,1,2:T(8,128)(4,1)} %broadcast_compare_fusion) | copy-start | bytes 1108996
  159.5 2.5 %copy-start.7 = (f32[8]{0:T(128)S(1)}, f32[8]{0:T(128)}, u32[]{:S(2)}) copy-start(f32[8]{0:T(128)} %param.25) | copy-start | bytes 100
  161.9 1.4 copy-start.6
  161.9 1.4 copy-start.12
  162.0 6.8 %copy-start.8 = (pred[128]{0:T(512)(128)(4,1)S(1)}, pred[128]{0:T(512)(128)(4,1)}, u32[]{:S(2)}) copy-start(pred[128]{0:T(512)(128)(4,1)} %iota_compare_fusion.1) | copy-start | bytes 388
  165.0 10.8 %all-to-all-start.1 = ((f32[32,1,8]{2,1,0:T(1,128)}), f32[32,1,8]{2,1,0:T(1,128)S(1)}, u32[]{:S(2)}, u32[]{:S(2)}) async-start(f32[32,1,8]{2,1,0:T(1,128)} %convolution_bitcast_fusion.1), calls=%async_computation.1 | async-start | bytes 32768 | tf_op jit(solution)/shard_map/all_to_all | solution.py:227

commit v3 on v2

--- a/solution.py
+++ b/solution.py
@@ -113,7 +113,18 @@
         pick_base = pick_base + cap
     work_idx = jnp.where(k < mine(keep + sum(into)), jnp.clip(work_idx, 0, work_base - 1), work_base - 1)
     pick = jnp.clip(pick, 0, pick_base - 1)
-    idx_ref[...] = jnp.concatenate([work_idx, pick] + [k * 0] * (idx_ref.shape[0] - 2), axis=0)
+    send_idx = k * 0
+    back_idx = k * 0
+    seg = 0
+    for e, cap in enumerate(caps):
+        inside = (k >= seg) & (k < seg + cap)
+        send_idx = jnp.where(inside, mine(starts[e]) + k - seg, send_idx)
+        back_idx = jnp.where(inside, mine(places[e]) + k - seg, back_idx)
+        seg = seg + cap
+    send_idx = jnp.clip(send_idx, 0, slot_count - 1)
+    back_idx = jnp.clip(back_idx, 0, work_rows + max(caps) - 1)
+    rows = [work_idx, pick, send_idx, back_idx]
+    idx_ref[...] = jnp.concatenate(rows + [k * 0] * (idx_ref.shape[0] - len(rows)), axis=0)
 
 
 def make_plan(counts_all, me, masks, caps, slot_count, work_rows):
@@ -121,7 +132,7 @@
     lanes = -(-groups // 128) * 128
     padded = jnp.zeros((1, lanes), jnp.int32).at[0, :groups].set(counts_all)
     rows = -(-(4 * len(masks) + 2) // 8) * 8
-    width = -(-max(work_rows, slot_count) // 128) * 128
+    width = -(-max(work_rows, slot_count, sum(caps)) // 128) * 128
     return pl.pallas_call(
         functools.partial(plan_kernel, masks, caps, slot_count, work_rows),
         out_shape=(
@@ -159,21 +170,20 @@
     caps = (FAR_CAP, LINK_CAP, LINK_CAP, LINK_CAP, CORE_CAP)
     work_rows = -(-slot_count // CHUNK) * CHUNK
     plan, lists = make_plan(counts_all, me, masks, caps, slot_count, work_rows)
-    mine = lax.dynamic_slice(plan, (0, me), (plan.shape[0], 1))[:, 0]
     edges = len(masks)
-    send = [mine[e] for e in range(edges)]
-    starts = [mine[2 * edges + e] for e in range(edges)]
-    places = [mine[3 * edges + e] for e in range(edges)]
-    work_count = mine[4 * edges + 1]
-
-    recv = [mine[edges + e] for e in range(edges)]
+    work_count = lax.dynamic_slice(plan, (4 * edges + 1, me), (1, 1))[0, 0]
+    segments = []
+    seg = 0
+    for cap in caps:
+        segments.append((seg, cap))
+        seg += cap
 
     margin = max(caps)
-    padded = jnp.concatenate([states, jnp.zeros((margin, row), states.dtype)])
     pairs = [[(d, d ^ m) for d in range(groups)] for m in masks]
+    outgoing = jnp.take(states, lists[2, :seg], axis=0, mode="clip")
     incoming = [
-        lax.ppermute(lax.dynamic_slice(padded, (starts[e], 0), (cap, row)), AXES, pairs[e])
-        for e, cap in enumerate(caps)
+        lax.ppermute(outgoing[first : first + cap], AXES, pairs[e])
+        for e, (first, cap) in enumerate(segments)
     ]
 
     pool = jnp.concatenate([states] + incoming, axis=0)
@@ -202,9 +212,10 @@
         jnp.zeros((work_rows + margin, width), jnp.bfloat16),
     )
 
+    returned = jnp.take(results, lists[3, :seg], axis=0, mode="clip")
     back = [
-        lax.ppermute(lax.dynamic_slice(results, (places[e], 0), (cap, width)), AXES, pairs[e])
-        for e, cap in enumerate(caps)
+        lax.ppermute(returned[first : first + cap], AXES, pairs[e])
+        for e, (first, cap) in enumerate(segments)
     ]
 
     gathered = jnp.take(

time: 177 us -> 182 us (1.028)
  between operations: 21.3 us -> 3.41 us
  local copies, waits for them, and re-layouts: 41.5 us -> 54.6 us
  waiting for transfers between devices: 18.8 us -> 25.7 us
  other arithmetic: 8.98 us -> 12.3 us
    gather x0 -> x2, local copies, waits for them, and re-layouts: none -> 9.16 us  [the longest x1 5.11 us: body(): outgoing = jnp.take(states, lists[2, :seg], axis=0, mode='clip')]
    ppermute x10, waiting for transfers between devices: 14 us -> 20.9 us  [the longest x5 18.4 us: body(): lax.ppermute(outgoing[first:first + cap], AXES, pairs[e])]
    slice x1 -> x7, local copies, waits for them, and re-layouts: 1.61 us -> 7.09 us  [the longest x3 6.24 us: body(): outgoing[first:first + cap]]
    dynamic_slice x6 -> x0, local copies, waits for them, and re-layouts: 4.67 us -> none  [the longest x3 4.4 us: body(): lax.dynamic_slice(padded, (starts[e], 0), (cap, row))]
    gather x1, local copies, waits for them, and re-layouts: 1.18 us -> 3.9 us  [body(): jnp.take(jnp.concatenate([results] + back, axis=0), lists[1, :slot_count]...]
    unnamed x34 -> x32, local copies, waits for them, and re-layouts: 15.2 us -> 14.6 us
  transfers between devices with their start and end apart: 12 -> 12, of which waited for: 5 -> 4; matrix products, arithmetic and copies ran while one was open for 12% -> 15% of each run, Pallas kernels for 0% -> 0%
where the time goes in v3:
time: 182 us; the launch traced here: 181 us
  matrix products  55.5 us (30%)
  local copies, waits for them, and re-layouts  54.6 us (30%)
  waiting for transfers between devices  25.7 us (14%)
  starting transfers between devices  24.7 us (14%)
  other arithmetic  12.3 us (7%)
  Pallas kernels  4.63 us (3%)
  between operations  3.41 us (2%)
    conv_general_dilated x3, matrix products, convolve(): lax.conv_general_dilated(inputs, kernel, (1, 1), 'SAME', dimension_number...  46.4 us
    ppermute x5, waiting for transfers between devices, body(): lax.ppermute(outgoing[first:first + cap], AXES, pairs[e])  18.4 us
    unnamed x32, local copies, waits for them, and re-layouts  14.6 us
    all_to_all x1, starting transfers between devices, body(): lax.all_to_all(jnp.broadcast_to(counts, (groups, 1)), AXES, 0, 0, tiled=T...  7.33 us
    dot_general x1, matrix products, evaluate(): jnp.einsum('bhwc,cf->bfhw', hidden, policy_weight, preferred_element_type...  7.22 us
    ppermute x5, starting transfers between devices, body(): lax.ppermute(outgoing[first:first + cap], AXES, pairs[e])  7.16 us
    gather x1, local copies, waits for them, and re-layouts, step(): rows = jnp.take(pool, idx, axis=0, mode='clip', indices_are_sorted=True)  6.81 us
    ppermute x5, starting transfers between devices, body(): lax.ppermute(returned[first:first + cap], AXES, pairs[e])  6.73 us
  transfers between devices with their start and end apart: 12, of which 4 were waited for; matrix products, arithmetic and copies ran while one was open for 15% of the time, Pallas kernels for 0%

profile of v3, /device:TPU:0, one launch (start us, length us, event | category | flops | bytes accessed | tf_op | source)
XLA Modules:
  0.0 181.2 jit_solution(16210547014466536815)
XLA Ops:
  1.3 0.6 broadcast_in_dim.65
  1.9 7.3 %all-to-all-start = ((s32[32,1,1]{2,1,0:T(1,128)}), s32[32,1,1]{2,1,0:T(1,128)S(1)}, u32[]{:S(2)}, u32[]{:S(2)}) async-start(s32[32,1,1]{2,1,0:T(1,128)} %broadcast_in_dim.65), calls=%async_computation | async-start | bytes 32768 | tf_op jit(solution)/shard_map/all_to_all | solution.py:165
  9.2 0.6 multiply_add_fusion
  9.8 3.4 %copy.51 = bf16[128,11552]{1,0:T(8,128)(2,1)S(1)} copy(bf16[128,11552]{0,1:T(8,128)(2,1)} %param.15) | data formatting | bytes 5914624 | tf_op args[0]
  13.2 1.8 %constant_dynamic-update-slice_fusion.6 = bf16[304,11552]{1,0:T(8,128)(2,1)} fusion(bf16[128,11552]{1,0:T(8,128)(2,1)S(1)} %copy.51), kind=kLoop, calls=%fused_computation.47 | loop fusion | bytes 5939200
  15.1 2.3 %broadcast_compare_fusion = pred[128,8,361]{0,1,2:T(8,128)(4,1)} fusion(s32[128,8,361]{0,1,2:T(8,128)} %param.18), kind=kLoop, calls=%fused_computation.33 | loop fusion | flops 369664 | bytes 1848320 | tf_op jit(solution)/shard_map/gt | solution.py:58
  17.4 0.5 iota_compare_fusion.1
  17.9 0.6 compare_reduce_fusion
  18.6 1.3 fusion.18
  19.9 0.5 scatter.4.counts_ref
  20.4 0.5 broadcast_in_dim.66.me_ref
  20.9 4.6 %shard_map.130 = (s32[24,128]{1,0:T(8,128)}, s32[8,256]{1,0:T(8,128)}) custom-call(s32[1,128]{1,0:T(1,128)} %scatter.4.counts_ref, s32[1,128]{1,0:T(1,128)} %broadcast_in_dim.66.me_ref), custom_call_target="tpu_custom_call" | custom-call | tf_op jit(solution)/shard_map/pallas_call | solution.py:136
  25.5 0.8 fusion.22
  26.3 0.6 pad_clamp_fusion.2
  26.9 5.1 %gather_fusion.1 = bf16[176,11552]{1,0:T(8,128)(2,1)} fusion(bf16[128,11552]{1,0:T(8,128)(2,1)S(1)} %copy.51, s32[1024]{0:T(1024)S(1)} %get-tuple-element.122), kind=kCustom, calls=%fused_computation.1 | custom fusion | bytes 8133312 | tf_op jit(solution)/shard_map/jit(_take)/gather | solution.py:183
  32.0 1.8 slice.88
  33.8 2.7 %collective-permute-start = (bf16[16,11552]{1,0:T(8,128)(2,1)}, bf16[16,11552]{1,0:T(8,128)(2,1)S(1)}, u32[]{:S(2)}, u32[]{:S(2)}) collective-permute-start(bf16[16,11552]{1,0:T(8,128)(2,1)} %slice.88), channel_id=1, source_target_pairs={{0,4},{1,5},{2,6},{3,7},{4,0},{5,1},{6,2},{7,3},{8,12},{9,13},{10,... | collective-permute-start | bytes 1109000 | tf_op jit(solution)/shard_map/ppermute | solution.py:185
  36.5 3.0 %fusion.20 = (bf16[32,11552]{1,0:T(8,128)(2,1)}, bf16[32,11552]{1,0:T(8,128)(2,1)}, bf16[32,11552]{1,0:T(8,128)(2,1)}) fusion(bf16[176,11552]{1,0:T(8,128)(2,1)} %gather_fusion.1), kind=kLoop, calls=%fused_computation.65 | loop fusion | bytes 4435968 | tf_op jit(solution)/shard_map/slice | solution.py:185
  39.5 1.5 slice.92
  40.9 1.3 fusion.23
  44.2 0.7 slice.64
  44.9 1.5 collective-permute-start.1
  46.4 1.5 collective-permute-start.2
  47.9 1.5 collective-permute-start.3
  49.4 0.7 slice_bitcast_fusion
  50.0 0.6 pad_clamp_fusion.1
  50.6 3.2 %collective-permute-done = bf16[16,11552]{1,0:T(8,128)(2,1)S(1)} collective-permute-done((bf16[16,11552]{1,0:T(8,128)(2,1)}, bf16[16,11552]{1,0:T(8,128)(2,1)S(1)}, u32[]{:S(2)}, u32[]{:S(2)}) %collective-permute-start) | collective-permute-done | bytes 369696 | tf_op jit(solution)/shard_map/ppermute | solution.py:185
  53.8 0.8 constant_dynamic-update-slice_fusion.5
  54.6 15.2 %collective-permute-done.1 = bf16[32,11552]{1,0:T(8,128)(2,1)} collective-permute-done((bf16[32,11552]{1,0:T(8,128)(2,1)}, bf16[32,11552]{1,0:T(8,128)(2,1)}, u32[]{:S(2)}, u32[]{:S(2)}) %collective-permute-start.1) | collective-permute-done | bytes 739360 | tf_op jit(solution)/shard_map/ppermute | solution.py:185
  69.8 2.1 %constant_dynamic-update-slice_fusion.4 = bf16[304,11552]{1,0:T(8,128)(2,1)} fusion(bf16[304,11552]{1,0:T(8,128)(2,1)} %constant_dynamic-update-slice_fusion.5, bf16[32,11552]{1,0:T(8,128)(2,1)} %collective-permute-done.1), kind=kLoop, calls=%fused_computation.45 | loop fusion | bytes 1490944
  71.9 0.9 constant_dynamic-update-slice_fusion.3
  72.8 0.9 constant_dynamic-update-slice_fusion.2
  73.8 2.6 %constant_dynamic-update-slice_fusion.1 = bf16[304,11552]{1,0:T(8,128)(2,1)} fusion(bf16[304,11552]{1,0:T(8,128)(2,1)} %constant_dynamic-update-slice_fusion.2, bf16[64,11552]{1,0:T(8,128)(2,1)} %collective-permute-done.4), kind=kLoop, calls=%fused_computation.42 | loop fusion | bytes 2981888 | tf_op jit(solution)/shard_map/concatenate | solution.py:189
  76.4 1.1 broadcast_in_dim.64
  77.6 66.4 %while.11 = (s32[]{:T(128)}, bf16[224,2944]{1,0:T(8,128)(2,1)}, s32[]{:T(128)}, s32[160]{0:T(256)S(1)}, bf16[304,11552]{1,0:T(8,128)(2,1)}, /*index=5*/bf16[3,3,...) while((s32[]{:T(128)}, bf16[224,2944]{1,0:T(8,128)(2,1)}, ...), condition=%wide.region_3.4_spmd, body=%wide.region_1.3_spmd.sunk | while | flops 33799694336 | bytes 71023168 | solution.py:208
  77.9 6.8 %gather_fusion = bf16[40,11552]{1,0:T(8,128)(2,1)} fusion(bf16[304,11552]{1,0:T(8,128)(2,1)} %get-tuple-element.233, s32[1024]{0:T(1024)S(1)} %pad_clamp_fusion.5), kind=kCustom, calls=%fused_computation.clone.1 | custom fusion | bytes 1848480 | tf_op jit(solution)/shard_map/while/body/jit(_take)/gather | solution.py:196
  84.7 3.3 %copy.71 = bf16[40,11552]{0,1:T(8,128)(2,1)S(1)} copy(bf16[40,11552]{1,0:T(8,128)(2,1)} %gather_fusion) | data formatting | bytes 1848320 | tf_op jit(solution)/shard_map/while/body/reshape | solution.py:37
  88.0 8.2 %maximum_convert_fusion.5 = bf16[40,19,19,256]{3,0,2,1:T(8,128)(2,1)S(1)} fusion(bf16[40,19,19,32]{0,3,2,1:T(8,128)(2,1)S(1)} %bitcast.89, bf16[3,3,32,256]{3,2,1,0:T(8,128)(2,1)S(1)} %get-tuple-element.234), kind=kOutput, calls=%fused_computation.7.clone.1 | convolution fusion | flops 1989857280 | bytes 8464896 | tf_op jit(solution)/shard_map/while/body/conv_general_dilated | solution.py:25
  96.2 18.4 %maximum_convert_fusion.6 = bf16[40,19,19,256]{3,0,2,1:T(8,128)(2,1)S(1)} fusion(bf16[40,19,19,256]{3,0,2,1:T(8,128)(2,1)S(1)} %maximum_convert_fusion.5, bf16[1,3,3,256,256]{4,3,2,1,0:T(8,128)(2,1)S(1)} %copy-done.8), kind=kOutput, calls=%fused_computation.6.clone.1 | convolution fusion | flops 15867105280 | bytes 15966208 | tf_op jit(solution)/shard_map/while/body/conv_general_dilated | solution.py:25
  114.6 19.9 %convert_reduce_fusion.3 = (f32[40,256]{1,0:T(8,128)S(1)}, bf16[40,19,19,256]{3,0,2,1:T(8,128)(2,1)}) fusion(bf16[40,19,19,256]{3,0,2,1:T(8,128)(2,1)S(1)} %maximum_convert_fusion.6, bf16[1,3,3,256,256]{4,3,2,1,0:T(8,128)(2,1)S(1)} %copy-done.9, bf16[40,19,19,256]{3,0,2,1:T(8,128)(2,1)S(1)} %maximum_convert_fusion.5), kind=kOutput, calls=%fused_computation.4.clone.1 | convolution fusion | flops 15881881600 | bytes 23400448 | tf_op jit(solution)/shard_map/while/body/conv_general_dilated | solution.py:25
  134.7 7.2 %convolution_convert_fusion.3 = bf16[40,19,19,8]{0,3,2,1:T(8,128)(2,1)S(1)} fusion(bf16[40,19,19,256]{3,0,2,1:T(8,128)(2,1)} %get-tuple-element.194, bf16[256,8]{0,1:T(8,128)(2,1)S(1)} %get-tuple-element.237), kind=kOutput, calls=%fused_computation.8.clone.1 | convolution fusion | flops 59261760 | bytes 7628416 | tf_op jit(solution)/shard_map/while/body/bhwc,cf->bfhw/dot_general | solution.py:43
  141.9 0.6 copy.73
  143.2 0.7 constant_dynamic-update-slice_fusion.14
  143.9 4.0 %gather_fusion.2 = bf16[176,2944]{1,0:T(8,128)(2,1)S(1)} fusion(bf16[224,2944]{1,0:T(8,128)(2,1)} %get-tuple-element.77, s32[1024]{0:T(1024)} %get-tuple-element.121), kind=kCustom, calls=%fused_computation.2 | custom fusion | bytes 2073280 | tf_op jit(solution)/shard_map/jit(_take)/gather | solution.py:215
  148.1 1.3 collective-permute-start.5
  149.3 1.2 constant_dynamic-update-slice_fusion.12
  150.6 2.5 %collective-permute-start.6 = (bf16[32,2944]{1,0:T(8,128)(2,1)S(1)}, bf16[32,2944]{1,0:T(8,128)(2,1)S(1)}, u32[]{:S(2)}, u32[]{:S(2)}) collective-permute-start(bf16[32,2944]{1,0:T(8,128)(2,1)S(1)} %get-tuple-element.118), channel_id=1, source_target_pairs={{0,2},{1,3},{2,0},{3,1},{4,6},{5,7},{6,4},{7,5},{8,10},{9,11},{10,... | collective-permute-start | bytes 565256 | tf_op jit(solution)/shard_map/ppermute | solution.py:217
  153.1 1.5 collective-permute-start.7
  154.6 1.4 collective-permute-start.8
  156.0 0.6 constant_dynamic-update-slice_fusion.11
  156.7 2.5 %collective-permute-done.6 = bf16[32,2944]{1,0:T(8,128)(2,1)S(1)} collective-permute-done((bf16[32,2944]{1,0:T(8,128)(2,1)S(1)}, bf16[32,2944]{1,0:T(8,128)(2,1)S(1)}, u32[]{:S(2)}, u32[]{:S(2)}) %collective-permute-start.6) | collective-permute-done | bytes 188448 | tf_op jit(solution)/shard_map/ppermute | solution.py:217
  159.2 0.7 constant_dynamic-update-slice_fusion.10
  159.9 0.7 constant_dynamic-update-slice_fusion.9
  160.5 0.7 constant_dynamic-update-slice_fusion.8
  161.2 0.8 constant_dynamic-update-slice_fusion.7
  162.0 3.9 %gather_fusion.3 = bf16[128,2944]{1,0:T(8,128)(2,1)S(1)} fusion(bf16[400,2944]{1,0:T(8,128)(2,1)} %constant_dynamic-update-slice_fusion.7, s32[1024]{0:T(1024)} %pad_clamp_fusion.1), kind=kCustom, calls=%fused_computation.3 | custom fusion | bytes 1507840 | tf_op jit(solution)/shard_map/jit(_take)/gather | solution.py:221
  166.9 0.6 select_reduce_fusion
  167.5 0.6 fusion.13
  168.3 1.7 convolution_bitcast_fusion.1
  170.0 3.5 %all-to-all-start.1 = ((f32[32,1,8]{2,1,0:T(1,128)}), f32[32,1,8]{2,1,0:T(1,128)S(1)}, u32[]{:S(2)}, u32[]{:S(2)}) async-start(f32[32,1,8]{2,1,0:T(1,128)} %convolution_bitcast_fusion.1), calls=%async_computation.1 | async-start | bytes 32768 | tf_op jit(solution)/shard_map/all_to_all | solution.py:238
  173.5 1.8 divide_select_fusion
  175.3 0.5 broadcast_select_fusion.1
  175.8 4.8 %all-to-all-done.1 = f32[32,1,8]{2,1,0:T(1,128)S(1)} async-done(((f32[32,1,8]{2,1,0:T(1,128)}), f32[32,1,8]{2,1,0:T(1,128)S(1)}, u32[]{:S(2)}, u32[]{:S(2)}) %all-to-all-start.1) | async-done | bytes 1056 | tf_op jit(solution)/shard_map/all_to_all | solution.py:238
  180.6 0.6 reduce_sum.28
  (51 shorter events, 2.3 us)
Async XLA Ops:
  1.9 16.7 %all-to-all-start = ((s32[32,1,1]{2,1,0:T(1,128)}), s32[32,1,1]{2,1,0:T(1,128)S(1)}, u32[]{:S(2)}, u32[]{:S(2)}) async-start(s32[32,1,1]{2,1,0:T(1,128)} %broadcast_in_dim.65), calls=%async_computation | async-start | bytes 32768 | tf_op jit(solution)/shard_map/all_to_all | solution.py:165
  33.8 20.0 %collective-permute-start = (bf16[16,11552]{1,0:T(8,128)(2,1)}, bf16[16,11552]{1,0:T(8,128)(2,1)S(1)}, u32[]{:S(2)}, u32[]{:S(2)}) collective-permute-start(bf16[16,11552]{1,0:T(8,128)(2,1)} %slice.88), channel_id=1, source_target_pairs={{0,4},{1,5},{2,6},{3,7},{4,0},{5,1},{6,2},{7,3},{8,12},{9,13},{10,... | collective-permute-start | bytes 1109000 | tf_op jit(solution)/shard_map/ppermute | solution.py:185
  44.9 25.0 %collective-permute-start.1 = (bf16[32,11552]{1,0:T(8,128)(2,1)}, bf16[32,11552]{1,0:T(8,128)(2,1)}, u32[]{:S(2)}, u32[]{:S(2)}) collective-permute-start(bf16[32,11552]{1,0:T(8,128)(2,1)} %get-tuple-element.115), channel_id=1, source_target_pairs={{0,2},{1,3},{2,0},{3,1},{4,6},{5,7},{6,4},{7,5},{8,10},{9,11},{10,... | collective-permute-start | bytes 2217992 | tf_op jit(solution)/shard_map/ppermute | solution.py:185
  46.4 25.5 %collective-permute-start.2 = (bf16[32,11552]{1,0:T(8,128)(2,1)}, bf16[32,11552]{1,0:T(8,128)(2,1)S(1)}, u32[]{:S(2)}, u32[]{:S(2)}) collective-permute-start(bf16[32,11552]{1,0:T(8,128)(2,1)} %get-tuple-element.114), channel_id=1, source_target_pairs={{0,16},{1,17},{2,18},{3,19},{4,20},{5,21},{6,22},{7,23},{8,24},{9,... | collective-permute-start | bytes 2217992 | tf_op jit(solution)/shard_map/ppermute | solution.py:185
  47.9 24.9 %collective-permute-start.3 = (bf16[32,11552]{1,0:T(8,128)(2,1)}, bf16[32,11552]{1,0:T(8,128)(2,1)S(1)}, u32[]{:S(2)}, u32[]{:S(2)}) collective-permute-start(bf16[32,11552]{1,0:T(8,128)(2,1)} %get-tuple-element.113), channel_id=1, source_target_pairs={{0,1},{1,0},{2,3},{3,2},{4,5},{5,4},{6,7},{7,6},{8,9},{9,8},{10,11... | collective-permute-start | bytes 2217992 | tf_op jit(solution)/shard_map/ppermute | solution.py:185
  49.4 24.4 %collective-permute-start.4 = (bf16[64,11552]{1,0:T(8,128)(2,1)S(1)}, bf16[64,11552]{1,0:T(8,128)(2,1)}, u32[]{:S(2)}, u32[]{:S(2)}) collective-permute-start(bf16[64,11552]{1,0:T(8,128)(2,1)S(1)} %slice.92), channel_id=1, source_target_pairs={{0,8},{1,9},{2,10},{3,11},{4,12},{5,13},{6,14},{7,15},{8,0},{9,1},... | collective-permute-start | bytes 4435976 | tf_op jit(solution)/shard_map/ppermute | solution.py:185
  73.7 3.8 %copy-start.2 = (bf16[3,3,32,256]{3,2,1,0:T(8,128)(2,1)S(1)}, bf16[3,3,32,256]{3,2,1,0:T(8,128)(2,1)}, u32[]{:S(2)}) copy-start(bf16[3,3,32,256]{3,2,1,0:T(8,128)(2,1)} %param.19) | copy-start | bytes 442372
  73.8 3.8 %copy-start.3 = (bf16[256,8]{0,1:T(8,128)(2,1)S(1)}, bf16[256,8]{0,1:T(8,128)(2,1)}, u32[]{:S(2)}) copy-start(bf16[256,8]{0,1:T(8,128)(2,1)} %param.22) | copy-start | bytes 12292
  73.8 3.8 %copy-start.4 = (bf16[256,8]{0,1:T(8,128)(2,1)S(1)}, bf16[256,8]{0,1:T(8,128)(2,1)}, u32[]{:S(2)}) copy-start(bf16[256,8]{0,1:T(8,128)(2,1)} %param.23) | copy-start | bytes 12292
  73.8 3.8 %copy-start.10 = (bf16[256]{0:T(256)(128)(2,1)S(1)}, bf16[256]{0:T(256)(128)(2,1)}, u32[]{:S(2)}) copy-start(bf16[256]{0:T(256)(128)(2,1)} %param.24) | copy-start | bytes 1540
  88.0 8.2 %copy-start.8 = (bf16[1,3,3,256,256]{4,3,2,1,0:T(8,128)(2,1)S(1)}, bf16[1,3,3,256,256]{4,3,2,1,0:T(8,128)(2,1)}, u32[]{:S(2)}) copy-start(bf16[1,3,3,256,256]{4,3,2,1,0:T(8,128)(2,1)} %get-tuple-element.235) | copy-start | bytes 3538948 | tf_op jit(solution)/shard_map/while
  96.2 18.4 %copy-start.9 = (bf16[1,3,3,256,256]{4,3,2,1,0:T(8,128)(2,1)S(1)}, bf16[1,3,3,256,256]{4,3,2,1,0:T(8,128)(2,1)}, u32[]{:S(2)}) copy-start(bf16[1,3,3,256,256]{4,3,2,1,0:T(8,128)(2,1)} %get-tuple-element.236) | copy-start | bytes 3538948 | tf_op jit(solution)/shard_map/while
  143.9 5.4 %copy-start = (bf16[224,2944]{1,0:T(8,128)(2,1)S(1)}, bf16[224,2944]{1,0:T(8,128)(2,1)}, u32[]{:S(2)}) copy-start(bf16[224,2944]{1,0:T(8,128)(2,1)} %get-tuple-element.77) | copy-start | bytes 3956740
  148.1 8.0 %collective-permute-start.5 = (bf16[16,2944]{1,0:T(8,128)(2,1)S(1)}, bf16[16,2944]{1,0:T(8,128)(2,1)S(1)}, u32[]{:S(2)}, u32[]{:S(2)}) collective-permute-start(bf16[16,2944]{1,0:T(8,128)(2,1)S(1)} %slice.93), channel_id=1, source_target_pairs={{0,4},{1,5},{2,6},{3,7},{4,0},{5,1},{6,2},{7,3},{8,12},{9,13},{10,... | collective-permute-start | bytes 282632 | tf_op jit(solution)/shard_map/ppermute | solution.py:217
  150.6 8.6 %collective-permute-start.6 = (bf16[32,2944]{1,0:T(8,128)(2,1)S(1)}, bf16[32,2944]{1,0:T(8,128)(2,1)S(1)}, u32[]{:S(2)}, u32[]{:S(2)}) collective-permute-start(bf16[32,2944]{1,0:T(8,128)(2,1)S(1)} %get-tuple-element.118), channel_id=1, source_target_pairs={{0,2},{1,3},{2,0},{3,1},{4,6},{5,7},{6,4},{7,5},{8,10},{9,11},{10,... | collective-permute-start | bytes 565256 | tf_op jit(solution)/shard_map/ppermute | solution.py:217
  153.1 6.8 %collective-permute-start.7 = (bf16[32,2944]{1,0:T(8,128)(2,1)S(1)}, bf16[32,2944]{1,0:T(8,128)(2,1)S(1)}, u32[]{:S(2)}, u32[]{:S(2)}) collective-permute-start(bf16[32,2944]{1,0:T(8,128)(2,1)S(1)} %get-tuple-element.117), channel_id=1, source_target_pairs={{0,16},{1,17},{2,18},{3,19},{4,20},{5,21},{6,22},{7,23},{8,24},{9,... | collective-permute-start | bytes 565256 | tf_op jit(solution)/shard_map/ppermute | solution.py:217
  154.6 6.0 %collective-permute-start.8 = (bf16[32,2944]{1,0:T(8,128)(2,1)S(1)}, bf16[32,2944]{1,0:T(8,128)(2,1)S(1)}, u32[]{:S(2)}, u32[]{:S(2)}) collective-permute-start(bf16[32,2944]{1,0:T(8,128)(2,1)S(1)} %get-tuple-element.116), channel_id=1, source_target_pairs={{0,1},{1,0},{2,3},{3,2},{4,5},{5,4},{6,7},{7,6},{8,9},{9,8},{10,11... | collective-permute-start | bytes 565256 | tf_op jit(solution)/shard_map/ppermute | solution.py:217
  156.0 5.2 %collective-permute-start.9 = (bf16[64,2944]{1,0:T(8,128)(2,1)S(1)}, bf16[64,2944]{1,0:T(8,128)(2,1)S(1)}, u32[]{:S(2)}, u32[]{:S(2)}) collective-permute-start(bf16[64,2944]{1,0:T(8,128)(2,1)S(1)} %slice.97), channel_id=1, source_target_pairs={{0,8},{1,9},{2,10},{3,11},{4,12},{5,13},{6,14},{7,15},{8,0},{9,1},... | collective-permute-start | bytes 1130504 | tf_op jit(solution)/shard_map/ppermute | solution.py:217
  165.9 1.0 copy-start.1
  165.9 1.0 copy-start.6
  166.9 1.4 copy-start.5
  166.9 1.4 copy-start.11
  166.9 6.5 %copy-start.7 = (pred[128]{0:T(512)(128)(4,1)S(1)}, pred[128]{0:T(512)(128)(4,1)}, u32[]{:S(2)}) copy-start(pred[128]{0:T(512)(128)(4,1)} %iota_compare_fusion.1) | copy-start | bytes 388
  170.0 10.6 %all-to-all-start.1 = ((f32[32,1,8]{2,1,0:T(1,128)}), f32[32,1,8]{2,1,0:T(1,128)S(1)}, u32[]{:S(2)}, u32[]{:S(2)}) async-start(f32[32,1,8]{2,1,0:T(1,128)} %convolution_bitcast_fusion.1), calls=%async_computation.1 | async-start | bytes 32768 | tf_op jit(solution)/shard_map/all_to_all | solution.py:238

commit v4 on v3

--- a/solution.py
+++ b/solution.py
@@ -15,10 +15,10 @@
 TREE_DEV = 8
 AXES = ("search", "net")
 CHUNK = 40
-PASSES = 3
+PASSES = 5
 CORE_CAP = 64
 LINK_CAP = 32
-FAR_CAP = 16
+FAR_CAP = 32
 
 
 def convolve(inputs, kernel):

time: 182 us -> 189 us (1.038)
  waiting for transfers between devices: 25.7 us -> 37.2 us
  local copies, waits for them, and re-layouts: 54.6 us -> 51.6 us
  starting transfers between devices: 24.7 us -> 22.2 us
  Pallas kernels: 4.63 us -> 6.76 us
    ppermute x5, waiting for transfers between devices: 18.4 us -> 26.6 us  [body(): lax.ppermute(outgoing[first:first + cap], AXES, pairs[e])]
    gather x1, local copies, waits for them, and re-layouts: 3.9 us -> 1.18 us  [body(): jnp.take(jnp.concatenate([results] + back, axis=0), lists[1, :slot_count]...]
    pallas_call x1, Pallas kernels: 4.63 us -> 6.76 us  [make_plan(): pl.pallas_call(functools.partial(plan_kernel, masks, caps, slot_count, wo...]
    ppermute x5, waiting for transfers between devices: 2.51 us -> 4.58 us  [body(): lax.ppermute(returned[first:first + cap], AXES, pairs[e])]
    slice x3 -> x2, local copies, waits for them, and re-layouts: 6.24 us -> 4.77 us  [body(): outgoing[first:first + cap]]
    unnamed x32 -> x34, local copies, waits for them, and re-layouts: 14.6 us -> 14.7 us
  transfers between devices with their start and end apart: 12 -> 12, of which waited for: 4 -> 6; matrix products, arithmetic and copies ran while one was open for 15% -> 12% of each run, Pallas kernels for 0% -> 0%
where the time goes in v4:
time: 189 us; the launch traced here: 188 us
  matrix products  55.5 us (29%)
  local copies, waits for them, and re-layouts  51.6 us (27%)
  waiting for transfers between devices  37.2 us (20%)
  starting transfers between devices  22.2 us (12%)
  other arithmetic  10.9 us (6%)
  Pallas kernels  6.76 us (4%)
  between operations  3.49 us (2%)
    conv_general_dilated x3, matrix products, convolve(): lax.conv_general_dilated(inputs, kernel, (1, 1), 'SAME', dimension_number...  46.4 us
    ppermute x5, waiting for transfers between devices, body(): lax.ppermute(outgoing[first:first + cap], AXES, pairs[e])  26.6 us
    unnamed x34, local copies, waits for them, and re-layouts  14.7 us
    all_to_all x1, starting transfers between devices, body(): lax.all_to_all(jnp.broadcast_to(counts, (groups, 1)), AXES, 0, 0, tiled=T...  7.33 us
    dot_general x1, matrix products, evaluate(): jnp.einsum('bhwc,cf->bfhw', hidden, policy_weight, preferred_element_type...  7.22 us
    gather x1, local copies, waits for them, and re-layouts, step(): rows = jnp.take(pool, idx, axis=0, mode='clip', indices_are_sorted=True)  7.01 us
    pallas_call x1, Pallas kernels, make_plan(): pl.pallas_call(functools.partial(plan_kernel, masks, caps, slot_count, wo...  6.76 us
    ppermute x5, starting transfers between devices, body(): lax.ppermute(outgoing[first:first + cap], AXES, pairs[e])  5.93 us
  transfers between devices with their start and end apart: 12, of which 6 were waited for; matrix products, arithmetic and copies ran while one was open for 12% of the time, Pallas kernels for 0%

profile of v4, /device:TPU:0, one launch (start us, length us, event | category | flops | bytes accessed | tf_op | source)
XLA Modules:
  0.0 188.0 jit_solution(17906637230775950575)
XLA Ops:
  1.3 0.6 broadcast_in_dim.65
  1.9 7.3 %all-to-all-start = ((s32[32,1,1]{2,1,0:T(1,128)}), s32[32,1,1]{2,1,0:T(1,128)S(1)}, u32[]{:S(2)}, u32[]{:S(2)}) async-start(s32[32,1,1]{2,1,0:T(1,128)} %broadcast_in_dim.65), calls=%async_computation | async-start | bytes 32768 | tf_op jit(solution)/shard_map/all_to_all | solution.py:165
  9.2 3.4 %copy.51 = bf16[128,11552]{1,0:T(8,128)(2,1)S(1)} copy(bf16[128,11552]{0,1:T(8,128)(2,1)} %param.15) | data formatting | bytes 5914624 | tf_op args[0]
  12.6 1.8 constant_dynamic-update-slice_fusion.6
  14.4 0.6 compare_reduce_fusion
  15.1 1.2 all-to-all-done
  16.3 1.3 fusion.18
  17.6 0.5 scatter.4.counts_ref
  18.1 0.5 broadcast_in_dim.66.me_ref
  18.6 6.8 %shard_map.130 = (s32[24,128]{1,0:T(8,128)}, s32[8,256]{1,0:T(8,128)}) custom-call(s32[1,128]{1,0:T(1,128)} %scatter.4.counts_ref, s32[1,128]{1,0:T(1,128)} %broadcast_in_dim.66.me_ref), custom_call_target="tpu_custom_call" | custom-call | tf_op jit(solution)/shard_map/pallas_call | solution.py:136
  25.4 0.8 fusion.22
  26.2 0.6 pad_clamp_fusion.2
  26.8 5.5 %gather_fusion.1 = bf16[192,11552]{1,0:T(8,128)(2,1)} fusion(bf16[128,11552]{1,0:T(8,128)(2,1)S(1)} %copy.51, s32[1024]{0:T(1024)S(1)} %get-tuple-element.124), kind=kCustom, calls=%fused_computation.1 | custom fusion | bytes 8872704 | tf_op jit(solution)/shard_map/jit(_take)/gather | solution.py:183
  32.3 3.3 %fusion.20 = (bf16[32,11552]{1,0:T(8,128)(2,1)S(1)}, bf16[32,11552]{1,0:T(8,128)(2,1)S(1)}, bf16[32,11552]{1,0:T(8,128)(2,1)}, bf16[32,11552]{1,0:T(8,128)(2,1)}) fusion(bf16[192,11552]{1,0:T(8,128)(2,1)} %gather_fusion.1), kind=kLoop, calls=%fused_computation.65 | loop fusion | bytes 5914624 | tf_op jit(solution)/shard_map/slice | solution.py:185
  35.6 1.4 collective-permute-start
  37.1 0.6 iota_compare_fusion.1
  37.6 0.6 multiply_add_fusion
  38.2 0.9 broadcast_compare_fusion
  39.2 1.5 slice.92
  40.6 1.3 fusion.23
  43.9 0.7 slice.64
  44.6 1.5 collective-permute-start.1
  46.1 1.5 collective-permute-start.2
  47.6 1.5 collective-permute-start.3
  49.0 0.7 slice_bitcast_fusion
  49.7 0.6 pad_clamp_fusion.1
  50.3 21.0 %collective-permute-done = bf16[32,11552]{1,0:T(8,128)(2,1)} collective-permute-done((bf16[32,11552]{1,0:T(8,128)(2,1)}, bf16[32,11552]{1,0:T(8,128)(2,1)}, u32[]{:S(2)}, u32[]{:S(2)}) %collective-permute-start) | collective-permute-done | bytes 739360 | tf_op jit(solution)/shard_map/ppermute | solution.py:185
  71.3 2.0 %constant_dynamic-update-slice_fusion.5 = bf16[320,11552]{1,0:T(8,128)(2,1)} fusion(bf16[320,11552]{1,0:T(8,128)(2,1)} %constant_dynamic-update-slice_fusion.6, bf16[32,11552]{1,0:T(8,128)(2,1)} %collective-permute-done), kind=kLoop, calls=%fused_computation.46 | loop fusion | bytes 1490944
  73.3 5.6 %collective-permute-done.1 = bf16[32,11552]{1,0:T(8,128)(2,1)} collective-permute-done((bf16[32,11552]{1,0:T(8,128)(2,1)}, bf16[32,11552]{1,0:T(8,128)(2,1)}, u32[]{:S(2)}, u32[]{:S(2)}) %collective-permute-start.1) | collective-permute-done | bytes 739360 | tf_op jit(solution)/shard_map/ppermute | solution.py:185
  78.9 2.0 %constant_dynamic-update-slice_fusion.4 = bf16[320,11552]{1,0:T(8,128)(2,1)} fusion(bf16[320,11552]{1,0:T(8,128)(2,1)} %constant_dynamic-update-slice_fusion.5, bf16[32,11552]{1,0:T(8,128)(2,1)} %collective-permute-done.1), kind=kLoop, calls=%fused_computation.45 | loop fusion | bytes 1490944
  80.9 2.0 %constant_dynamic-update-slice_fusion.3 = bf16[320,11552]{1,0:T(8,128)(2,1)} fusion(bf16[320,11552]{1,0:T(8,128)(2,1)} %constant_dynamic-update-slice_fusion.4, bf16[32,11552]{1,0:T(8,128)(2,1)} %collective-permute-done.2), kind=kLoop, calls=%fused_computation.44 | loop fusion | bytes 1490944
  83.0 2.1 %constant_dynamic-update-slice_fusion.2 = bf16[320,11552]{1,0:T(8,128)(2,1)} fusion(bf16[320,11552]{1,0:T(8,128)(2,1)} %constant_dynamic-update-slice_fusion.3, bf16[32,11552]{1,0:T(8,128)(2,1)} %collective-permute-done.3), kind=kLoop, calls=%fused_computation.43 | loop fusion | bytes 1490944
  85.1 2.6 %constant_dynamic-update-slice_fusion.1 = bf16[320,11552]{1,0:T(8,128)(2,1)} fusion(bf16[320,11552]{1,0:T(8,128)(2,1)} %constant_dynamic-update-slice_fusion.2, bf16[64,11552]{1,0:T(8,128)(2,1)} %collective-permute-done.4), kind=kLoop, calls=%fused_computation.42 | loop fusion | bytes 2981888 | tf_op jit(solution)/shard_map/concatenate | solution.py:189
  87.7 1.1 broadcast_in_dim.64
  88.9 66.6 %while.11 = (s32[]{:T(128)}, bf16[224,2944]{1,0:T(8,128)(2,1)}, s32[]{:T(128)}, s32[160]{0:T(256)S(1)}, bf16[320,11552]{1,0:T(8,128)(2,1)}, /*index=5*/bf16[3,3,...) while((s32[]{:T(128)}, bf16[224,2944]{1,0:T(8,128)(2,1)}, ...), condition=%wide.region_3.4_spmd, body=%wide.region_1.3_spmd.sunk | while | flops 33799694336 | bytes 71023168 | solution.py:208
  89.2 7.0 %gather_fusion = bf16[40,11552]{1,0:T(8,128)(2,1)} fusion(bf16[320,11552]{1,0:T(8,128)(2,1)} %get-tuple-element.235, s32[1024]{0:T(1024)S(1)} %pad_clamp_fusion.5), kind=kCustom, calls=%fused_computation.clone.1 | custom fusion | bytes 1848480 | tf_op jit(solution)/shard_map/while/body/jit(_take)/gather | solution.py:196
  96.2 3.3 %copy.71 = bf16[40,11552]{0,1:T(8,128)(2,1)S(1)} copy(bf16[40,11552]{1,0:T(8,128)(2,1)} %gather_fusion) | data formatting | bytes 1848320 | tf_op jit(solution)/shard_map/while/body/reshape | solution.py:37
  99.5 8.2 %maximum_convert_fusion.5 = bf16[40,19,19,256]{3,0,2,1:T(8,128)(2,1)S(1)} fusion(bf16[40,19,19,32]{0,3,2,1:T(8,128)(2,1)S(1)} %bitcast.89, bf16[3,3,32,256]{3,2,1,0:T(8,128)(2,1)S(1)} %get-tuple-element.236), kind=kOutput, calls=%fused_computation.7.clone.1 | convolution fusion | flops 1989857280 | bytes 8464896 | tf_op jit(solution)/shard_map/while/body/conv_general_dilated | solution.py:25
  107.7 18.3 %maximum_convert_fusion.6 = bf16[40,19,19,256]{3,0,2,1:T(8,128)(2,1)S(1)} fusion(bf16[40,19,19,256]{3,0,2,1:T(8,128)(2,1)S(1)} %maximum_convert_fusion.5, bf16[1,3,3,256,256]{4,3,2,1,0:T(8,128)(2,1)S(1)} %copy-done.9), kind=kOutput, calls=%fused_computation.6.clone.1 | convolution fusion | flops 15867105280 | bytes 15966208 | tf_op jit(solution)/shard_map/while/body/conv_general_dilated | solution.py:25
  126.1 19.9 %convert_reduce_fusion.3 = (f32[40,256]{1,0:T(8,128)S(1)}, bf16[40,19,19,256]{3,0,2,1:T(8,128)(2,1)}) fusion(bf16[40,19,19,256]{3,0,2,1:T(8,128)(2,1)S(1)} %maximum_convert_fusion.6, bf16[1,3,3,256,256]{4,3,2,1,0:T(8,128)(2,1)S(1)} %copy-done.10, bf16[40,19,19,256]{3,0,2,1:T(8,128)(2,1)S(1)} %maximum_convert_fusion.5), kind=kOutput, calls=%fused_computation.4.clone.1 | convolution fusion | flops 15881881600 | bytes 23400448 | tf_op jit(solution)/shard_map/while/body/conv_general_dilated | solution.py:25
  146.1 0.2 copy.72
  146.2 7.2 %convolution_convert_fusion.3 = bf16[40,19,19,8]{0,3,2,1:T(8,128)(2,1)S(1)} fusion(bf16[40,19,19,256]{3,0,2,1:T(8,128)(2,1)} %get-tuple-element.196, bf16[256,8]{0,1:T(8,128)(2,1)S(1)} %get-tuple-element.239), kind=kOutput, calls=%fused_computation.8.clone.1 | convolution fusion | flops 59261760 | bytes 7628416 | tf_op jit(solution)/shard_map/while/body/bhwc,cf->bfhw/dot_general | solution.py:43
  153.5 0.6 copy.73
  154.1 0.2 convert_element_type.69
  154.4 0.1 fusion.56
  154.8 0.7 constant_dynamic-update-slice_fusion.14
  155.5 4.1 %gather_fusion.2 = bf16[192,2944]{1,0:T(8,128)(2,1)S(1)} fusion(bf16[224,2944]{1,0:T(8,128)(2,1)} %get-tuple-element.77, s32[1024]{0:T(1024)} %get-tuple-element.123), kind=kCustom, calls=%fused_computation.2 | custom fusion | bytes 2261760 | tf_op jit(solution)/shard_map/jit(_take)/gather | solution.py:215
  159.8 2.3 %collective-permute-start.6 = (bf16[32,2944]{1,0:T(8,128)(2,1)S(1)}, bf16[32,2944]{1,0:T(8,128)(2,1)S(1)}, u32[]{:S(2)}, u32[]{:S(2)}) collective-permute-start(bf16[32,2944]{1,0:T(8,128)(2,1)S(1)} %get-tuple-element.119), channel_id=1, source_target_pairs={{0,2},{1,3},{2,0},{3,1},{4,6},{5,7},{6,4},{7,5},{8,10},{9,11},{10,... | collective-permute-start | bytes 565256 | tf_op jit(solution)/shard_map/ppermute | solution.py:217
  162.0 1.5 collective-permute-start.7
  163.5 1.5 collective-permute-start.8
  165.1 4.4 %collective-permute-done.5 = bf16[32,2944]{1,0:T(8,128)(2,1)S(1)} collective-permute-done((bf16[32,2944]{1,0:T(8,128)(2,1)S(1)}, bf16[32,2944]{1,0:T(8,128)(2,1)S(1)}, u32[]{:S(2)}, u32[]{:S(2)}) %collective-permute-start.5) | collective-permute-done | bytes 188448 | tf_op jit(solution)/shard_map/ppermute | solution.py:217
  169.5 0.2 collective-permute-done.6
  169.8 1.2 gather_fusion.3
  171.0 1.2 copy.57
  172.2 1.3 reshape.122
  173.5 0.6 select_reduce_fusion
  174.1 0.6 fusion.13
  174.7 0.2 fusion.15
  174.9 1.6 convolution_bitcast_fusion.1
  176.6 3.7 %all-to-all-start.1 = ((f32[32,1,8]{2,1,0:T(1,128)}), f32[32,1,8]{2,1,0:T(1,128)S(1)}, u32[]{:S(2)}, u32[]{:S(2)}) async-start(f32[32,1,8]{2,1,0:T(1,128)} %convolution_bitcast_fusion.1), calls=%async_computation.1 | async-start | bytes 32768 | tf_op jit(solution)/shard_map/all_to_all | solution.py:238
  180.3 1.8 divide_select_fusion
  182.1 0.5 broadcast_select_fusion.1
  182.6 4.8 %all-to-all-done.1 = f32[32,1,8]{2,1,0:T(1,128)S(1)} async-done(((f32[32,1,8]{2,1,0:T(1,128)}), f32[32,1,8]{2,1,0:T(1,128)S(1)}, u32[]{:S(2)}, u32[]{:S(2)}) %all-to-all-start.1) | async-done | bytes 1056 | tf_op jit(solution)/shard_map/all_to_all | solution.py:238
  187.4 0.6 reduce_sum.28
  (51 shorter events, 1.0 us)
Async XLA Ops:
  1.9 14.4 %all-to-all-start = ((s32[32,1,1]{2,1,0:T(1,128)}), s32[32,1,1]{2,1,0:T(1,128)S(1)}, u32[]{:S(2)}, u32[]{:S(2)}) async-start(s32[32,1,1]{2,1,0:T(1,128)} %broadcast_in_dim.65), calls=%async_computation | async-start | bytes 32768 | tf_op jit(solution)/shard_map/all_to_all | solution.py:165
  32.3 5.9 %copy-start.3 = (s32[128,8,361]{0,1,2:T(8,128)S(1)}, s32[128,8,361]{0,1,2:T(8,128)}, u32[]{:S(2)}) copy-start(s32[128,8,361]{0,1,2:T(8,128)} %param.18) | copy-start | bytes 4435972
  35.6 35.7 %collective-permute-start = (bf16[32,11552]{1,0:T(8,128)(2,1)}, bf16[32,11552]{1,0:T(8,128)(2,1)}, u32[]{:S(2)}, u32[]{:S(2)}) collective-permute-start(bf16[32,11552]{1,0:T(8,128)(2,1)} %get-tuple-element.116), channel_id=1, source_target_pairs={{0,4},{1,5},{2,6},{3,7},{4,0},{5,1},{6,2},{7,3},{8,12},{9,13},{10,... | collective-permute-start | bytes 2217992 | tf_op jit(solution)/shard_map/ppermute | solution.py:185
  44.6 34.3 %collective-permute-start.1 = (bf16[32,11552]{1,0:T(8,128)(2,1)}, bf16[32,11552]{1,0:T(8,128)(2,1)}, u32[]{:S(2)}, u32[]{:S(2)}) collective-permute-start(bf16[32,11552]{1,0:T(8,128)(2,1)} %get-tuple-element.115), channel_id=1, source_target_pairs={{0,2},{1,3},{2,0},{3,1},{4,6},{5,7},{6,4},{7,5},{8,10},{9,11},{10,... | collective-permute-start | bytes 2217992 | tf_op jit(solution)/shard_map/ppermute | solution.py:185
  46.1 34.9 %collective-permute-start.2 = (bf16[32,11552]{1,0:T(8,128)(2,1)S(1)}, bf16[32,11552]{1,0:T(8,128)(2,1)}, u32[]{:S(2)}, u32[]{:S(2)}) collective-permute-start(bf16[32,11552]{1,0:T(8,128)(2,1)S(1)} %get-tuple-element.114), channel_id=1, source_target_pairs={{0,16},{1,17},{2,18},{3,19},{4,20},{5,21},{6,22},{7,23},{8,24},{9,... | collective-permute-start | bytes 2217992 | tf_op jit(solution)/shard_map/ppermute | solution.py:185
  47.6 35.4 %collective-permute-start.3 = (bf16[32,11552]{1,0:T(8,128)(2,1)S(1)}, bf16[32,11552]{1,0:T(8,128)(2,1)}, u32[]{:S(2)}, u32[]{:S(2)}) collective-permute-start(bf16[32,11552]{1,0:T(8,128)(2,1)S(1)} %get-tuple-element.113), channel_id=1, source_target_pairs={{0,1},{1,0},{2,3},{3,2},{4,5},{5,4},{6,7},{7,6},{8,9},{9,8},{10,11... | collective-permute-start | bytes 2217992 | tf_op jit(solution)/shard_map/ppermute | solution.py:185
  49.0 36.0 %collective-permute-start.4 = (bf16[64,11552]{1,0:T(8,128)(2,1)S(1)}, bf16[64,11552]{1,0:T(8,128)(2,1)}, u32[]{:S(2)}, u32[]{:S(2)}) collective-permute-start(bf16[64,11552]{1,0:T(8,128)(2,1)S(1)} %slice.92), channel_id=1, source_target_pairs={{0,8},{1,9},{2,10},{3,11},{4,12},{5,13},{6,14},{7,15},{8,0},{9,1},... | collective-permute-start | bytes 4435976 | tf_op jit(solution)/shard_map/ppermute | solution.py:185
  85.0 3.8 %copy-start.2 = (bf16[3,3,32,256]{3,2,1,0:T(8,128)(2,1)S(1)}, bf16[3,3,32,256]{3,2,1,0:T(8,128)(2,1)}, u32[]{:S(2)}) copy-start(bf16[3,3,32,256]{3,2,1,0:T(8,128)(2,1)} %param.19) | copy-start | bytes 442372
  85.0 3.8 %copy-start.4 = (bf16[256,8]{0,1:T(8,128)(2,1)S(1)}, bf16[256,8]{0,1:T(8,128)(2,1)}, u32[]{:S(2)}) copy-start(bf16[256,8]{0,1:T(8,128)(2,1)} %param.22) | copy-start | bytes 12292
  85.0 3.8 %copy-start.5 = (bf16[256,8]{0,1:T(8,128)(2,1)S(1)}, bf16[256,8]{0,1:T(8,128)(2,1)}, u32[]{:S(2)}) copy-start(bf16[256,8]{0,1:T(8,128)(2,1)} %param.23) | copy-start | bytes 12292
  85.0 3.8 %copy-start.11 = (bf16[256]{0:T(256)(128)(2,1)S(1)}, bf16[256]{0:T(256)(128)(2,1)}, u32[]{:S(2)}) copy-start(bf16[256]{0:T(256)(128)(2,1)} %param.24) | copy-start | bytes 1540
  99.5 8.2 %copy-start.9 = (bf16[1,3,3,256,256]{4,3,2,1,0:T(8,128)(2,1)S(1)}, bf16[1,3,3,256,256]{4,3,2,1,0:T(8,128)(2,1)}, u32[]{:S(2)}) copy-start(bf16[1,3,3,256,256]{4,3,2,1,0:T(8,128)(2,1)} %get-tuple-element.237) | copy-start | bytes 3538948 | tf_op jit(solution)/shard_map/while
  107.7 18.4 %copy-start.10 = (bf16[1,3,3,256,256]{4,3,2,1,0:T(8,128)(2,1)S(1)}, bf16[1,3,3,256,256]{4,3,2,1,0:T(8,128)(2,1)}, u32[]{:S(2)}) copy-start(bf16[1,3,3,256,256]{4,3,2,1,0:T(8,128)(2,1)} %get-tuple-element.238) | copy-start | bytes 3538948 | tf_op jit(solution)/shard_map/while
  159.6 5.4 %copy-start = (bf16[224,2944]{1,0:T(8,128)(2,1)S(1)}, bf16[224,2944]{1,0:T(8,128)(2,1)}, u32[]{:S(2)}) copy-start(bf16[224,2944]{1,0:T(8,128)(2,1)} %get-tuple-element.77) | copy-start | bytes 3956740
  159.7 9.8 %collective-permute-start.5 = (bf16[32,2944]{1,0:T(8,128)(2,1)S(1)}, bf16[32,2944]{1,0:T(8,128)(2,1)S(1)}, u32[]{:S(2)}, u32[]{:S(2)}) collective-permute-start(bf16[32,2944]{1,0:T(8,128)(2,1)S(1)} %get-tuple-element.120), channel_id=1, source_target_pairs={{0,4},{1,5},{2,6},{3,7},{4,0},{5,1},{6,2},{7,3},{8,12},{9,13},{10,... | collective-permute-start | bytes 565256 | tf_op jit(solution)/shard_map/ppermute | solution.py:217
  159.8 9.9 %collective-permute-start.6 = (bf16[32,2944]{1,0:T(8,128)(2,1)S(1)}, bf16[32,2944]{1,0:T(8,128)(2,1)S(1)}, u32[]{:S(2)}, u32[]{:S(2)}) collective-permute-start(bf16[32,2944]{1,0:T(8,128)(2,1)S(1)} %get-tuple-element.119), channel_id=1, source_target_pairs={{0,2},{1,3},{2,0},{3,1},{4,6},{5,7},{6,4},{7,5},{8,10},{9,11},{10,... | collective-permute-start | bytes 565256 | tf_op jit(solution)/shard_map/ppermute | solution.py:217
  162.0 7.6 %collective-permute-start.7 = (bf16[32,2944]{1,0:T(8,128)(2,1)S(1)}, bf16[32,2944]{1,0:T(8,128)(2,1)S(1)}, u32[]{:S(2)}, u32[]{:S(2)}) collective-permute-start(bf16[32,2944]{1,0:T(8,128)(2,1)S(1)} %get-tuple-element.118), channel_id=1, source_target_pairs={{0,16},{1,17},{2,18},{3,19},{4,20},{5,21},{6,22},{7,23},{8,24},{9,... | collective-permute-start | bytes 565256 | tf_op jit(solution)/shard_map/ppermute | solution.py:217
  163.5 6.2 %collective-permute-start.8 = (bf16[32,2944]{1,0:T(8,128)(2,1)S(1)}, bf16[32,2944]{1,0:T(8,128)(2,1)S(1)}, u32[]{:S(2)}, u32[]{:S(2)}) collective-permute-start(bf16[32,2944]{1,0:T(8,128)(2,1)S(1)} %get-tuple-element.117), channel_id=1, source_target_pairs={{0,1},{1,0},{2,3},{3,2},{4,5},{5,4},{6,7},{7,6},{8,9},{9,8},{10,11... | collective-permute-start | bytes 565256 | tf_op jit(solution)/shard_map/ppermute | solution.py:217
  165.0 4.8 %collective-permute-start.9 = (bf16[64,2944]{1,0:T(8,128)(2,1)S(1)}, bf16[64,2944]{1,0:T(8,128)(2,1)S(1)}, u32[]{:S(2)}, u32[]{:S(2)}) collective-permute-start(bf16[64,2944]{1,0:T(8,128)(2,1)S(1)} %slice.97), channel_id=1, source_target_pairs={{0,8},{1,9},{2,10},{3,11},{4,12},{5,13},{6,14},{7,15},{8,0},{9,1},... | collective-permute-start | bytes 1130504 | tf_op jit(solution)/shard_map/ppermute | solution.py:217
  171.0 2.5 %copy-start.1 = (pred[128,8,361]{0,1,2:T(8,128)(4,1)S(1)}, pred[128,8,361]{0,1,2:T(8,128)(4,1)}, u32[]{:S(2)}) copy-start(pred[128,8,361]{0,1,2:T(8,128)(4,1)} %broadcast_compare_fusion) | copy-start | bytes 1108996
  171.0 2.5 %copy-start.7 = (f32[8]{0:T(128)S(1)}, f32[8]{0:T(128)}, u32[]{:S(2)}) copy-start(f32[8]{0:T(128)} %param.25) | copy-start | bytes 100
  173.5 1.4 copy-start.6
  173.5 1.4 copy-start.12
  173.5 6.8 %copy-start.8 = (pred[128]{0:T(512)(128)(4,1)S(1)}, pred[128]{0:T(512)(128)(4,1)}, u32[]{:S(2)}) copy-start(pred[128]{0:T(512)(128)(4,1)} %iota_compare_fusion.1) | copy-start | bytes 388
  176.6 10.9 %all-to-all-start.1 = ((f32[32,1,8]{2,1,0:T(1,128)}), f32[32,1,8]{2,1,0:T(1,128)S(1)}, u32[]{:S(2)}, u32[]{:S(2)}) async-start(f32[32,1,8]{2,1,0:T(1,128)} %convolution_bitcast_fusion.1), calls=%async_computation.1 | async-start | bytes 32768 | tf_op jit(solution)/shard_map/all_to_all | solution.py:238

commit v5 on v2

--- a/solution.py
+++ b/solution.py
@@ -15,7 +15,7 @@
 TREE_DEV = 8
 AXES = ("search", "net")
 CHUNK = 40
-PASSES = 3
+PASSES = 5
 CORE_CAP = 64
 LINK_CAP = 32
 FAR_CAP = 16

time: 177 us -> 180 us (1.017)
  Pallas kernels: 4.62 us -> 6.75 us
    pallas_call x1, Pallas kernels: 4.62 us -> 6.75 us  [make_plan(): pl.pallas_call(functools.partial(plan_kernel, masks, caps, slot_count, wo...]
where the time goes in v5:
time: 180 us; the launch traced here: 179 us
  matrix products  55.5 us (31%)
  local copies, waits for them, and re-layouts  41.5 us (23%)
  starting transfers between devices  25.4 us (14%)
  between operations  21.3 us (12%)
  waiting for transfers between devices  18.9 us (10%)
  other arithmetic  8.98 us (5%)
  Pallas kernels  6.75 us (4%)
    conv_general_dilated x3, matrix products, convolve(): lax.conv_general_dilated(inputs, kernel, (1, 1), 'SAME', dimension_number...  46.4 us
    unnamed x34, local copies, waits for them, and re-layouts  15.2 us
    ppermute x5, waiting for transfers between devices, body(): lax.ppermute(lax.dynamic_slice(padded, (starts[e], 0), (cap, row)), AXES,...  10.2 us
    all_to_all x1, starting transfers between devices, body(): lax.all_to_all(jnp.broadcast_to(counts, (groups, 1)), AXES, 0, 0, tiled=T...  7.33 us
    ppermute x5, starting transfers between devices, body(): lax.ppermute(lax.dynamic_slice(results, (places[e], 0), (cap, width)), AX...  7.24 us
    dot_general x1, matrix products, evaluate(): jnp.einsum('bhwc,cf->bfhw', hidden, policy_weight, preferred_element_type...  7.22 us
    ppermute x5, starting transfers between devices, body(): lax.ppermute(lax.dynamic_slice(padded, (starts[e], 0), (cap, row)), AXES,...  7.16 us
    gather x1, local copies, waits for them, and re-layouts, step(): rows = jnp.take(pool, idx, axis=0, mode='clip', indices_are_sorted=True)  6.81 us
  transfers between devices with their start and end apart: 12, of which 5 were waited for; matrix products, arithmetic and copies ran while one was open for 12% of the time, Pallas kernels for 0%

profile of v5, /device:TPU:0, one launch (start us, length us, event | category | flops | bytes accessed | tf_op | source)
XLA Modules:
  0.0 178.6 jit_solution(3532800779313081684)
XLA Ops:
  1.3 0.6 broadcast_in_dim.58
  1.9 7.3 %all-to-all-start = ((s32[32,1,1]{2,1,0:T(1,128)}), s32[32,1,1]{2,1,0:T(1,128)S(1)}, u32[]{:S(2)}, u32[]{:S(2)}) async-start(s32[32,1,1]{2,1,0:T(1,128)} %broadcast_in_dim.58), calls=%async_computation | async-start | bytes 32768 | tf_op jit(solution)/shard_map/all_to_all | solution.py:154
  9.2 0.6 multiply_add_fusion
  9.8 3.4 %copy.51 = bf16[128,11552]{1,0:T(8,128)(2,1)S(1)} copy(bf16[128,11552]{0,1:T(8,128)(2,1)} %param.15) | data formatting | bytes 5914624 | tf_op args[0]
  13.2 1.8 %constant_dynamic-update-slice_fusion.6 = bf16[304,11552]{1,0:T(8,128)(2,1)} fusion(bf16[128,11552]{1,0:T(8,128)(2,1)S(1)} %copy.51), kind=kLoop, calls=%fused_computation.50 | loop fusion | bytes 5939200
  15.1 1.0 broadcast_compare_fusion
  16.1 0.5 iota_compare_fusion.1
  16.6 0.6 compare_reduce_fusion
  17.3 1.3 fusion.18
  18.6 0.5 scatter.4.counts_ref
  19.1 0.5 broadcast_in_dim.59.me_ref
  19.6 6.7 %shard_map.130 = (s32[24,128]{1,0:T(8,128)}, s32[8,256]{1,0:T(8,128)}) custom-call(s32[1,128]{1,0:T(1,128)} %scatter.4.counts_ref, s32[1,128]{1,0:T(1,128)} %broadcast_in_dim.59.me_ref), custom_call_target="tpu_custom_call" | custom-call | tf_op jit(solution)/shard_map/pallas_call | solution.py:125
  26.4 1.6 fusion.20
  43.2 1.9 %pad_dynamic-slice_fusion.1 = (bf16[32,11552]{1,0:T(8,128)(2,1)}, bf16[32,11552]{1,0:T(8,128)(2,1)}, bf16[32,11552]{1,0:T(8,128)(2,1)}) fusion(s32[]{:T(128)S(6)} %select_n.69, bf16[128,11552]{1,0:T(8,128)(2,1)S(1)} %copy.51, s32[]{:T(128)S(6)} %select_n.67, s32[]{:T(128)S(6)} %select_n.68), kind=kLoop, calls=%fused_computation.26 | loop fusion | bytes 5175308 | tf_op jit(solution)/shard_map/dynamic_slice | solution.py:175
  45.1 1.8 collective-permute-start.1
  47.5 0.9 pad_dynamic-slice_fusion.4
  48.4 2.4 %collective-permute-start = (bf16[16,11552]{1,0:T(8,128)(2,1)}, bf16[16,11552]{1,0:T(8,128)(2,1)S(1)}, u32[]{:S(2)}, u32[]{:S(2)}) collective-permute-start(bf16[16,11552]{1,0:T(8,128)(2,1)} %pad_dynamic-slice_fusion.4), channel_id=1, source_target_pairs={{0,4},{1,5},{2,6},{3,7},{4,0},{5,1},{6,2},{7,3},{8,12},{9,13},{10,... | collective-permute-start | bytes 1109000 | tf_op jit(solution)/shard_map/ppermute | solution.py:175
  50.8 1.5 collective-permute-start.2
  52.3 1.5 collective-permute-start.3
  54.5 1.6 pad_dynamic-slice_fusion
  56.1 0.7 slice.73
  60.0 0.7 slice_bitcast_fusion
  60.7 0.6 pad_clamp_fusion.1
  61.3 10.1 %collective-permute-done = bf16[16,11552]{1,0:T(8,128)(2,1)S(1)} collective-permute-done((bf16[16,11552]{1,0:T(8,128)(2,1)}, bf16[16,11552]{1,0:T(8,128)(2,1)S(1)}, u32[]{:S(2)}, u32[]{:S(2)}) %collective-permute-start) | collective-permute-done | bytes 369696 | tf_op jit(solution)/shard_map/ppermute | solution.py:175
  71.4 0.8 constant_dynamic-update-slice_fusion.5
  72.2 2.1 %constant_dynamic-update-slice_fusion.4 = bf16[304,11552]{1,0:T(8,128)(2,1)} fusion(bf16[304,11552]{1,0:T(8,128)(2,1)} %constant_dynamic-update-slice_fusion.5, bf16[32,11552]{1,0:T(8,128)(2,1)} %collective-permute-done.1), kind=kLoop, calls=%fused_computation.48 | loop fusion | bytes 1490944
  74.3 2.0 %constant_dynamic-update-slice_fusion.3 = bf16[304,11552]{1,0:T(8,128)(2,1)} fusion(bf16[304,11552]{1,0:T(8,128)(2,1)} %constant_dynamic-update-slice_fusion.4, bf16[32,11552]{1,0:T(8,128)(2,1)} %collective-permute-done.2), kind=kLoop, calls=%fused_computation.47 | loop fusion | bytes 1490944
  76.3 2.1 %constant_dynamic-update-slice_fusion.2 = bf16[304,11552]{1,0:T(8,128)(2,1)} fusion(bf16[304,11552]{1,0:T(8,128)(2,1)} %constant_dynamic-update-slice_fusion.3, bf16[32,11552]{1,0:T(8,128)(2,1)} %collective-permute-done.3), kind=kLoop, calls=%fused_computation.46 | loop fusion | bytes 1490944
  78.4 1.2 constant_dynamic-update-slice_fusion.1
  79.6 1.1 broadcast_in_dim.57
  80.8 66.4 %while.11 = (s32[]{:T(128)}, bf16[224,2944]{1,0:T(8,128)(2,1)}, s32[]{:T(128)}, s32[160]{0:T(256)S(1)}, bf16[304,11552]{1,0:T(8,128)(2,1)}, /*index=5*/bf16[3,3,...) while((s32[]{:T(128)}, bf16[224,2944]{1,0:T(8,128)(2,1)}, ...), condition=%wide.region_3.4_spmd, body=%wide.region_1.3_spmd.sunk | while | flops 33799694336 | bytes 71023168 | solution.py:198
  81.1 6.8 %gather_fusion = bf16[40,11552]{1,0:T(8,128)(2,1)} fusion(bf16[304,11552]{1,0:T(8,128)(2,1)} %get-tuple-element.240, s32[1024]{0:T(1024)S(1)} %pad_clamp_fusion.3), kind=kCustom, calls=%fused_computation.clone.1 | custom fusion | bytes 1848480 | tf_op jit(solution)/shard_map/while/body/jit(_take)/gather | solution.py:186
  87.9 3.3 %copy.71 = bf16[40,11552]{0,1:T(8,128)(2,1)S(1)} copy(bf16[40,11552]{1,0:T(8,128)(2,1)} %gather_fusion) | data formatting | bytes 1848320 | tf_op jit(solution)/shard_map/while/body/reshape | solution.py:37
  91.2 8.2 %maximum_convert_fusion.5 = bf16[40,19,19,256]{3,0,2,1:T(8,128)(2,1)S(1)} fusion(bf16[40,19,19,32]{0,3,2,1:T(8,128)(2,1)S(1)} %bitcast.97, bf16[3,3,32,256]{3,2,1,0:T(8,128)(2,1)S(1)} %get-tuple-element.241), kind=kOutput, calls=%fused_computation.5.clone.1 | convolution fusion | flops 1989857280 | bytes 8464896 | tf_op jit(solution)/shard_map/while/body/conv_general_dilated | solution.py:25
  99.4 18.3 %maximum_convert_fusion.6 = bf16[40,19,19,256]{3,0,2,1:T(8,128)(2,1)S(1)} fusion(bf16[40,19,19,256]{3,0,2,1:T(8,128)(2,1)S(1)} %maximum_convert_fusion.5, bf16[1,3,3,256,256]{4,3,2,1,0:T(8,128)(2,1)S(1)} %copy-done.9), kind=kOutput, calls=%fused_computation.4.clone.1 | convolution fusion | flops 15867105280 | bytes 15966208 | tf_op jit(solution)/shard_map/while/body/conv_general_dilated | solution.py:25
  117.8 19.9 %convert_reduce_fusion.3 = (f32[40,256]{1,0:T(8,128)S(1)}, bf16[40,19,19,256]{3,0,2,1:T(8,128)(2,1)}) fusion(bf16[40,19,19,256]{3,0,2,1:T(8,128)(2,1)S(1)} %maximum_convert_fusion.6, bf16[1,3,3,256,256]{4,3,2,1,0:T(8,128)(2,1)S(1)} %copy-done.10, bf16[40,19,19,256]{3,0,2,1:T(8,128)(2,1)S(1)} %maximum_convert_fusion.5), kind=kOutput, calls=%fused_computation.2.clone.1 | convolution fusion | flops 15881881600 | bytes 23400448 | tf_op jit(solution)/shard_map/while/body/conv_general_dilated | solution.py:25
  137.6 0.1 fusion.52
  137.8 0.2 copy.72
  137.9 7.2 %convolution_convert_fusion.3 = bf16[40,19,19,8]{0,3,2,1:T(8,128)(2,1)S(1)} fusion(bf16[40,19,19,256]{3,0,2,1:T(8,128)(2,1)} %get-tuple-element.201, bf16[256,8]{0,1:T(8,128)(2,1)S(1)} %get-tuple-element.244), kind=kOutput, calls=%fused_computation.6.clone.1 | convolution fusion | flops 59261760 | bytes 7628416 | tf_op jit(solution)/shard_map/while/body/bhwc,cf->bfhw/dot_general | solution.py:43
  145.2 0.6 copy.73
  145.8 0.2 convert_element_type.69
  146.1 0.1 fusion.53
  146.4 0.7 constant_dynamic-update-slice_fusion.14
  147.2 1.5 constant_dynamic-update-slice_fusion.12
  148.7 0.2 copy-done
  148.9 3.3 %collective-permute-start.5 = (bf16[16,2944]{1,0:T(8,128)(2,1)S(1)}, bf16[16,2944]{1,0:T(8,128)(2,1)S(1)}, u32[]{:S(2)}, u32[]{:S(2)}) collective-permute-start(bf16[16,2944]{1,0:T(8,128)(2,1)S(1)} %constant_dynamic-slice_fusion.4), channel_id=1, source_target_pairs={{0,4},{1,5},{2,6},{3,7},{4,0},{5,1},{6,2},{7,3},{8,12},{9,13},{10,... | collective-permute-start | bytes 282632 | tf_op jit(solution)/shard_map/ppermute | solution.py:206
  152.2 0.1 constant_dynamic-slice_fusion.1
  152.3 0.9 collective-permute-start.6
  153.2 1.5 collective-permute-start.7
  154.8 1.5 collective-permute-start.8
  156.4 2.3 %collective-permute-done.6 = bf16[32,2944]{1,0:T(8,128)(2,1)S(1)} collective-permute-done((bf16[32,2944]{1,0:T(8,128)(2,1)S(1)}, bf16[32,2944]{1,0:T(8,128)(2,1)S(1)}, u32[]{:S(2)}, u32[]{:S(2)}) %collective-permute-start.6) | collective-permute-done | bytes 188448 | tf_op jit(solution)/shard_map/ppermute | solution.py:206
  158.8 1.5 collective-permute-done.8
  160.4 1.2 gather_fusion.1
  161.6 1.2 copy.57
  162.8 1.3 reshape.142
  164.1 0.6 select_reduce_fusion
  164.7 0.6 fusion.13
  165.3 0.2 fusion.15
  165.5 1.7 convolution_bitcast_fusion.1
  167.2 3.7 %all-to-all-start.1 = ((f32[32,1,8]{2,1,0:T(1,128)}), f32[32,1,8]{2,1,0:T(1,128)S(1)}, u32[]{:S(2)}, u32[]{:S(2)}) async-start(f32[32,1,8]{2,1,0:T(1,128)} %convolution_bitcast_fusion.1), calls=%async_computation.1 | async-start | bytes 32768 | tf_op jit(solution)/shard_map/all_to_all | solution.py:227
  170.9 1.8 %divide_select_fusion = f32[128,8,362]{0,1,2:T(8,128)} fusion(f32[128,8,362]{0,2,1:T(8,128)S(1)} %reshape.142, pred[128,8,361]{0,1,2:T(8,128)(4,1)S(1)} %copy-done.1, f32[128,8]{0,1:T(8,128)S(1)} %fusion.13, f32[128,8]{0,1:T(8,128)S(1)} %select_reduce_fusion, f32[8]{0:T(128)S(1)} %copy-done.7, pred[128]{0:T(512)(128)(4,1)S(1)} %copy-done.8), kind=kLoop, calls=%fused_computation.31 | loop fusion | flops 1853440 | bytes 3343520 | tf_op jit(solution)/shard_map/jit(_where)/select_n | solution.py:218
  172.7 0.5 broadcast_select_fusion.1
  173.2 4.8 %all-to-all-done.1 = f32[32,1,8]{2,1,0:T(1,128)S(1)} async-done(((f32[32,1,8]{2,1,0:T(1,128)}), f32[32,1,8]{2,1,0:T(1,128)S(1)}, u32[]{:S(2)}, u32[]{:S(2)}) %all-to-all-start.1) | async-done | bytes 1056 | tf_op jit(solution)/shard_map/all_to_all | solution.py:227
  178.0 0.6 reduce_sum.28
  (49 shorter events, 1.0 us)
Async XLA Ops:
  1.9 15.4 %all-to-all-start = ((s32[32,1,1]{2,1,0:T(1,128)}), s32[32,1,1]{2,1,0:T(1,128)S(1)}, u32[]{:S(2)}, u32[]{:S(2)}) async-start(s32[32,1,1]{2,1,0:T(1,128)} %broadcast_in_dim.58), calls=%async_computation | async-start | bytes 32768 | tf_op jit(solution)/shard_map/all_to_all | solution.py:154
  13.2 1.9 %copy-start.3 = (s32[128,8,361]{0,1,2:T(8,128)S(1)}, s32[128,8,361]{0,1,2:T(8,128)}, u32[]{:S(2)}) copy-start(s32[128,8,361]{0,1,2:T(8,128)} %param.18) | copy-start | bytes 4435972
  45.1 27.1 %collective-permute-start.1 = (bf16[32,11552]{1,0:T(8,128)(2,1)}, bf16[32,11552]{1,0:T(8,128)(2,1)}, u32[]{:S(2)}, u32[]{:S(2)}) collective-permute-start(bf16[32,11552]{1,0:T(8,128)(2,1)} %get-tuple-element.114), channel_id=1, source_target_pairs={{0,2},{1,3},{2,0},{3,1},{4,6},{5,7},{6,4},{7,5},{8,10},{9,11},{10,... | collective-permute-start | bytes 2217992 | tf_op jit(solution)/shard_map/ppermute | solution.py:175
  48.4 22.9 %collective-permute-start = (bf16[16,11552]{1,0:T(8,128)(2,1)}, bf16[16,11552]{1,0:T(8,128)(2,1)S(1)}, u32[]{:S(2)}, u32[]{:S(2)}) collective-permute-start(bf16[16,11552]{1,0:T(8,128)(2,1)} %pad_dynamic-slice_fusion.4), channel_id=1, source_target_pairs={{0,4},{1,5},{2,6},{3,7},{4,0},{5,1},{6,2},{7,3},{8,12},{9,13},{10,... | collective-permute-start | bytes 1109000 | tf_op jit(solution)/shard_map/ppermute | solution.py:175
  50.8 23.4 %collective-permute-start.2 = (bf16[32,11552]{1,0:T(8,128)(2,1)}, bf16[32,11552]{1,0:T(8,128)(2,1)}, u32[]{:S(2)}, u32[]{:S(2)}) collective-permute-start(bf16[32,11552]{1,0:T(8,128)(2,1)} %get-tuple-element.115), channel_id=1, source_target_pairs={{0,16},{1,17},{2,18},{3,19},{4,20},{5,21},{6,22},{7,23},{8,24},{9,... | collective-permute-start | bytes 2217992 | tf_op jit(solution)/shard_map/ppermute | solution.py:175
  52.3 24.0 %collective-permute-start.3 = (bf16[32,11552]{1,0:T(8,128)(2,1)}, bf16[32,11552]{1,0:T(8,128)(2,1)}, u32[]{:S(2)}, u32[]{:S(2)}) collective-permute-start(bf16[32,11552]{1,0:T(8,128)(2,1)} %get-tuple-element.113), channel_id=1, source_target_pairs={{0,1},{1,0},{2,3},{3,2},{4,5},{5,4},{6,7},{7,6},{8,9},{9,8},{10,11... | collective-permute-start | bytes 2217992 | tf_op jit(solution)/shard_map/ppermute | solution.py:175
  56.1 22.3 %collective-permute-start.4 = (bf16[64,11552]{1,0:T(8,128)(2,1)}, bf16[64,11552]{1,0:T(8,128)(2,1)S(1)}, u32[]{:S(2)}, u32[]{:S(2)}) collective-permute-start(bf16[64,11552]{1,0:T(8,128)(2,1)} %pad_dynamic-slice_fusion), channel_id=1, source_target_pairs={{0,8},{1,9},{2,10},{3,11},{4,12},{5,13},{6,14},{7,15},{8,0},{9,1},... | collective-permute-start | bytes 4435976 | tf_op jit(solution)/shard_map/ppermute | solution.py:175
  78.4 2.4 %copy-start.2 = (bf16[3,3,32,256]{3,2,1,0:T(8,128)(2,1)S(1)}, bf16[3,3,32,256]{3,2,1,0:T(8,128)(2,1)}, u32[]{:S(2)}) copy-start(bf16[3,3,32,256]{3,2,1,0:T(8,128)(2,1)} %param.19) | copy-start | bytes 442372
  78.4 2.4 %copy-start.4 = (bf16[256,8]{0,1:T(8,128)(2,1)S(1)}, bf16[256,8]{0,1:T(8,128)(2,1)}, u32[]{:S(2)}) copy-start(bf16[256,8]{0,1:T(8,128)(2,1)} %param.22) | copy-start | bytes 12292
  78.4 2.4 %copy-start.5 = (bf16[256,8]{0,1:T(8,128)(2,1)S(1)}, bf16[256,8]{0,1:T(8,128)(2,1)}, u32[]{:S(2)}) copy-start(bf16[256,8]{0,1:T(8,128)(2,1)} %param.23) | copy-start | bytes 12292
  78.4 2.4 %copy-start.11 = (bf16[256]{0:T(256)(128)(2,1)S(1)}, bf16[256]{0:T(256)(128)(2,1)}, u32[]{:S(2)}) copy-start(bf16[256]{0:T(256)(128)(2,1)} %param.24) | copy-start | bytes 1540
  91.2 8.2 %copy-start.9 = (bf16[1,3,3,256,256]{4,3,2,1,0:T(8,128)(2,1)S(1)}, bf16[1,3,3,256,256]{4,3,2,1,0:T(8,128)(2,1)}, u32[]{:S(2)}) copy-start(bf16[1,3,3,256,256]{4,3,2,1,0:T(8,128)(2,1)} %get-tuple-element.242) | copy-start | bytes 3538948 | tf_op jit(solution)/shard_map/while
  99.4 18.4 %copy-start.10 = (bf16[1,3,3,256,256]{4,3,2,1,0:T(8,128)(2,1)S(1)}, bf16[1,3,3,256,256]{4,3,2,1,0:T(8,128)(2,1)}, u32[]{:S(2)}) copy-start(bf16[1,3,3,256,256]{4,3,2,1,0:T(8,128)(2,1)} %get-tuple-element.243) | copy-start | bytes 3538948 | tf_op jit(solution)/shard_map/while
  147.2 1.7 copy-start
  148.9 7.5 %collective-permute-start.5 = (bf16[16,2944]{1,0:T(8,128)(2,1)S(1)}, bf16[16,2944]{1,0:T(8,128)(2,1)S(1)}, u32[]{:S(2)}, u32[]{:S(2)}) collective-permute-start(bf16[16,2944]{1,0:T(8,128)(2,1)S(1)} %constant_dynamic-slice_fusion.4), channel_id=1, source_target_pairs={{0,4},{1,5},{2,6},{3,7},{4,0},{5,1},{6,2},{7,3},{8,12},{9,13},{10,... | collective-permute-start | bytes 282632 | tf_op jit(solution)/shard_map/ppermute | solution.py:206
  152.3 6.4 %collective-permute-start.6 = (bf16[32,2944]{1,0:T(8,128)(2,1)S(1)}, bf16[32,2944]{1,0:T(8,128)(2,1)S(1)}, u32[]{:S(2)}, u32[]{:S(2)}) collective-permute-start(bf16[32,2944]{1,0:T(8,128)(2,1)S(1)} %get-tuple-element.118), channel_id=1, source_target_pairs={{0,2},{1,3},{2,0},{3,1},{4,6},{5,7},{6,4},{7,5},{8,10},{9,11},{10,... | collective-permute-start | bytes 565256 | tf_op jit(solution)/shard_map/ppermute | solution.py:206
  153.2 5.6 %collective-permute-start.7 = (bf16[32,2944]{1,0:T(8,128)(2,1)S(1)}, bf16[32,2944]{1,0:T(8,128)(2,1)S(1)}, u32[]{:S(2)}, u32[]{:S(2)}) collective-permute-start(bf16[32,2944]{1,0:T(8,128)(2,1)S(1)} %get-tuple-element.117), channel_id=1, source_target_pairs={{0,16},{1,17},{2,18},{3,19},{4,20},{5,21},{6,22},{7,23},{8,24},{9,... | collective-permute-start | bytes 565256 | tf_op jit(solution)/shard_map/ppermute | solution.py:206
  154.8 5.6 %collective-permute-start.8 = (bf16[32,2944]{1,0:T(8,128)(2,1)S(1)}, bf16[32,2944]{1,0:T(8,128)(2,1)S(1)}, u32[]{:S(2)}, u32[]{:S(2)}) collective-permute-start(bf16[32,2944]{1,0:T(8,128)(2,1)S(1)} %get-tuple-element.116), channel_id=1, source_target_pairs={{0,1},{1,0},{2,3},{3,2},{4,5},{5,4},{6,7},{7,6},{8,9},{9,8},{10,11... | collective-permute-start | bytes 565256 | tf_op jit(solution)/shard_map/ppermute | solution.py:206
  156.3 4.0 %collective-permute-start.9 = (bf16[64,2944]{1,0:T(8,128)(2,1)S(1)}, bf16[64,2944]{1,0:T(8,128)(2,1)S(1)}, u32[]{:S(2)}, u32[]{:S(2)}) collective-permute-start(bf16[64,2944]{1,0:T(8,128)(2,1)S(1)} %constant_dynamic-slice_fusion), channel_id=1, source_target_pairs={{0,8},{1,9},{2,10},{3,11},{4,12},{5,13},{6,14},{7,15},{8,0},{9,1},... | collective-permute-start | bytes 1130504 | tf_op jit(solution)/shard_map/ppermute | solution.py:206
  161.6 2.5 %copy-start.1 = (pred[128,8,361]{0,1,2:T(8,128)(4,1)S(1)}, pred[128,8,361]{0,1,2:T(8,128)(4,1)}, u32[]{:S(2)}) copy-start(pred[128,8,361]{0,1,2:T(8,128)(4,1)} %broadcast_compare_fusion) | copy-start | bytes 1108996
  161.6 2.5 %copy-start.7 = (f32[8]{0:T(128)S(1)}, f32[8]{0:T(128)}, u32[]{:S(2)}) copy-start(f32[8]{0:T(128)} %param.25) | copy-start | bytes 100
  164.1 1.4 copy-start.6
  164.1 1.4 copy-start.12
  164.1 6.8 %copy-start.8 = (pred[128]{0:T(512)(128)(4,1)S(1)}, pred[128]{0:T(512)(128)(4,1)}, u32[]{:S(2)}) copy-start(pred[128]{0:T(512)(128)(4,1)} %iota_compare_fusion.1) | copy-start | bytes 388
  167.2 10.8 %all-to-all-start.1 = ((f32[32,1,8]{2,1,0:T(1,128)}), f32[32,1,8]{2,1,0:T(1,128)S(1)}, u32[]{:S(2)}, u32[]{:S(2)}) async-start(f32[32,1,8]{2,1,0:T(1,128)} %convolution_bitcast_fusion.1), calls=%async_computation.1 | async-start | bytes 32768 | tf_op jit(solution)/shard_map/all_to_all | solution.py:227

commit v6 on v5

--- a/solution.py
+++ b/solution.py
@@ -67,23 +67,25 @@
     lanes = counts_all.shape[1]
     lane = lax.broadcasted_iota(jnp.int32, counts_all.shape, 1)
 
+    takes_up = {m: pltpu.roll(lane, m, 1) == (lane ^ m) for m in masks}
+
     def swap(x, mask):
-        up = pltpu.roll(x, mask, 1)
-        up_from = pltpu.roll(lane, mask, 1)
-        down = pltpu.roll(x, lanes - mask, 1)
-        return jnp.where(up_from == (lane ^ mask), up, down)
+        return jnp.where(takes_up[mask], pltpu.roll(x, mask, 1), pltpu.roll(x, lanes - mask, 1))
 
     flows = [jnp.zeros_like(counts_all) for _ in masks]
+    sent = jnp.zeros_like(counts_all)
+    got = jnp.zeros_like(counts_all)
     for _ in range(PASSES):
         for e, (mask, cap) in enumerate(zip(masks, caps)):
-            sent = sum(flows)
-            got = sum(swap(f, m) for f, m in zip(flows, masks))
             load = counts_all - sent + got
             own = counts_all - sent
             move = jnp.right_shift(jnp.maximum(load - swap(load, mask), 0), 1)
             cancel = jnp.minimum(move, swap(flows[e], mask))
             add = jnp.clip(move - cancel, 0, jnp.minimum(cap - flows[e], own))
-            flows[e] = flows[e] + add - swap(cancel, mask)
+            cancelled = swap(cancel, mask)
+            flows[e] = flows[e] + add - cancelled
+            sent = sent + add - cancelled
+            got = got + swap(add, mask) - cancel
     into = [swap(f, m) for f, m in zip(flows, masks)]
     keep = counts_all - sum(flows)
     starts, places = [], []

time: 180 us -> 178 us (0.989)
  no operation moved by 1% of the time
where the time goes in v6:
time: 178 us; the launch traced here: 177 us
  matrix products  55.5 us (31%)
  local copies, waits for them, and re-layouts  41.5 us (23%)
  starting transfers between devices  25.4 us (14%)
  between operations  21.3 us (12%)
  waiting for transfers between devices  18.9 us (11%)
  other arithmetic  8.98 us (5%)
  Pallas kernels  5.07 us (3%)
    conv_general_dilated x3, matrix products, convolve(): lax.conv_general_dilated(inputs, kernel, (1, 1), 'SAME', dimension_number...  46.4 us
    unnamed x34, local copies, waits for them, and re-layouts  15.2 us
    ppermute x5, waiting for transfers between devices, body(): lax.ppermute(lax.dynamic_slice(padded, (starts[e], 0), (cap, row)), AXES,...  10.2 us
    all_to_all x1, starting transfers between devices, body(): lax.all_to_all(jnp.broadcast_to(counts, (groups, 1)), AXES, 0, 0, tiled=T...  7.33 us
    ppermute x5, starting transfers between devices, body(): lax.ppermute(lax.dynamic_slice(results, (places[e], 0), (cap, width)), AX...  7.23 us
    dot_general x1, matrix products, evaluate(): jnp.einsum('bhwc,cf->bfhw', hidden, policy_weight, preferred_element_type...  7.22 us
    ppermute x5, starting transfers between devices, body(): lax.ppermute(lax.dynamic_slice(padded, (starts[e], 0), (cap, row)), AXES,...  7.16 us
    gather x1, local copies, waits for them, and re-layouts, step(): rows = jnp.take(pool, idx, axis=0, mode='clip', indices_are_sorted=True)  6.81 us
  transfers between devices with their start and end apart: 12, of which 5 were waited for; matrix products, arithmetic and copies ran while one was open for 12% of the time, Pallas kernels for 0%

profile of v6, /device:TPU:0, one launch (start us, length us, event | category | flops | bytes accessed | tf_op | source)
XLA Modules:
  0.0 176.9 jit_solution(11509083515676758318)
XLA Ops:
  1.3 0.6 broadcast_in_dim.58
  1.9 7.3 %all-to-all-start = ((s32[32,1,1]{2,1,0:T(1,128)}), s32[32,1,1]{2,1,0:T(1,128)S(1)}, u32[]{:S(2)}, u32[]{:S(2)}) async-start(s32[32,1,1]{2,1,0:T(1,128)} %broadcast_in_dim.58), calls=%async_computation | async-start | bytes 32768 | tf_op jit(solution)/shard_map/all_to_all | solution.py:156
  9.2 0.6 multiply_add_fusion
  9.8 3.4 %copy.51 = bf16[128,11552]{1,0:T(8,128)(2,1)S(1)} copy(bf16[128,11552]{0,1:T(8,128)(2,1)} %param.15) | data formatting | bytes 5914624 | tf_op args[0]
  13.2 1.8 %constant_dynamic-update-slice_fusion.6 = bf16[304,11552]{1,0:T(8,128)(2,1)} fusion(bf16[128,11552]{1,0:T(8,128)(2,1)S(1)} %copy.51), kind=kLoop, calls=%fused_computation.50 | loop fusion | bytes 5939200
  15.1 1.0 broadcast_compare_fusion
  16.1 0.5 iota_compare_fusion.1
  16.6 0.6 compare_reduce_fusion
  17.3 1.3 fusion.18
  18.6 0.5 scatter.4.counts_ref
  19.1 0.5 broadcast_in_dim.59.me_ref
  19.6 5.1 %shard_map.130 = (s32[24,128]{1,0:T(8,128)}, s32[8,256]{1,0:T(8,128)}) custom-call(s32[1,128]{1,0:T(1,128)} %scatter.4.counts_ref, s32[1,128]{1,0:T(1,128)} %broadcast_in_dim.59.me_ref), custom_call_target="tpu_custom_call" | custom-call | tf_op jit(solution)/shard_map/pallas_call | solution.py:127
  24.7 1.6 fusion.20
  41.5 1.9 %pad_dynamic-slice_fusion.1 = (bf16[32,11552]{1,0:T(8,128)(2,1)}, bf16[32,11552]{1,0:T(8,128)(2,1)}, bf16[32,11552]{1,0:T(8,128)(2,1)}) fusion(s32[]{:T(128)S(6)} %select_n.69, bf16[128,11552]{1,0:T(8,128)(2,1)S(1)} %copy.51, s32[]{:T(128)S(6)} %select_n.67, s32[]{:T(128)S(6)} %select_n.68), kind=kLoop, calls=%fused_computation.26 | loop fusion | bytes 5175308 | tf_op jit(solution)/shard_map/dynamic_slice | solution.py:177
  43.4 1.8 %collective-permute-start.1 = (bf16[32,11552]{1,0:T(8,128)(2,1)}, bf16[32,11552]{1,0:T(8,128)(2,1)}, u32[]{:S(2)}, u32[]{:S(2)}) collective-permute-start(bf16[32,11552]{1,0:T(8,128)(2,1)} %get-tuple-element.114), channel_id=1, source_target_pairs={{0,2},{1,3},{2,0},{3,1},{4,6},{5,7},{6,4},{7,5},{8,10},{9,11},{10,... | collective-permute-start | bytes 2217992 | tf_op jit(solution)/shard_map/ppermute | solution.py:177
  45.8 0.9 pad_dynamic-slice_fusion.4
  46.7 2.4 %collective-permute-start = (bf16[16,11552]{1,0:T(8,128)(2,1)}, bf16[16,11552]{1,0:T(8,128)(2,1)S(1)}, u32[]{:S(2)}, u32[]{:S(2)}) collective-permute-start(bf16[16,11552]{1,0:T(8,128)(2,1)} %pad_dynamic-slice_fusion.4), channel_id=1, source_target_pairs={{0,4},{1,5},{2,6},{3,7},{4,0},{5,1},{6,2},{7,3},{8,12},{9,13},{10,... | collective-permute-start | bytes 1109000 | tf_op jit(solution)/shard_map/ppermute | solution.py:177
  49.2 1.5 collective-permute-start.2
  50.6 1.5 collective-permute-start.3
  52.8 1.6 pad_dynamic-slice_fusion
  54.4 0.7 slice.73
  58.3 0.7 slice_bitcast_fusion
  59.0 0.6 pad_clamp_fusion.1
  59.6 10.1 %collective-permute-done = bf16[16,11552]{1,0:T(8,128)(2,1)S(1)} collective-permute-done((bf16[16,11552]{1,0:T(8,128)(2,1)}, bf16[16,11552]{1,0:T(8,128)(2,1)S(1)}, u32[]{:S(2)}, u32[]{:S(2)}) %collective-permute-start) | collective-permute-done | bytes 369696 | tf_op jit(solution)/shard_map/ppermute | solution.py:177
  69.7 0.8 constant_dynamic-update-slice_fusion.5
  70.5 2.1 %constant_dynamic-update-slice_fusion.4 = bf16[304,11552]{1,0:T(8,128)(2,1)} fusion(bf16[304,11552]{1,0:T(8,128)(2,1)} %constant_dynamic-update-slice_fusion.5, bf16[32,11552]{1,0:T(8,128)(2,1)} %collective-permute-done.1), kind=kLoop, calls=%fused_computation.48 | loop fusion | bytes 1490944
  72.6 2.0 %constant_dynamic-update-slice_fusion.3 = bf16[304,11552]{1,0:T(8,128)(2,1)} fusion(bf16[304,11552]{1,0:T(8,128)(2,1)} %constant_dynamic-update-slice_fusion.4, bf16[32,11552]{1,0:T(8,128)(2,1)} %collective-permute-done.2), kind=kLoop, calls=%fused_computation.47 | loop fusion | bytes 1490944
  74.6 2.1 %constant_dynamic-update-slice_fusion.2 = bf16[304,11552]{1,0:T(8,128)(2,1)} fusion(bf16[304,11552]{1,0:T(8,128)(2,1)} %constant_dynamic-update-slice_fusion.3, bf16[32,11552]{1,0:T(8,128)(2,1)} %collective-permute-done.3), kind=kLoop, calls=%fused_computation.46 | loop fusion | bytes 1490944
  76.7 1.2 constant_dynamic-update-slice_fusion.1
  77.9 1.1 broadcast_in_dim.57
  79.1 66.4 %while.11 = (s32[]{:T(128)}, bf16[224,2944]{1,0:T(8,128)(2,1)}, s32[]{:T(128)}, s32[160]{0:T(256)S(1)}, bf16[304,11552]{1,0:T(8,128)(2,1)}, /*index=5*/bf16[3,3,...) while((s32[]{:T(128)}, bf16[224,2944]{1,0:T(8,128)(2,1)}, ...), condition=%wide.region_3.4_spmd, body=%wide.region_1.3_spmd.sunk | while | flops 33799694336 | bytes 71023168 | solution.py:200
  79.4 6.8 %gather_fusion = bf16[40,11552]{1,0:T(8,128)(2,1)} fusion(bf16[304,11552]{1,0:T(8,128)(2,1)} %get-tuple-element.240, s32[1024]{0:T(1024)S(1)} %pad_clamp_fusion.3), kind=kCustom, calls=%fused_computation.clone.1 | custom fusion | bytes 1848480 | tf_op jit(solution)/shard_map/while/body/jit(_take)/gather | solution.py:188
  86.2 3.3 %copy.71 = bf16[40,11552]{0,1:T(8,128)(2,1)S(1)} copy(bf16[40,11552]{1,0:T(8,128)(2,1)} %gather_fusion) | data formatting | bytes 1848320 | tf_op jit(solution)/shard_map/while/body/reshape | solution.py:37
  89.5 8.2 %maximum_convert_fusion.5 = bf16[40,19,19,256]{3,0,2,1:T(8,128)(2,1)S(1)} fusion(bf16[40,19,19,32]{0,3,2,1:T(8,128)(2,1)S(1)} %bitcast.97, bf16[3,3,32,256]{3,2,1,0:T(8,128)(2,1)S(1)} %get-tuple-element.241), kind=kOutput, calls=%fused_computation.5.clone.1 | convolution fusion | flops 1989857280 | bytes 8464896 | tf_op jit(solution)/shard_map/while/body/conv_general_dilated | solution.py:25
  97.7 18.4 %maximum_convert_fusion.6 = bf16[40,19,19,256]{3,0,2,1:T(8,128)(2,1)S(1)} fusion(bf16[40,19,19,256]{3,0,2,1:T(8,128)(2,1)S(1)} %maximum_convert_fusion.5, bf16[1,3,3,256,256]{4,3,2,1,0:T(8,128)(2,1)S(1)} %copy-done.9), kind=kOutput, calls=%fused_computation.4.clone.1 | convolution fusion | flops 15867105280 | bytes 15966208 | tf_op jit(solution)/shard_map/while/body/conv_general_dilated | solution.py:25
  116.1 19.9 %convert_reduce_fusion.3 = (f32[40,256]{1,0:T(8,128)S(1)}, bf16[40,19,19,256]{3,0,2,1:T(8,128)(2,1)}) fusion(bf16[40,19,19,256]{3,0,2,1:T(8,128)(2,1)S(1)} %maximum_convert_fusion.6, bf16[1,3,3,256,256]{4,3,2,1,0:T(8,128)(2,1)S(1)} %copy-done.10, bf16[40,19,19,256]{3,0,2,1:T(8,128)(2,1)S(1)} %maximum_convert_fusion.5), kind=kOutput, calls=%fused_computation.2.clone.1 | convolution fusion | flops 15881881600 | bytes 23400448 | tf_op jit(solution)/shard_map/while/body/conv_general_dilated | solution.py:25
  136.0 0.1 fusion.52
  136.1 0.2 copy.72
  136.3 7.2 %convolution_convert_fusion.3 = bf16[40,19,19,8]{0,3,2,1:T(8,128)(2,1)S(1)} fusion(bf16[40,19,19,256]{3,0,2,1:T(8,128)(2,1)} %get-tuple-element.201, bf16[256,8]{0,1:T(8,128)(2,1)S(1)} %get-tuple-element.244), kind=kOutput, calls=%fused_computation.6.clone.1 | convolution fusion | flops 59261760 | bytes 7628416 | tf_op jit(solution)/shard_map/while/body/bhwc,cf->bfhw/dot_general | solution.py:43
  143.5 0.6 copy.73
  144.2 0.2 convert_element_type.69
  144.4 0.1 fusion.53
  144.8 0.7 constant_dynamic-update-slice_fusion.14
  145.5 1.5 constant_dynamic-update-slice_fusion.12
  147.0 0.2 copy-done
  147.2 3.3 %collective-permute-start.5 = (bf16[16,2944]{1,0:T(8,128)(2,1)S(1)}, bf16[16,2944]{1,0:T(8,128)(2,1)S(1)}, u32[]{:S(2)}, u32[]{:S(2)}) collective-permute-start(bf16[16,2944]{1,0:T(8,128)(2,1)S(1)} %constant_dynamic-slice_fusion.4), channel_id=1, source_target_pairs={{0,4},{1,5},{2,6},{3,7},{4,0},{5,1},{6,2},{7,3},{8,12},{9,13},{10,... | collective-permute-start | bytes 282632 | tf_op jit(solution)/shard_map/ppermute | solution.py:208
  150.5 0.1 constant_dynamic-slice_fusion.1
  150.6 0.9 collective-permute-start.6
  151.6 1.5 collective-permute-start.7
  153.1 1.5 collective-permute-start.8
  154.8 2.3 %collective-permute-done.6 = bf16[32,2944]{1,0:T(8,128)(2,1)S(1)} collective-permute-done((bf16[32,2944]{1,0:T(8,128)(2,1)S(1)}, bf16[32,2944]{1,0:T(8,128)(2,1)S(1)}, u32[]{:S(2)}, u32[]{:S(2)}) %collective-permute-start.6) | collective-permute-done | bytes 188448 | tf_op jit(solution)/shard_map/ppermute | solution.py:208
  157.2 1.5 collective-permute-done.8
  158.7 1.2 gather_fusion.1
  159.9 1.2 copy.57
  161.1 1.3 reshape.142
  162.4 0.6 select_reduce_fusion
  163.0 0.6 fusion.13
  163.6 0.2 fusion.15
  163.8 1.7 convolution_bitcast_fusion.1
  165.5 3.7 %all-to-all-start.1 = ((f32[32,1,8]{2,1,0:T(1,128)}), f32[32,1,8]{2,1,0:T(1,128)S(1)}, u32[]{:S(2)}, u32[]{:S(2)}) async-start(f32[32,1,8]{2,1,0:T(1,128)} %convolution_bitcast_fusion.1), calls=%async_computation.1 | async-start | bytes 32768 | tf_op jit(solution)/shard_map/all_to_all | solution.py:229
  169.2 1.8 %divide_select_fusion = f32[128,8,362]{0,1,2:T(8,128)} fusion(f32[128,8,362]{0,2,1:T(8,128)S(1)} %reshape.142, pred[128,8,361]{0,1,2:T(8,128)(4,1)S(1)} %copy-done.1, f32[128,8]{0,1:T(8,128)S(1)} %fusion.13, f32[128,8]{0,1:T(8,128)S(1)} %select_reduce_fusion, f32[8]{0:T(128)S(1)} %copy-done.7, pred[128]{0:T(512)(128)(4,1)S(1)} %copy-done.8), kind=kLoop, calls=%fused_computation.31 | loop fusion | flops 1853440 | bytes 3343520 | tf_op jit(solution)/shard_map/jit(_where)/select_n | solution.py:220
  171.0 0.5 broadcast_select_fusion.1
  171.5 4.8 %all-to-all-done.1 = f32[32,1,8]{2,1,0:T(1,128)S(1)} async-done(((f32[32,1,8]{2,1,0:T(1,128)}), f32[32,1,8]{2,1,0:T(1,128)S(1)}, u32[]{:S(2)}, u32[]{:S(2)}) %all-to-all-start.1) | async-done | bytes 1056 | tf_op jit(solution)/shard_map/all_to_all | solution.py:229
  176.3 0.6 reduce_sum.28
  (49 shorter events, 1.0 us)
Async XLA Ops:
  1.9 15.4 %all-to-all-start = ((s32[32,1,1]{2,1,0:T(1,128)}), s32[32,1,1]{2,1,0:T(1,128)S(1)}, u32[]{:S(2)}, u32[]{:S(2)}) async-start(s32[32,1,1]{2,1,0:T(1,128)} %broadcast_in_dim.58), calls=%async_computation | async-start | bytes 32768 | tf_op jit(solution)/shard_map/all_to_all | solution.py:156
  13.2 1.9 %copy-start.3 = (s32[128,8,361]{0,1,2:T(8,128)S(1)}, s32[128,8,361]{0,1,2:T(8,128)}, u32[]{:S(2)}) copy-start(s32[128,8,361]{0,1,2:T(8,128)} %param.18) | copy-start | bytes 4435972
  43.4 27.1 %collective-permute-start.1 = (bf16[32,11552]{1,0:T(8,128)(2,1)}, bf16[32,11552]{1,0:T(8,128)(2,1)}, u32[]{:S(2)}, u32[]{:S(2)}) collective-permute-start(bf16[32,11552]{1,0:T(8,128)(2,1)} %get-tuple-element.114), channel_id=1, source_target_pairs={{0,2},{1,3},{2,0},{3,1},{4,6},{5,7},{6,4},{7,5},{8,10},{9,11},{10,... | collective-permute-start | bytes 2217992 | tf_op jit(solution)/shard_map/ppermute | solution.py:177
  46.7 22.9 %collective-permute-start = (bf16[16,11552]{1,0:T(8,128)(2,1)}, bf16[16,11552]{1,0:T(8,128)(2,1)S(1)}, u32[]{:S(2)}, u32[]{:S(2)}) collective-permute-start(bf16[16,11552]{1,0:T(8,128)(2,1)} %pad_dynamic-slice_fusion.4), channel_id=1, source_target_pairs={{0,4},{1,5},{2,6},{3,7},{4,0},{5,1},{6,2},{7,3},{8,12},{9,13},{10,... | collective-permute-start | bytes 1109000 | tf_op jit(solution)/shard_map/ppermute | solution.py:177
  49.2 23.4 %collective-permute-start.2 = (bf16[32,11552]{1,0:T(8,128)(2,1)}, bf16[32,11552]{1,0:T(8,128)(2,1)}, u32[]{:S(2)}, u32[]{:S(2)}) collective-permute-start(bf16[32,11552]{1,0:T(8,128)(2,1)} %get-tuple-element.115), channel_id=1, source_target_pairs={{0,16},{1,17},{2,18},{3,19},{4,20},{5,21},{6,22},{7,23},{8,24},{9,... | collective-permute-start | bytes 2217992 | tf_op jit(solution)/shard_map/ppermute | solution.py:177
  50.6 24.0 %collective-permute-start.3 = (bf16[32,11552]{1,0:T(8,128)(2,1)}, bf16[32,11552]{1,0:T(8,128)(2,1)}, u32[]{:S(2)}, u32[]{:S(2)}) collective-permute-start(bf16[32,11552]{1,0:T(8,128)(2,1)} %get-tuple-element.113), channel_id=1, source_target_pairs={{0,1},{1,0},{2,3},{3,2},{4,5},{5,4},{6,7},{7,6},{8,9},{9,8},{10,11... | collective-permute-start | bytes 2217992 | tf_op jit(solution)/shard_map/ppermute | solution.py:177
  54.4 22.3 %collective-permute-start.4 = (bf16[64,11552]{1,0:T(8,128)(2,1)}, bf16[64,11552]{1,0:T(8,128)(2,1)S(1)}, u32[]{:S(2)}, u32[]{:S(2)}) collective-permute-start(bf16[64,11552]{1,0:T(8,128)(2,1)} %pad_dynamic-slice_fusion), channel_id=1, source_target_pairs={{0,8},{1,9},{2,10},{3,11},{4,12},{5,13},{6,14},{7,15},{8,0},{9,1},... | collective-permute-start | bytes 4435976 | tf_op jit(solution)/shard_map/ppermute | solution.py:177
  76.7 2.4 %copy-start.2 = (bf16[3,3,32,256]{3,2,1,0:T(8,128)(2,1)S(1)}, bf16[3,3,32,256]{3,2,1,0:T(8,128)(2,1)}, u32[]{:S(2)}) copy-start(bf16[3,3,32,256]{3,2,1,0:T(8,128)(2,1)} %param.19) | copy-start | bytes 442372
  76.7 2.4 %copy-start.4 = (bf16[256,8]{0,1:T(8,128)(2,1)S(1)}, bf16[256,8]{0,1:T(8,128)(2,1)}, u32[]{:S(2)}) copy-start(bf16[256,8]{0,1:T(8,128)(2,1)} %param.22) | copy-start | bytes 12292
  76.7 2.4 %copy-start.5 = (bf16[256,8]{0,1:T(8,128)(2,1)S(1)}, bf16[256,8]{0,1:T(8,128)(2,1)}, u32[]{:S(2)}) copy-start(bf16[256,8]{0,1:T(8,128)(2,1)} %param.23) | copy-start | bytes 12292
  76.7 2.4 %copy-start.11 = (bf16[256]{0:T(256)(128)(2,1)S(1)}, bf16[256]{0:T(256)(128)(2,1)}, u32[]{:S(2)}) copy-start(bf16[256]{0:T(256)(128)(2,1)} %param.24) | copy-start | bytes 1540
  89.5 8.2 %copy-start.9 = (bf16[1,3,3,256,256]{4,3,2,1,0:T(8,128)(2,1)S(1)}, bf16[1,3,3,256,256]{4,3,2,1,0:T(8,128)(2,1)}, u32[]{:S(2)}) copy-start(bf16[1,3,3,256,256]{4,3,2,1,0:T(8,128)(2,1)} %get-tuple-element.242) | copy-start | bytes 3538948 | tf_op jit(solution)/shard_map/while
  97.7 18.4 %copy-start.10 = (bf16[1,3,3,256,256]{4,3,2,1,0:T(8,128)(2,1)S(1)}, bf16[1,3,3,256,256]{4,3,2,1,0:T(8,128)(2,1)}, u32[]{:S(2)}) copy-start(bf16[1,3,3,256,256]{4,3,2,1,0:T(8,128)(2,1)} %get-tuple-element.243) | copy-start | bytes 3538948 | tf_op jit(solution)/shard_map/while
  145.5 1.7 copy-start
  147.2 7.5 %collective-permute-start.5 = (bf16[16,2944]{1,0:T(8,128)(2,1)S(1)}, bf16[16,2944]{1,0:T(8,128)(2,1)S(1)}, u32[]{:S(2)}, u32[]{:S(2)}) collective-permute-start(bf16[16,2944]{1,0:T(8,128)(2,1)S(1)} %constant_dynamic-slice_fusion.4), channel_id=1, source_target_pairs={{0,4},{1,5},{2,6},{3,7},{4,0},{5,1},{6,2},{7,3},{8,12},{9,13},{10,... | collective-permute-start | bytes 282632 | tf_op jit(solution)/shard_map/ppermute | solution.py:208
  150.6 6.4 %collective-permute-start.6 = (bf16[32,2944]{1,0:T(8,128)(2,1)S(1)}, bf16[32,2944]{1,0:T(8,128)(2,1)S(1)}, u32[]{:S(2)}, u32[]{:S(2)}) collective-permute-start(bf16[32,2944]{1,0:T(8,128)(2,1)S(1)} %get-tuple-element.118), channel_id=1, source_target_pairs={{0,2},{1,3},{2,0},{3,1},{4,6},{5,7},{6,4},{7,5},{8,10},{9,11},{10,... | collective-permute-start | bytes 565256 | tf_op jit(solution)/shard_map/ppermute | solution.py:208
  151.6 5.6 %collective-permute-start.7 = (bf16[32,2944]{1,0:T(8,128)(2,1)S(1)}, bf16[32,2944]{1,0:T(8,128)(2,1)S(1)}, u32[]{:S(2)}, u32[]{:S(2)}) collective-permute-start(bf16[32,2944]{1,0:T(8,128)(2,1)S(1)} %get-tuple-element.117), channel_id=1, source_target_pairs={{0,16},{1,17},{2,18},{3,19},{4,20},{5,21},{6,22},{7,23},{8,24},{9,... | collective-permute-start | bytes 565256 | tf_op jit(solution)/shard_map/ppermute | solution.py:208
  153.1 5.6 %collective-permute-start.8 = (bf16[32,2944]{1,0:T(8,128)(2,1)S(1)}, bf16[32,2944]{1,0:T(8,128)(2,1)S(1)}, u32[]{:S(2)}, u32[]{:S(2)}) collective-permute-start(bf16[32,2944]{1,0:T(8,128)(2,1)S(1)} %get-tuple-element.116), channel_id=1, source_target_pairs={{0,1},{1,0},{2,3},{3,2},{4,5},{5,4},{6,7},{7,6},{8,9},{9,8},{10,11... | collective-permute-start | bytes 565256 | tf_op jit(solution)/shard_map/ppermute | solution.py:208
  154.6 4.0 %collective-permute-start.9 = (bf16[64,2944]{1,0:T(8,128)(2,1)S(1)}, bf16[64,2944]{1,0:T(8,128)(2,1)S(1)}, u32[]{:S(2)}, u32[]{:S(2)}) collective-permute-start(bf16[64,2944]{1,0:T(8,128)(2,1)S(1)} %constant_dynamic-slice_fusion), channel_id=1, source_target_pairs={{0,8},{1,9},{2,10},{3,11},{4,12},{5,13},{6,14},{7,15},{8,0},{9,1},... | collective-permute-start | bytes 1130504 | tf_op jit(solution)/shard_map/ppermute | solution.py:208
  159.9 2.5 %copy-start.1 = (pred[128,8,361]{0,1,2:T(8,128)(4,1)S(1)}, pred[128,8,361]{0,1,2:T(8,128)(4,1)}, u32[]{:S(2)}) copy-start(pred[128,8,361]{0,1,2:T(8,128)(4,1)} %broadcast_compare_fusion) | copy-start | bytes 1108996
  159.9 2.5 %copy-start.7 = (f32[8]{0:T(128)S(1)}, f32[8]{0:T(128)}, u32[]{:S(2)}) copy-start(f32[8]{0:T(128)} %param.25) | copy-start | bytes 100
  162.4 1.4 copy-start.6
  162.4 1.4 copy-start.12
  162.4 6.8 %copy-start.8 = (pred[128]{0:T(512)(128)(4,1)S(1)}, pred[128]{0:T(512)(128)(4,1)}, u32[]{:S(2)}) copy-start(pred[128]{0:T(512)(128)(4,1)} %iota_compare_fusion.1) | copy-start | bytes 388
  165.5 10.8 %all-to-all-start.1 = ((f32[32,1,8]{2,1,0:T(1,128)}), f32[32,1,8]{2,1,0:T(1,128)S(1)}, u32[]{:S(2)}, u32[]{:S(2)}) async-start(f32[32,1,8]{2,1,0:T(1,128)} %convolution_bitcast_fusion.1), calls=%async_computation.1 | async-start | bytes 32768 | tf_op jit(solution)/shard_map/all_to_all | solution.py:229

commit v7 on v6

--- a/solution.py
+++ b/solution.py
@@ -16,7 +16,7 @@
 AXES = ("search", "net")
 CHUNK = 40
 PASSES = 5
-CORE_CAP = 64
+CORE_CAP = 48
 LINK_CAP = 32
 FAR_CAP = 16
 

time: 178 us -> 177 us (level)
  no operation moved by 1% of the time
where the time goes in v7:
time: 177 us; the launch traced here: 176 us
  matrix products  55.5 us (31%)
  local copies, waits for them, and re-layouts  40.9 us (23%)
  starting transfers between devices  25.4 us (14%)
  between operations  21.1 us (12%)
  waiting for transfers between devices  19.2 us (11%)
  other arithmetic  9.04 us (5%)
  Pallas kernels  5.11 us (3%)
    conv_general_dilated x3, matrix products, convolve(): lax.conv_general_dilated(inputs, kernel, (1, 1), 'SAME', dimension_number...  46.4 us
    unnamed x34, local copies, waits for them, and re-layouts  15.2 us
    ppermute x5, waiting for transfers between devices, body(): lax.ppermute(lax.dynamic_slice(padded, (starts[e], 0), (cap, row)), AXES,...  10.5 us
    all_to_all x1, starting transfers between devices, body(): lax.all_to_all(jnp.broadcast_to(counts, (groups, 1)), AXES, 0, 0, tiled=T...  7.33 us
    ppermute x5, starting transfers between devices, body(): lax.ppermute(lax.dynamic_slice(results, (places[e], 0), (cap, width)), AX...  7.25 us
    dot_general x1, matrix products, evaluate(): jnp.einsum('bhwc,cf->bfhw', hidden, policy_weight, preferred_element_type...  7.22 us
    ppermute x5, starting transfers between devices, body(): lax.ppermute(lax.dynamic_slice(padded, (starts[e], 0), (cap, row)), AXES,...  7.16 us
    gather x1, local copies, waits for them, and re-layouts, step(): rows = jnp.take(pool, idx, axis=0, mode='clip', indices_are_sorted=True)  6.65 us
  transfers between devices with their start and end apart: 12, of which 5 were waited for; matrix products, arithmetic and copies ran while one was open for 12% of the time, Pallas kernels for 0%

profile of v7, /device:TPU:0, one launch (start us, length us, event | category | flops | bytes accessed | tf_op | source)
XLA Modules:
  0.0 176.5 jit_solution(12813512107747730234)
XLA Ops:
  1.3 0.6 broadcast_in_dim.58
  1.9 7.3 %all-to-all-start = ((s32[32,1,1]{2,1,0:T(1,128)}), s32[32,1,1]{2,1,0:T(1,128)S(1)}, u32[]{:S(2)}, u32[]{:S(2)}) async-start(s32[32,1,1]{2,1,0:T(1,128)} %broadcast_in_dim.58), calls=%async_computation | async-start | bytes 32768 | tf_op jit(solution)/shard_map/all_to_all | solution.py:156
  9.2 0.6 multiply_add_fusion
  9.8 3.4 %copy.51 = bf16[128,11552]{1,0:T(8,128)(2,1)S(1)} copy(bf16[128,11552]{0,1:T(8,128)(2,1)} %param.15) | data formatting | bytes 5914624 | tf_op args[0]
  13.2 1.8 %constant_dynamic-update-slice_fusion.6 = bf16[288,11552]{1,0:T(8,128)(2,1)} fusion(bf16[128,11552]{1,0:T(8,128)(2,1)S(1)} %copy.51), kind=kLoop, calls=%fused_computation.50 | loop fusion | bytes 5939200
  15.1 0.9 broadcast_compare_fusion
  16.1 0.6 iota_compare_fusion.1
  16.7 0.6 compare_reduce_fusion
  17.3 1.3 fusion.18
  18.6 0.5 scatter.4.counts_ref
  19.1 0.6 broadcast_in_dim.59.me_ref
  19.7 5.1 %shard_map.130 = (s32[24,128]{1,0:T(8,128)}, s32[8,256]{1,0:T(8,128)}) custom-call(s32[1,128]{1,0:T(1,128)} %scatter.4.counts_ref, s32[1,128]{1,0:T(1,128)} %broadcast_in_dim.59.me_ref), custom_call_target="tpu_custom_call" | custom-call | tf_op jit(solution)/shard_map/pallas_call | solution.py:127
  24.8 1.6 fusion.20
  41.5 1.9 %pad_dynamic-slice_fusion.1 = (bf16[32,11552]{1,0:T(8,128)(2,1)}, bf16[32,11552]{1,0:T(8,128)(2,1)}, bf16[32,11552]{1,0:T(8,128)(2,1)}) fusion(s32[]{:T(128)S(6)} %select_n.69, bf16[128,11552]{1,0:T(8,128)(2,1)S(1)} %copy.51, s32[]{:T(128)S(6)} %select_n.67, s32[]{:T(128)S(6)} %select_n.68), kind=kLoop, calls=%fused_computation.26 | loop fusion | bytes 5175308 | tf_op jit(solution)/shard_map/dynamic_slice | solution.py:177
  43.4 1.8 %collective-permute-start.1 = (bf16[32,11552]{1,0:T(8,128)(2,1)}, bf16[32,11552]{1,0:T(8,128)(2,1)}, u32[]{:S(2)}, u32[]{:S(2)}) collective-permute-start(bf16[32,11552]{1,0:T(8,128)(2,1)} %get-tuple-element.114), channel_id=1, source_target_pairs={{0,2},{1,3},{2,0},{3,1},{4,6},{5,7},{6,4},{7,5},{8,10},{9,11},{10,... | collective-permute-start | bytes 2217992 | tf_op jit(solution)/shard_map/ppermute | solution.py:177
  45.7 0.9 pad_dynamic-slice_fusion.4
  46.6 2.4 %collective-permute-start = (bf16[16,11552]{1,0:T(8,128)(2,1)}, bf16[16,11552]{1,0:T(8,128)(2,1)S(1)}, u32[]{:S(2)}, u32[]{:S(2)}) collective-permute-start(bf16[16,11552]{1,0:T(8,128)(2,1)} %pad_dynamic-slice_fusion.4), channel_id=1, source_target_pairs={{0,4},{1,5},{2,6},{3,7},{4,0},{5,1},{6,2},{7,3},{8,12},{9,13},{10,... | collective-permute-start | bytes 1109000 | tf_op jit(solution)/shard_map/ppermute | solution.py:177
  49.0 1.5 collective-permute-start.2
  50.5 1.5 collective-permute-start.3
  52.7 1.4 pad_dynamic-slice_fusion
  54.1 0.7 slice.73
  58.0 0.7 slice_bitcast_fusion
  58.7 0.6 pad_clamp_fusion.1
  59.3 10.4 %collective-permute-done = bf16[16,11552]{1,0:T(8,128)(2,1)S(1)} collective-permute-done((bf16[16,11552]{1,0:T(8,128)(2,1)}, bf16[16,11552]{1,0:T(8,128)(2,1)S(1)}, u32[]{:S(2)}, u32[]{:S(2)}) %collective-permute-start) | collective-permute-done | bytes 369696 | tf_op jit(solution)/shard_map/ppermute | solution.py:177
  69.7 0.8 constant_dynamic-update-slice_fusion.5
  70.5 2.1 %constant_dynamic-update-slice_fusion.4 = bf16[288,11552]{1,0:T(8,128)(2,1)} fusion(bf16[288,11552]{1,0:T(8,128)(2,1)} %constant_dynamic-update-slice_fusion.5, bf16[32,11552]{1,0:T(8,128)(2,1)} %collective-permute-done.1), kind=kLoop, calls=%fused_computation.48 | loop fusion | bytes 1490944
  72.6 2.0 %constant_dynamic-update-slice_fusion.3 = bf16[288,11552]{1,0:T(8,128)(2,1)} fusion(bf16[288,11552]{1,0:T(8,128)(2,1)} %constant_dynamic-update-slice_fusion.4, bf16[32,11552]{1,0:T(8,128)(2,1)} %collective-permute-done.2), kind=kLoop, calls=%fused_computation.47 | loop fusion | bytes 1490944
  74.6 2.1 %constant_dynamic-update-slice_fusion.2 = bf16[288,11552]{1,0:T(8,128)(2,1)} fusion(bf16[288,11552]{1,0:T(8,128)(2,1)} %constant_dynamic-update-slice_fusion.3, bf16[32,11552]{1,0:T(8,128)(2,1)} %collective-permute-done.3), kind=kLoop, calls=%fused_computation.46 | loop fusion | bytes 1490944
  76.7 1.1 constant_dynamic-update-slice_fusion.1
  77.8 1.1 broadcast_in_dim.57
  78.9 66.2 %while.11 = (s32[]{:T(128)}, bf16[208,2944]{1,0:T(8,128)(2,1)}, s32[]{:T(128)}, s32[160]{0:T(256)S(1)}, bf16[288,11552]{1,0:T(8,128)(2,1)}, /*index=5*/bf16[3,3,...) while((s32[]{:T(128)}, bf16[208,2944]{1,0:T(8,128)(2,1)}, ...), condition=%wide.region_3.4_spmd, body=%wide.region_1.3_spmd.sunk | while | flops 33799694336 | bytes 71023168 | solution.py:200
  79.2 6.7 %gather_fusion = bf16[40,11552]{1,0:T(8,128)(2,1)} fusion(bf16[288,11552]{1,0:T(8,128)(2,1)} %get-tuple-element.240, s32[1024]{0:T(1024)S(1)} %pad_clamp_fusion.3), kind=kCustom, calls=%fused_computation.clone.1 | custom fusion | bytes 1848480 | tf_op jit(solution)/shard_map/while/body/jit(_take)/gather | solution.py:188
  85.9 3.3 %copy.71 = bf16[40,11552]{0,1:T(8,128)(2,1)S(1)} copy(bf16[40,11552]{1,0:T(8,128)(2,1)} %gather_fusion) | data formatting | bytes 1848320 | tf_op jit(solution)/shard_map/while/body/reshape | solution.py:37
  89.2 8.2 %maximum_convert_fusion.5 = bf16[40,19,19,256]{3,0,2,1:T(8,128)(2,1)S(1)} fusion(bf16[40,19,19,32]{0,3,2,1:T(8,128)(2,1)S(1)} %bitcast.97, bf16[3,3,32,256]{3,2,1,0:T(8,128)(2,1)S(1)} %get-tuple-element.241), kind=kOutput, calls=%fused_computation.5.clone.1 | convolution fusion | flops 1989857280 | bytes 8464896 | tf_op jit(solution)/shard_map/while/body/conv_general_dilated | solution.py:25
  97.4 18.3 %maximum_convert_fusion.6 = bf16[40,19,19,256]{3,0,2,1:T(8,128)(2,1)S(1)} fusion(bf16[40,19,19,256]{3,0,2,1:T(8,128)(2,1)S(1)} %maximum_convert_fusion.5, bf16[1,3,3,256,256]{4,3,2,1,0:T(8,128)(2,1)S(1)} %copy-done.9), kind=kOutput, calls=%fused_computation.4.clone.1 | convolution fusion | flops 15867105280 | bytes 15966208 | tf_op jit(solution)/shard_map/while/body/conv_general_dilated | solution.py:25
  115.7 19.9 %convert_reduce_fusion.3 = (f32[40,256]{1,0:T(8,128)S(1)}, bf16[40,19,19,256]{3,0,2,1:T(8,128)(2,1)}) fusion(bf16[40,19,19,256]{3,0,2,1:T(8,128)(2,1)S(1)} %maximum_convert_fusion.6, bf16[1,3,3,256,256]{4,3,2,1,0:T(8,128)(2,1)S(1)} %copy-done.10, bf16[40,19,19,256]{3,0,2,1:T(8,128)(2,1)S(1)} %maximum_convert_fusion.5), kind=kOutput, calls=%fused_computation.2.clone.1 | convolution fusion | flops 15881881600 | bytes 23400448 | tf_op jit(solution)/shard_map/while/body/conv_general_dilated | solution.py:25
  135.6 0.1 fusion.52
  135.7 0.2 copy.72
  135.9 7.2 %convolution_convert_fusion.3 = bf16[40,19,19,8]{0,3,2,1:T(8,128)(2,1)S(1)} fusion(bf16[40,19,19,256]{3,0,2,1:T(8,128)(2,1)} %get-tuple-element.201, bf16[256,8]{0,1:T(8,128)(2,1)S(1)} %get-tuple-element.244), kind=kOutput, calls=%fused_computation.6.clone.1 | convolution fusion | flops 59261760 | bytes 7628416 | tf_op jit(solution)/shard_map/while/body/bhwc,cf->bfhw/dot_general | solution.py:43
  143.1 0.6 copy.73
  143.8 0.2 convert_element_type.69
  144.1 0.1 fusion.53
  144.4 0.7 constant_dynamic-update-slice_fusion.14
  145.1 1.5 constant_dynamic-update-slice_fusion.12
  146.6 0.2 copy-done
  146.8 3.3 %collective-permute-start.5 = (bf16[16,2944]{1,0:T(8,128)(2,1)S(1)}, bf16[16,2944]{1,0:T(8,128)(2,1)S(1)}, u32[]{:S(2)}, u32[]{:S(2)}) collective-permute-start(bf16[16,2944]{1,0:T(8,128)(2,1)S(1)} %constant_dynamic-slice_fusion.4), channel_id=1, source_target_pairs={{0,4},{1,5},{2,6},{3,7},{4,0},{5,1},{6,2},{7,3},{8,12},{9,13},{10,... | collective-permute-start | bytes 282632 | tf_op jit(solution)/shard_map/ppermute | solution.py:208
  150.1 0.1 constant_dynamic-slice_fusion.1
  150.3 0.9 collective-permute-start.6
  151.2 1.5 collective-permute-start.7
  152.7 1.5 collective-permute-start.8
  154.3 2.4 %collective-permute-done.6 = bf16[32,2944]{1,0:T(8,128)(2,1)S(1)} collective-permute-done((bf16[32,2944]{1,0:T(8,128)(2,1)S(1)}, bf16[32,2944]{1,0:T(8,128)(2,1)S(1)}, u32[]{:S(2)}, u32[]{:S(2)}) %collective-permute-start.6) | collective-permute-done | bytes 188448 | tf_op jit(solution)/shard_map/ppermute | solution.py:208
  156.8 1.5 collective-permute-done.8
  158.3 1.2 gather_fusion.1
  159.5 1.2 copy.57
  160.7 1.3 reshape.142
  162.0 0.6 select_reduce_fusion
  162.6 0.6 fusion.13
  163.2 0.2 fusion.15
  163.4 1.7 convolution_bitcast_fusion.1
  165.1 3.7 %all-to-all-start.1 = ((f32[32,1,8]{2,1,0:T(1,128)}), f32[32,1,8]{2,1,0:T(1,128)S(1)}, u32[]{:S(2)}, u32[]{:S(2)}) async-start(f32[32,1,8]{2,1,0:T(1,128)} %convolution_bitcast_fusion.1), calls=%async_computation.1 | async-start | bytes 32768 | tf_op jit(solution)/shard_map/all_to_all | solution.py:229
  168.8 1.8 %divide_select_fusion = f32[128,8,362]{0,1,2:T(8,128)} fusion(f32[128,8,362]{0,2,1:T(8,128)S(1)} %reshape.142, pred[128,8,361]{0,1,2:T(8,128)(4,1)S(1)} %copy-done.1, f32[128,8]{0,1:T(8,128)S(1)} %fusion.13, f32[128,8]{0,1:T(8,128)S(1)} %select_reduce_fusion, f32[8]{0:T(128)S(1)} %copy-done.7, pred[128]{0:T(512)(128)(4,1)S(1)} %copy-done.8), kind=kLoop, calls=%fused_computation.31 | loop fusion | flops 1853440 | bytes 3343520 | tf_op jit(solution)/shard_map/jit(_where)/select_n | solution.py:220
  170.6 0.5 broadcast_select_fusion.1
  171.1 4.8 %all-to-all-done.1 = f32[32,1,8]{2,1,0:T(1,128)S(1)} async-done(((f32[32,1,8]{2,1,0:T(1,128)}), f32[32,1,8]{2,1,0:T(1,128)S(1)}, u32[]{:S(2)}, u32[]{:S(2)}) %all-to-all-start.1) | async-done | bytes 1056 | tf_op jit(solution)/shard_map/all_to_all | solution.py:229
  175.9 0.6 reduce_sum.28
  (49 shorter events, 0.9 us)
Async XLA Ops:
  1.9 15.4 %all-to-all-start = ((s32[32,1,1]{2,1,0:T(1,128)}), s32[32,1,1]{2,1,0:T(1,128)S(1)}, u32[]{:S(2)}, u32[]{:S(2)}) async-start(s32[32,1,1]{2,1,0:T(1,128)} %broadcast_in_dim.58), calls=%async_computation | async-start | bytes 32768 | tf_op jit(solution)/shard_map/all_to_all | solution.py:156
  13.2 1.9 %copy-start.3 = (s32[128,8,361]{0,1,2:T(8,128)S(1)}, s32[128,8,361]{0,1,2:T(8,128)}, u32[]{:S(2)}) copy-start(s32[128,8,361]{0,1,2:T(8,128)} %param.18) | copy-start | bytes 4435972
  43.4 27.1 %collective-permute-start.1 = (bf16[32,11552]{1,0:T(8,128)(2,1)}, bf16[32,11552]{1,0:T(8,128)(2,1)}, u32[]{:S(2)}, u32[]{:S(2)}) collective-permute-start(bf16[32,11552]{1,0:T(8,128)(2,1)} %get-tuple-element.114), channel_id=1, source_target_pairs={{0,2},{1,3},{2,0},{3,1},{4,6},{5,7},{6,4},{7,5},{8,10},{9,11},{10,... | collective-permute-start | bytes 2217992 | tf_op jit(solution)/shard_map/ppermute | solution.py:177
  46.6 23.0 %collective-permute-start = (bf16[16,11552]{1,0:T(8,128)(2,1)}, bf16[16,11552]{1,0:T(8,128)(2,1)S(1)}, u32[]{:S(2)}, u32[]{:S(2)}) collective-permute-start(bf16[16,11552]{1,0:T(8,128)(2,1)} %pad_dynamic-slice_fusion.4), channel_id=1, source_target_pairs={{0,4},{1,5},{2,6},{3,7},{4,0},{5,1},{6,2},{7,3},{8,12},{9,13},{10,... | collective-permute-start | bytes 1109000 | tf_op jit(solution)/shard_map/ppermute | solution.py:177
  49.0 23.5 %collective-permute-start.2 = (bf16[32,11552]{1,0:T(8,128)(2,1)}, bf16[32,11552]{1,0:T(8,128)(2,1)}, u32[]{:S(2)}, u32[]{:S(2)}) collective-permute-start(bf16[32,11552]{1,0:T(8,128)(2,1)} %get-tuple-element.115), channel_id=1, source_target_pairs={{0,16},{1,17},{2,18},{3,19},{4,20},{5,21},{6,22},{7,23},{8,24},{9,... | collective-permute-start | bytes 2217992 | tf_op jit(solution)/shard_map/ppermute | solution.py:177
  50.5 24.1 %collective-permute-start.3 = (bf16[32,11552]{1,0:T(8,128)(2,1)}, bf16[32,11552]{1,0:T(8,128)(2,1)}, u32[]{:S(2)}, u32[]{:S(2)}) collective-permute-start(bf16[32,11552]{1,0:T(8,128)(2,1)} %get-tuple-element.113), channel_id=1, source_target_pairs={{0,1},{1,0},{2,3},{3,2},{4,5},{5,4},{6,7},{7,6},{8,9},{9,8},{10,11... | collective-permute-start | bytes 2217992 | tf_op jit(solution)/shard_map/ppermute | solution.py:177
  54.0 22.7 %collective-permute-start.4 = (bf16[48,11552]{1,0:T(8,128)(2,1)}, bf16[48,11552]{1,0:T(8,128)(2,1)S(1)}, u32[]{:S(2)}, u32[]{:S(2)}) collective-permute-start(bf16[48,11552]{1,0:T(8,128)(2,1)} %pad_dynamic-slice_fusion), channel_id=1, source_target_pairs={{0,8},{1,9},{2,10},{3,11},{4,12},{5,13},{6,14},{7,15},{8,0},{9,1},... | collective-permute-start | bytes 3326984 | tf_op jit(solution)/shard_map/ppermute | solution.py:177
  74.6 4.3 %copy-start.2 = (bf16[3,3,32,256]{3,2,1,0:T(8,128)(2,1)S(1)}, bf16[3,3,32,256]{3,2,1,0:T(8,128)(2,1)}, u32[]{:S(2)}) copy-start(bf16[3,3,32,256]{3,2,1,0:T(8,128)(2,1)} %param.19) | copy-start | bytes 442372
  74.6 4.3 %copy-start.4 = (bf16[256,8]{0,1:T(8,128)(2,1)S(1)}, bf16[256,8]{0,1:T(8,128)(2,1)}, u32[]{:S(2)}) copy-start(bf16[256,8]{0,1:T(8,128)(2,1)} %param.22) | copy-start | bytes 12292
  74.6 4.3 %copy-start.5 = (bf16[256,8]{0,1:T(8,128)(2,1)S(1)}, bf16[256,8]{0,1:T(8,128)(2,1)}, u32[]{:S(2)}) copy-start(bf16[256,8]{0,1:T(8,128)(2,1)} %param.23) | copy-start | bytes 12292
  74.6 4.3 %copy-start.11 = (bf16[256]{0:T(256)(128)(2,1)S(1)}, bf16[256]{0:T(256)(128)(2,1)}, u32[]{:S(2)}) copy-start(bf16[256]{0:T(256)(128)(2,1)} %param.24) | copy-start | bytes 1540
  89.2 8.2 %copy-start.9 = (bf16[1,3,3,256,256]{4,3,2,1,0:T(8,128)(2,1)S(1)}, bf16[1,3,3,256,256]{4,3,2,1,0:T(8,128)(2,1)}, u32[]{:S(2)}) copy-start(bf16[1,3,3,256,256]{4,3,2,1,0:T(8,128)(2,1)} %get-tuple-element.242) | copy-start | bytes 3538948 | tf_op jit(solution)/shard_map/while
  97.4 18.4 %copy-start.10 = (bf16[1,3,3,256,256]{4,3,2,1,0:T(8,128)(2,1)S(1)}, bf16[1,3,3,256,256]{4,3,2,1,0:T(8,128)(2,1)}, u32[]{:S(2)}) copy-start(bf16[1,3,3,256,256]{4,3,2,1,0:T(8,128)(2,1)} %get-tuple-element.243) | copy-start | bytes 3538948 | tf_op jit(solution)/shard_map/while
  145.1 1.7 copy-start
  146.8 7.5 %collective-permute-start.5 = (bf16[16,2944]{1,0:T(8,128)(2,1)S(1)}, bf16[16,2944]{1,0:T(8,128)(2,1)S(1)}, u32[]{:S(2)}, u32[]{:S(2)}) collective-permute-start(bf16[16,2944]{1,0:T(8,128)(2,1)S(1)} %constant_dynamic-slice_fusion.4), channel_id=1, source_target_pairs={{0,4},{1,5},{2,6},{3,7},{4,0},{5,1},{6,2},{7,3},{8,12},{9,13},{10,... | collective-permute-start | bytes 282632 | tf_op jit(solution)/shard_map/ppermute | solution.py:208
  150.3 6.4 %collective-permute-start.6 = (bf16[32,2944]{1,0:T(8,128)(2,1)S(1)}, bf16[32,2944]{1,0:T(8,128)(2,1)S(1)}, u32[]{:S(2)}, u32[]{:S(2)}) collective-permute-start(bf16[32,2944]{1,0:T(8,128)(2,1)S(1)} %get-tuple-element.118), channel_id=1, source_target_pairs={{0,2},{1,3},{2,0},{3,1},{4,6},{5,7},{6,4},{7,5},{8,10},{9,11},{10,... | collective-permute-start | bytes 565256 | tf_op jit(solution)/shard_map/ppermute | solution.py:208
  151.2 5.6 %collective-permute-start.7 = (bf16[32,2944]{1,0:T(8,128)(2,1)S(1)}, bf16[32,2944]{1,0:T(8,128)(2,1)S(1)}, u32[]{:S(2)}, u32[]{:S(2)}) collective-permute-start(bf16[32,2944]{1,0:T(8,128)(2,1)S(1)} %get-tuple-element.117), channel_id=1, source_target_pairs={{0,16},{1,17},{2,18},{3,19},{4,20},{5,21},{6,22},{7,23},{8,24},{9,... | collective-permute-start | bytes 565256 | tf_op jit(solution)/shard_map/ppermute | solution.py:208
  152.7 5.6 %collective-permute-start.8 = (bf16[32,2944]{1,0:T(8,128)(2,1)S(1)}, bf16[32,2944]{1,0:T(8,128)(2,1)S(1)}, u32[]{:S(2)}, u32[]{:S(2)}) collective-permute-start(bf16[32,2944]{1,0:T(8,128)(2,1)S(1)} %get-tuple-element.116), channel_id=1, source_target_pairs={{0,1},{1,0},{2,3},{3,2},{4,5},{5,4},{6,7},{7,6},{8,9},{9,8},{10,11... | collective-permute-start | bytes 565256 | tf_op jit(solution)/shard_map/ppermute | solution.py:208
  154.2 4.0 %collective-permute-start.9 = (bf16[48,2944]{1,0:T(8,128)(2,1)S(1)}, bf16[48,2944]{1,0:T(8,128)(2,1)S(1)}, u32[]{:S(2)}, u32[]{:S(2)}) collective-permute-start(bf16[48,2944]{1,0:T(8,128)(2,1)S(1)} %constant_dynamic-slice_fusion), channel_id=1, source_target_pairs={{0,8},{1,9},{2,10},{3,11},{4,12},{5,13},{6,14},{7,15},{8,0},{9,1},... | collective-permute-start | bytes 847880 | tf_op jit(solution)/shard_map/ppermute | solution.py:208
  159.5 2.5 %copy-start.1 = (pred[128,8,361]{0,1,2:T(8,128)(4,1)S(1)}, pred[128,8,361]{0,1,2:T(8,128)(4,1)}, u32[]{:S(2)}) copy-start(pred[128,8,361]{0,1,2:T(8,128)(4,1)} %broadcast_compare_fusion) | copy-start | bytes 1108996
  159.5 2.5 %copy-start.7 = (f32[8]{0:T(128)S(1)}, f32[8]{0:T(128)}, u32[]{:S(2)}) copy-start(f32[8]{0:T(128)} %param.25) | copy-start | bytes 100
  162.0 1.4 copy-start.6
  162.0 1.4 copy-start.12
  162.0 6.8 %copy-start.8 = (pred[128]{0:T(512)(128)(4,1)S(1)}, pred[128]{0:T(512)(128)(4,1)}, u32[]{:S(2)}) copy-start(pred[128]{0:T(512)(128)(4,1)} %iota_compare_fusion.1) | copy-start | bytes 388
  165.1 10.8 %all-to-all-start.1 = ((f32[32,1,8]{2,1,0:T(1,128)}), f32[32,1,8]{2,1,0:T(1,128)S(1)}, u32[]{:S(2)}, u32[]{:S(2)}) async-start(f32[32,1,8]{2,1,0:T(1,128)} %convolution_bitcast_fusion.1), calls=%async_computation.1 | async-start | bytes 32768 | tf_op jit(solution)/shard_map/all_to_all | solution.py:229
